TPU v7x, 256 devices: a whole 4x4x8 slice. The times are simulated.
256 devices in a mesh: ctx: 64 (over z, y_hi, x), tp: 4 (over y_lo, core).
Axes of the slice: x: 4, y: 4 (y_hi: 2, y_lo: 2; y = y_hi * 2 + y_lo), z: 8, core: 2. Of those that a mesh axis runs over, the one named last changes fastest.
Arguments:
- query_in: bfloat16 [2048, 8192], P('tp', 'ctx'), may hold values from -6 to 6
- key_in: bfloat16 [2048, 8192], P('tp', 'ctx'), may hold values from -6 to 6
- value_in: bfloat16 [2048, 8192], P('tp', 'ctx'), may hold values from -6 to 6
- short_weights: float32 [3, 2048, 7], P(None, 'tp'), may hold values from -3 to 3
- filters: float32 [4, 512, 8192], P('tp', 'ctx'), may hold values from 0 to 1
- out_weight: bfloat16 [4096, 2048], P(None, 'tp'), may hold values from -0.125 to 0.125
- cotangent: bfloat16 [4096, 8192], P('tp', 'ctx'), may hold values from -16 to 16
Outputs:
- mixed_out: bfloat16 [4096, 8192], P('tp', 'ctx')
- grad_query: bfloat16 [2048, 8192], P('tp', 'ctx')
- grad_key: bfloat16 [2048, 8192], P('tp', 'ctx')
- grad_value: bfloat16 [2048, 8192], P('tp', 'ctx')
- grad_filters: float32 [4, 512, 8192], P('tp', 'ctx')
- grad_out_weight: float32 [4096, 2048], P('ctx', 'tp')
All inputs are finite; a program needn't handle non-finite values.
Results may differ from a plain program's by a relative error of at most 0.012.
Values may be sent and summed in bfloat16 or wider, within the bound.
No kernel may reach another device: no remote copies, remote signals or barrier semaphores. Data moves between devices by JAX's collectives and lax.ppermute only.
A program may use at most 128 MiB of HBM per device.

v0:
```python
import math

import jax
import jax.numpy as jnp
from jax import lax
from jax.sharding import Mesh, PartitionSpec as P

BLOCK = 128
CTX_HI = "ctx_hi"
CTX_LO = "ctx_lo"
CTX = (CTX_HI, CTX_LO)
LO_SIZE = 8


TWO_PI = 2.0 * math.pi
DFT_PRECISION = lax.Precision.HIGH


def from_behind(value, axis, steps):
    count = lax.axis_size(axis)
    first, last = (max(0, -steps), min(count, count - steps))
    return lax.ppermute(value, axis, [(source, source + steps) for source in range(first, last)])


def fourier_table(count):
    element_indices = jnp.arange(count, dtype=jnp.int32)
    angles = (element_indices[:, None] * element_indices[None, :] % count).astype(jnp.float32) * (
        TWO_PI / count
    )
    return (jnp.cos(angles), -jnp.sin(angles))


def make_tables(length, block_width):
    row_count = 2 * length // block_width
    full_len = row_count * block_width
    outer_re, outer_im = fourier_table(row_count)
    inner_re, inner_im = fourier_table(block_width)
    row_index = jnp.arange(row_count, dtype=jnp.int32)[:, None]
    col_index = jnp.arange(block_width, dtype=jnp.int32)[None, :]
    angles = (row_index * col_index % full_len).astype(jnp.float32) * (TWO_PI / full_len)
    return (outer_re, outer_im, inner_re, inner_im, jnp.cos(angles), -jnp.sin(angles))


def spectrum(signal, tables):
    outer_re, outer_im, inner_re, inner_im, twist_re, twist_im = tables
    channels, length = signal.shape
    block_width = inner_re.shape[0]
    half_rows = length // block_width
    blocks = signal.reshape(channels, half_rows, block_width)
    section_re = jnp.einsum("kn,cnm->ckm", outer_re[:, :half_rows], blocks, precision=DFT_PRECISION)
    section_im = jnp.einsum("kn,cnm->ckm", outer_im[:, :half_rows], blocks, precision=DFT_PRECISION)
    turned_re = section_re * twist_re - section_im * twist_im
    turned_im = section_re * twist_im + section_im * twist_re
    frequency_real_component = jnp.matmul(turned_re, inner_re, precision=DFT_PRECISION) - jnp.matmul(
        turned_im, inner_im, precision=DFT_PRECISION
    )
    spec_im = jnp.matmul(turned_re, inner_im, precision=DFT_PRECISION) + jnp.matmul(
        turned_im, inner_re, precision=DFT_PRECISION
    )
    return (frequency_real_component, spec_im)


def inverse(frequency_real_component, spec_im, tables):
    outer_re, outer_im, inner_re, inner_im, twist_re, twist_im = tables
    channels, row_count, block_width = frequency_real_component.shape
    half_rows = row_count // 2
    back_re = jnp.matmul(frequency_real_component, inner_re, precision=DFT_PRECISION) + jnp.matmul(
        spec_im, inner_im, precision=DFT_PRECISION
    )
    back_im = jnp.matmul(spec_im, inner_re, precision=DFT_PRECISION) - jnp.matmul(
        frequency_real_component, inner_im, precision=DFT_PRECISION
    )
    turned_re = back_re * twist_re + back_im * twist_im
    turned_im = back_im * twist_re - back_re * twist_im
    signal = jnp.einsum("nk,ckm->cnm", outer_re[:half_rows], turned_re, precision=DFT_PRECISION)
    signal = signal + jnp.einsum("nk,ckm->cnm", outer_im[:half_rows], turned_im, precision=DFT_PRECISION)
    return (signal / (row_count * block_width)).reshape(channels, half_rows * block_width)


def causal_taps(stacked, earlier, weights):
    tap_count = weights.shape[2]
    length = stacked.shape[2]
    extended = jnp.concatenate([earlier, stacked], axis=2).astype(jnp.float32)
    running_total = jnp.zeros(stacked.shape, jnp.float32)
    for offset in range(tap_count):
        begin = tap_count - 1 - offset
        running_total = (
            running_total
            + weights[:, :, offset : offset + 1] * extended[:, :, begin : begin + length]
        )
    return running_total


def anticausal_taps(stacked, following, weights):
    tap_count = weights.shape[2]
    length = stacked.shape[2]
    extended = jnp.concatenate([stacked, following], axis=2).astype(jnp.float32)
    running_total = jnp.zeros(stacked.shape, jnp.float32)
    for offset in range(tap_count):
        running_total = (
            running_total
            + weights[:, :, offset : offset + 1] * extended[:, :, offset : offset + length]
        )
    return running_total


def to_channels(block):
    return lax.all_to_all(block, CTX, split_axis=0, concat_axis=1, tiled=True)


def to_positions(block):
    return lax.all_to_all(block, CTX, split_axis=1, concat_axis=0, tiled=True)


def swap_layouts(channel_block, position_block):
    count = lax.axis_size(CTX)
    channels, length = channel_block.shape
    local_len = length // count
    outgoing = jnp.stack(
        [
            channel_block.reshape(channels, count, local_len).transpose(1, 0, 2),
            position_block.reshape(count, channels, local_len),
        ],
        axis=1,
    )
    incoming = lax.all_to_all(outgoing, CTX, split_axis=0, concat_axis=0, tiled=True)
    positions = incoming[:, 0].reshape(count * channels, local_len)
    channels_out = incoming[:, 1].transpose(1, 0, 2).reshape(channels, length)
    return positions, channels_out


def weight_gradient(full_cotangent, gated_out):
    hi_count = lax.axis_size(CTX_HI)
    lo_count = lax.axis_size(CTX_LO)
    features, local_len = full_cotangent.shape
    rows = features // (hi_count * lo_count)
    group_gated = lax.all_gather(gated_out, CTX_LO, axis=1, tiled=True)
    group_gated = group_gated.reshape(gated_out.shape[0], lo_count, local_len)
    by_target = full_cotangent.reshape(hi_count, lo_count, rows, local_len).transpose(1, 0, 2, 3)
    group_rows = lax.all_to_all(by_target, CTX_LO, split_axis=0, concat_axis=0, tiled=True)
    weight_partial = lax.dot_general(
        group_rows, group_gated, (((0, 3), (1, 2)), ((), ())), preferred_element_type=jnp.float32
    ).astype(jnp.bfloat16)
    received = lax.all_to_all(weight_partial, CTX_HI, split_axis=0, concat_axis=0, tiled=True)
    return received.astype(jnp.float32).sum(0)


def per_device(query_in, key_in, value_in, short_weights, filters, out_weight, cotangent):
    tap_count = short_weights.shape[2]
    local_len = query_in.shape[1]
    stacked = jnp.stack([query_in, key_in, value_in])
    earlier = from_behind(stacked[:, :, local_len - (tap_count - 1) :], CTX, 1)
    shorts = causal_taps(stacked, earlier, short_weights).astype(jnp.bfloat16)
    product = (shorts[1].astype(jnp.float32) * shorts[2].astype(jnp.float32)).astype(jnp.bfloat16)
    product_chan = to_channels(product)
    tables = make_tables(product_chan.shape[1], BLOCK)
    kernel_re, kernel_im = spectrum(filters[0], tables)
    product_re, product_im = spectrum(product_chan.astype(jnp.float32), tables)
    convolved_chan = inverse(
        product_re * kernel_re - product_im * kernel_im,
        product_re * kernel_im + product_im * kernel_re,
        tables,
    ).astype(jnp.bfloat16)
    full_cotangent = lax.all_gather(cotangent, "tp", axis=0, tiled=True)
    grad_gated = lax.dot_general(
        out_weight, full_cotangent, (((0,), (0,)), ((), ())), preferred_element_type=jnp.float32
    )
    grad_conv = (grad_gated * shorts[0].astype(jnp.float32)).astype(jnp.bfloat16)
    convolved, grad_chan = swap_layouts(convolved_chan, grad_conv)
    gated_out = (shorts[0].astype(jnp.float32) * convolved.astype(jnp.float32)).astype(jnp.bfloat16)
    mixed_out = lax.psum_scatter(
        jnp.dot(out_weight, gated_out, preferred_element_type=jnp.float32).astype(jnp.bfloat16),
        "tp",
        scatter_dimension=0,
        tiled=True,
    )
    grad_out_weight = weight_gradient(full_cotangent, gated_out)
    gradient_re, gradient_im = spectrum(grad_chan.astype(jnp.float32), tables)
    grad_product_chan = inverse(
        kernel_re * gradient_re + kernel_im * gradient_im,
        kernel_re * gradient_im - kernel_im * gradient_re,
        tables,
    ).astype(jnp.bfloat16)
    grad_filters = inverse(
        product_re * gradient_re + product_im * gradient_im,
        product_re * gradient_im - product_im * gradient_re,
        tables,
    ).reshape(filters.shape)
    derivative_of_multiple = to_positions(grad_product_chan)
    grad_shorts = jnp.stack(
        [
            grad_gated * convolved.astype(jnp.float32),
            derivative_of_multiple.astype(jnp.float32) * shorts[2].astype(jnp.float32),
            derivative_of_multiple.astype(jnp.float32) * shorts[1].astype(jnp.float32),
        ]
    ).astype(jnp.bfloat16)
    following = from_behind(grad_shorts[:, :, : tap_count - 1], CTX, -1)
    gradients = anticausal_taps(grad_shorts, following, short_weights).astype(jnp.bfloat16)
    return (mixed_out, gradients[0], gradients[1], gradients[2], grad_filters, grad_out_weight)


def solution(mesh):
    ctx_count, tp_count = mesh.devices.shape
    split_mesh = Mesh(
        mesh.devices.reshape(ctx_count // LO_SIZE, LO_SIZE, tp_count), (CTX_HI, CTX_LO, "tp")
    )
    placed = (
        P("tp", CTX),
        P("tp", CTX),
        P("tp", CTX),
        P(None, "tp", None),
        P("tp", CTX, None),
        P(None, "tp"),
        P("tp", CTX),
    )
    return jax.shard_map(
        per_device,
        mesh=split_mesh,
        in_specs=placed,
        out_specs=(
            P("tp", CTX),
            P("tp", CTX),
            P("tp", CTX),
            P("tp", CTX),
            P("tp", CTX, None),
            P(CTX, "tp"),
        ),
        check_vma=False,
    )
```

profile of v0, /device:TPU:22, one launch (start us, length us, event | category | flops | bytes accessed | tf_op | source)
XLA Modules:
  0.0 173.0 jit_solution(17147601801514148057)
XLA Ops:
  7.2 1.0 copy.243
  8.3 1.0 copy.242
  9.3 1.0 copy.241
  11.0 3.5 %collective-permute-start = (bf16[3,512,6]{1,2,0:T(8,128)(2,1)}, bf16[3,512,6]{1,2,0:T(8,128)(2,1)}, u32[]{:S(2)}, u32[]{:S(2)}) collective-permute-start(bf16[3,512,6]{1,2,0:T(8,128)(2,1)} %pad_maximum_fusion.3), channel_id=1, source_target_pairs={{0,4},{4,8},{8,12},{12,16},{16,20},{20,24},{24,28},{28,32},{32,36}... | collective-permute-start | bytes 55304 | tf_op jit(solution)/shard_map/ppermute | solution.py:22
  18.5 0.9 maximum_convert_fusion
  20.9 14.2 %all-to-all-start = ((bf16[64,8,128]{2,1,0:T(8,128)(2,1)}), bf16[64,8,128]{2,1,0:T(8,128)(2,1)}, u32[]{:S(2)}, u32[]{:S(2)}) async-start(bf16[64,8,128]{2,1,0:T(8,128)(2,1)} %bitcast.5), calls=%async_computation | async-start | bytes 262144 | tf_op jit(solution)/shard_map/all_to_all | solution.py:108
  35.1 1.5 convolution_subtract_fusion.4
  36.6 6.8 %all-to-all-done = bf16[64,8,128]{2,1,0:T(8,128)(2,1)} async-done(((bf16[64,8,128]{2,1,0:T(8,128)(2,1)}), bf16[64,8,128]{2,1,0:T(8,128)(2,1)}, u32[]{:S(2)}, u32[]{:S(2)}) %all-to-all-start) | async-done | bytes 131104 | tf_op jit(solution)/shard_map/all_to_all | solution.py:108
  43.4 1.3 convolution_bitcast_fusion.3
  44.7 1.3 convolution_bitcast_fusion.4
  47.5 0.8 convolution_subtract_fusion.5
  48.3 1.6 multiply_subtract_fusion.3
  53.4 4.0 %fusion.55 = (bf16[512,128]{0,1:T(8,128)(2,1)S(1)}, f32[512,128]{0,1:T(8,128)}) fusion(bf16[3,512,128]{1,2,0:T(8,128)(2,1)S(1)} %fusion.19, bf16[4096,512]{1,0:T(8,128)(2,1)} %param.12, bf16[4096,128]{1,0:T(8,128)(2,1)} %all-gather.3.cloned.1.call-done), kind=kOutput, calls=%fused_computation.110 | convolution fusion | flops 537067520 | bytes 5767168 | tf_op jit(solution)/shard_map/dot_general | solution.py:165
  57.6 0.9 copy.276
  58.5 8.6 %all-to-all-start.1 = ((bf16[64,2,8,128]{3,2,1,0:T(8,128)(2,1)}), bf16[64,2,8,128]{3,2,1,0:T(8,128)(2,1)S(1)}, u32[]{:S(2)}, u32[]{:S(2)}) async-start(bf16[64,2,8,128]{3,2,1,0:T(8,128)(2,1)} %copy.276), calls=%async_computation.1 | async-start | bytes 524288 | tf_op jit(solution)/shard_map/all_to_all | solution.py:126
  67.3 2.3 %copy.316 = bf16[8,8,64,128]{3,2,1,0:T(8,128)(2,1)} copy(bf16[8,8,64,128]{3,2,0,1:T(8,128)(2,1)} %bitcast.229) | data formatting | bytes 2097152 | tf_op jit(solution)/shard_map/transpose | solution.py:139
  69.6 7.2 %all-to-all-done.1 = bf16[64,2,8,128]{3,2,1,0:T(8,128)(2,1)S(1)} async-done(((bf16[64,2,8,128]{3,2,1,0:T(8,128)(2,1)}), bf16[64,2,8,128]{3,2,1,0:T(8,128)(2,1)S(1)}, u32[]{:S(2)}, u32[]{:S(2)}) %all-to-all-start.1) | async-done | bytes 262176 | tf_op jit(solution)/shard_map/all_to_all | solution.py:126
  79.1 1.6 fusion.81
  80.7 1.8 %copy.278 = f32[512,128]{0,1:T(8,128)} copy(f32[512,128]{1,0:T(8,128)} %get-tuple-element.46) | data formatting | bytes 524288 | tf_op jit(solution)/shard_map/convert_element_type | solution.py:170
  83.2 2.8 %multiply_add_fusion = (f32[8,128,128]{2,1,0:T(8,128)}, f32[8,128,128]{2,1,0:T(8,128)S(1)}, f32[8,128,128]{2,1,0:T(8,128)S(1)}, f32[8,128,128]{2,1,0:T(8,128)S(1)}) fusion(f32[8,128,128]{2,1,0:T(8,128)} %get-tuple-element.56, f32[8,128,128]{2,1,0:T(8,128)S(1)} %convolution_subtract_fusion.5, f32[8,128,128]{2,1,0:T(8,128)S(1)} %convolution_subtract_fusion.2, ...), kind=kOutput, calls=%fused_computation.75 | convolution fusion | flops 102989824 | bytes 6422528 | tf_op jit(solution)/shard_map/dot_general | solution.py:57
  91.2 9.2 %all-to-all-start.2 = ((bf16[8,64,128]{2,0,1:T(8,128)(2,1)}), bf16[8,64,128]{2,0,1:T(8,128)(2,1)}, u32[]{:S(2)}, u32[]{:S(2)}) async-start(bf16[8,64,128]{2,0,1:T(8,128)(2,1)} %copy.301), calls=%async_computation.3 | async-start | bytes 262144 | tf_op jit(solution)/shard_map/all_to_all | solution.py:112
  101.6 4.7 %fusion = bf16[4096,128]{0,1:T(8,128)(2,1)} fusion(bf16[512,128]{0,1:T(8,128)(2,1)} %get-tuple-element.44, bf16[4096,512]{1,0:T(8,128)(2,1)} %param.12), kind=kOutput, calls=%fused_computation.1 | convolution fusion | flops 537395200 | bytes 5373952 | tf_op jit(solution)/shard_map/dot_general | solution.py:172
  107.0 1.7 all-to-all-done.2
  108.7 8.6 %all-to-all-start.3 = ((bf16[8,8,64,128]{3,2,1,0:T(8,128)(2,1)}), bf16[8,8,64,128]{3,2,1,0:T(8,128)(2,1)}, u32[]{:S(2)}, u32[]{:S(2)}) async-start(bf16[8,8,64,128]{3,2,1,0:T(8,128)(2,1)} %copy.316), calls=%async_computation.4 | async-start | bytes 2097152 | tf_op jit(solution)/shard_map/all_to_all | solution.py:140
  118.5 0.9 convert_bitcast_fusion
  119.6 2.8 %collective-permute-start.1 = (bf16[3,512,6]{1,2,0:T(8,128)(2,1)S(1)}, bf16[3,512,6]{1,2,0:T(8,128)(2,1)S(1)}, u32[]{:S(2)}, u32[]{:S(2)}) collective-permute-start(bf16[3,512,6]{1,2,0:T(8,128)(2,1)S(1)} %pad_maximum_fusion.1), channel_id=1, source_target_pairs={{4,0},{8,4},{12,8},{16,12},{20,16},{24,20},{28,24},{32,28},{36,32}... | collective-permute-start | bytes 55304 | tf_op jit(solution)/shard_map/ppermute | solution.py:22
  122.4 5.5 %all-to-all-done.3 = bf16[8,8,64,128]{3,2,1,0:T(8,128)(2,1)} async-done(((bf16[8,8,64,128]{3,2,1,0:T(8,128)(2,1)}), bf16[8,8,64,128]{3,2,1,0:T(8,128)(2,1)}, u32[]{:S(2)}, u32[]{:S(2)}) %all-to-all-start.3) | async-done | bytes 1048608 | tf_op jit(solution)/shard_map/all_to_all | solution.py:140
  127.9 11.7 %all-gather.5.cloned.1.call-done = bf16[512,1024]{0,1:T(8,128)(2,1)} async-done(((bf16[512,128]{0,1:T(8,128)(2,1)}), bf16[512,1024]{0,1:T(8,128)(2,1)}) %all-gather.5.cloned.1.call-update) | async-done | bytes 1048592 | tf_op jit(solution)/shard_map/all_gather | solution.py:137
  139.6 3.1 %fusion.2 = bf16[8,64,512]{2,1,0:T(8,128)(2,1)} fusion(bf16[512,8,128,1]{0,2,3,1:T(8,128)(2,1)} %bitcast.233, bf16[8,8,64,128]{3,2,1,0:T(8,128)(2,1)} %all-to-all-done.3), kind=kOutput, calls=%fused_computation.4 | convolution fusion | flops 537133056 | bytes 2621440 | tf_op jit(solution)/shard_map/dot_general | solution.py:141
  142.7 4.7 %all-to-all-start.4 = ((bf16[8,64,512]{2,1,0:T(8,128)(2,1)}), bf16[8,64,512]{2,1,0:T(8,128)(2,1)S(1)}, u32[]{:S(2)}, u32[]{:S(2)}) async-start(bf16[8,64,512]{2,1,0:T(8,128)(2,1)} %fusion.2), calls=%async_computation.5 | async-start | bytes 1048576 | tf_op jit(solution)/shard_map/all_to_all | solution.py:144
  151.7 12.2 %reduce-scatter.2.cloned.1.call-done = bf16[1024,128]{0,1:T(8,128)(2,1)} async-done(((bf16[4096,128]{0,1:T(8,128)(2,1)}), bf16[1024,128]{0,1:T(8,128)(2,1)}) %reduce-scatter.2.cloned.1.call-update) | async-done | bytes 262160 | tf_op jit(solution)/shard_map/reduce_scatter | solution.py:171
  164.0 1.8 %copy.319 = bf16[1024,128]{1,0:T(8,128)(2,1)} copy(bf16[1024,128]{0,1:T(8,128)(2,1)} %reduce-scatter.2.cloned.1.call-done) | data formatting | bytes 524288
  (126 shorter events, 27.6 us)
Async XLA Ops:
  7.2 8.2 %copy-start = (f32[1,8,8192]{2,1,0:T(8,128)S(1)}, f32[1,8,8192]{2,1,0:T(8,128)}, u32[]{:S(2)}) copy-start(f32[1,8,8192]{2,1,0:T(8,128)} %param.11) | copy-start | bytes 786436
  7.2 10.5 %copy-start.27 = (f32[3,512,7]{1,2,0:T(8,128)S(1)}, f32[3,512,7]{1,2,0:T(8,128)}, u32[]{:S(2)}) copy-start(f32[3,512,7]{1,2,0:T(8,128)} %param.10) | copy-start | bytes 129028
  7.2 46.2 %all-gather.3.cloned.1.call-start = ((), (), s32[]{:S(2)}) async-start(), calls=%async_computation.6 | async-start | bytes 1310720 | tf_op jit(solution)/shard_map/all_gather | solution.py:164
  10.3 4.5 %copy-start.13 = (bf16[512,128]{0,1:T(8,128)(2,1)}, bf16[512,128]{0,1:T(8,128)(2,1)S(1)}, u32[]{:S(2)}) copy-start(bf16[512,128]{0,1:T(8,128)(2,1)S(1)} %copy.241) | copy-start | bytes 393220
  11.0 7.5 %collective-permute-start = (bf16[3,512,6]{1,2,0:T(8,128)(2,1)}, bf16[3,512,6]{1,2,0:T(8,128)(2,1)}, u32[]{:S(2)}, u32[]{:S(2)}) collective-permute-start(bf16[3,512,6]{1,2,0:T(8,128)(2,1)} %pad_maximum_fusion.3), channel_id=1, source_target_pairs={{0,4},{4,8},{8,12},{12,16},{16,20},{20,24},{24,28},{28,32},{32,36}... | collective-permute-start | bytes 55304 | tf_op jit(solution)/shard_map/ppermute | solution.py:22
  14.8 62.8 %copy-start.4 = (f32[128,128]{0,1:T(8,128)}, f32[128,128]{0,1:T(8,128)S(1)}, u32[]{:S(2)}) copy-start(f32[128,128]{0,1:T(8,128)S(1)} %sine_negate_fusion.1) | copy-start | bytes 196612
  15.1 37.4 %copy-start.7 = (f32[128,128]{0,1:T(8,128)}, f32[128,128]{0,1:T(8,128)S(1)}, u32[]{:S(2)}) copy-start(f32[128,128]{0,1:T(8,128)S(1)} %fusion.125) | copy-start | bytes 196612
  16.3 3.1 %copy-start.10 = (f32[128,128]{1,0:T(8,128)}, f32[128,128]{1,0:T(8,128)S(1)}, u32[]{:S(2)}) copy-start(f32[128,128]{1,0:T(8,128)S(1)} %copy.253) | copy-start | bytes 196612
  16.4 3.0 %copy-start.11 = (f32[128,128]{1,0:T(8,128)}, f32[128,128]{1,0:T(8,128)S(1)}, u32[]{:S(2)}) copy-start(f32[128,128]{1,0:T(8,128)S(1)} %copy.251) | copy-start | bytes 196612
  20.1 33.3 %copy-start.2 = (bf16[3,512,128]{1,2,0:T(8,128)(2,1)}, bf16[3,512,128]{1,2,0:T(8,128)(2,1)S(1)}, u32[]{:S(2)}) copy-start(bf16[3,512,128]{1,2,0:T(8,128)(2,1)S(1)} %fusion.19) | copy-start | bytes 1179652
  20.9 22.5 %all-to-all-start = ((bf16[64,8,128]{2,1,0:T(8,128)(2,1)}), bf16[64,8,128]{2,1,0:T(8,128)(2,1)}, u32[]{:S(2)}, u32[]{:S(2)}) async-start(bf16[64,8,128]{2,1,0:T(8,128)(2,1)} %bitcast.5), calls=%async_computation | async-start | bytes 262144 | tf_op jit(solution)/shard_map/all_to_all | solution.py:108
  57.4 20.5 %copy-start.8 = (f32[128,128]{0,1:T(8,128)S(1)}, f32[128,128]{0,1:T(8,128)}, u32[]{:S(2)}) copy-start(f32[128,128]{0,1:T(8,128)} %copy-done.7) | copy-start | bytes 196612
  58.5 18.3 %all-to-all-start.1 = ((bf16[64,2,8,128]{3,2,1,0:T(8,128)(2,1)}), bf16[64,2,8,128]{3,2,1,0:T(8,128)(2,1)S(1)}, u32[]{:S(2)}, u32[]{:S(2)}) async-start(bf16[64,2,8,128]{3,2,1,0:T(8,128)(2,1)} %copy.276), calls=%async_computation.1 | async-start | bytes 524288 | tf_op jit(solution)/shard_map/all_to_all | solution.py:126
  67.0 72.6 %all-gather.5.cloned.1.call-start = ((), (), s32[]{:S(2)}) async-start(), calls=%async_computation.8 | async-start | bytes 1179648 | tf_op jit(solution)/shard_map/all_gather | solution.py:137
  86.1 2.6 %copy-start.3 = (bf16[3,512,128]{1,2,0:T(8,128)(2,1)S(1)}, bf16[3,512,128]{1,2,0:T(8,128)(2,1)}, u32[]{:S(2)}) copy-start(bf16[3,512,128]{1,2,0:T(8,128)(2,1)} %copy-done.2) | copy-start | bytes 1179652
  86.1 2.6 %copy-start.15 = (f32[512,128]{0,1:T(8,128)S(1)}, f32[512,128]{0,1:T(8,128)}, u32[]{:S(2)}) copy-start(f32[512,128]{0,1:T(8,128)} %copy.278) | copy-start | bytes 786436
  86.1 2.6 %copy-start.16 = (f32[512,128]{0,1:T(8,128)S(1)}, f32[512,128]{0,1:T(8,128)}, u32[]{:S(2)}) copy-start(f32[512,128]{0,1:T(8,128)} %get-tuple-element.55) | copy-start | bytes 786436
  86.1 3.4 %copy-start.9 = (f32[128,128]{0,1:T(8,128)S(1)}, f32[128,128]{0,1:T(8,128)}, u32[]{:S(2)}) copy-start(f32[128,128]{0,1:T(8,128)} %copy-done.7) | copy-start | bytes 196612
  86.1 3.9 %copy-start.5 = (f32[128,128]{0,1:T(8,128)S(1)}, f32[128,128]{0,1:T(8,128)}, u32[]{:S(2)}) copy-start(f32[128,128]{0,1:T(8,128)} %copy-done.4) | copy-start | bytes 196612
  87.4 13.6 %copy-start.1 = (f32[8,128,128]{2,1,0:T(8,128)S(1)}, f32[8,128,128]{2,1,0:T(8,128)}, u32[]{:S(2)}) copy-start(f32[8,128,128]{2,1,0:T(8,128)} %get-tuple-element.30) | copy-start | bytes 1572868
  91.2 17.5 %all-to-all-start.2 = ((bf16[8,64,128]{2,0,1:T(8,128)(2,1)}), bf16[8,64,128]{2,0,1:T(8,128)(2,1)}, u32[]{:S(2)}, u32[]{:S(2)}) async-start(bf16[8,64,128]{2,0,1:T(8,128)(2,1)} %copy.301), calls=%async_computation.3 | async-start | bytes 262144 | tf_op jit(solution)/shard_map/all_to_all | solution.py:112
  107.0 12.6 %copy-start.12 = (bf16[1,512,128]{1,2,0:T(8,128)(2,1)S(1)}, bf16[1,512,128]{1,2,0:T(8,128)(2,1)}, u32[]{:S(2)}) copy-start(bf16[1,512,128]{1,2,0:T(8,128)(2,1)} %get-tuple-element.43) | copy-start | bytes 393220
  108.7 19.2 %all-to-all-start.3 = ((bf16[8,8,64,128]{3,2,1,0:T(8,128)(2,1)}), bf16[8,8,64,128]{3,2,1,0:T(8,128)(2,1)}, u32[]{:S(2)}, u32[]{:S(2)}) async-start(bf16[8,8,64,128]{3,2,1,0:T(8,128)(2,1)} %copy.316), calls=%async_computation.4 | async-start | bytes 2097152 | tf_op jit(solution)/shard_map/all_to_all | solution.py:140
  117.3 46.7 %reduce-scatter.2.cloned.1.call-start = ((), (), s32[]{:S(2)}) async-start(), calls=%async_computation.7 | async-start | bytes 1310720 | tf_op jit(solution)/shard_map/reduce_scatter | solution.py:171
  118.0 29.4 %copy-start.6 = (f32[128,128]{0,1:T(8,128)S(1)}, f32[128,128]{0,1:T(8,128)}, u32[]{:S(2)}) copy-start(f32[128,128]{0,1:T(8,128)} %copy-done.4) | copy-start | bytes 196612
  119.6 29.0 %collective-permute-start.1 = (bf16[3,512,6]{1,2,0:T(8,128)(2,1)S(1)}, bf16[3,512,6]{1,2,0:T(8,128)(2,1)S(1)}, u32[]{:S(2)}, u32[]{:S(2)}) collective-permute-start(bf16[3,512,6]{1,2,0:T(8,128)(2,1)S(1)} %pad_maximum_fusion.1), channel_id=1, source_target_pairs={{4,0},{8,4},{12,8},{16,12},{20,16},{24,20},{28,24},{32,28},{36,32}... | collective-permute-start | bytes 55304 | tf_op jit(solution)/shard_map/ppermute | solution.py:22
  139.6 9.1 %copy-start.18 = (f32[3,512]{1,0:T(4,128)S(1)}, f32[3,512]{1,0:T(4,128)}, u32[]{:S(2)}) copy-start(f32[3,512]{1,0:T(4,128)} %copy-done.17) | copy-start | bytes 18436
  139.6 9.1 %copy-start.20 = (f32[3,512]{1,0:T(4,128)S(1)}, f32[3,512]{1,0:T(4,128)}, u32[]{:S(2)}) copy-start(f32[3,512]{1,0:T(4,128)} %copy-done.19) | copy-start | bytes 18436
  139.6 9.1 %copy-start.22 = (f32[3,512]{1,0:T(4,128)S(1)}, f32[3,512]{1,0:T(4,128)}, u32[]{:S(2)}) copy-start(f32[3,512]{1,0:T(4,128)} %copy-done.21) | copy-start | bytes 18436
  139.6 9.1 %copy-start.24 = (f32[3,512]{1,0:T(4,128)S(1)}, f32[3,512]{1,0:T(4,128)}, u32[]{:S(2)}) copy-start(f32[3,512]{1,0:T(4,128)} %copy-done.23) | copy-start | bytes 18436
  139.6 9.1 %copy-start.26 = (f32[3,512,1]{1,0,2:T(4,128)S(1)}, f32[3,512,1]{1,0,2:T(4,128)}, u32[]{:S(2)}) copy-start(f32[3,512,1]{1,0,2:T(4,128)} %copy-done.25) | copy-start | bytes 18436
  142.7 23.1 %all-to-all-start.4 = ((bf16[8,64,512]{2,1,0:T(8,128)(2,1)}), bf16[8,64,512]{2,1,0:T(8,128)(2,1)S(1)}, u32[]{:S(2)}, u32[]{:S(2)}) async-start(bf16[8,64,512]{2,1,0:T(8,128)(2,1)} %fusion.2), calls=%async_computation.5 | async-start | bytes 1048576 | tf_op jit(solution)/shard_map/all_to_all | solution.py:144
  (6 other events, 6.9 us)
Sparse Core Ops, SparseCore 0:
  14.6 25.6 all-gather.2
  89.6 49.8 all-gather.4
  142.1 21.7 reduce-scatter.1
where the time goes:
time: 176 us; the launch traced here: 173 us
  starting transfers between devices  51.8 us (29%)
  waiting for transfers between devices  45.3 us (26%)
  matrix products  39.4 us (22%)
  local copies, waits for them, and re-layouts  15 us (9%)
  between operations  14.6 us (8%)
  other arithmetic  6.96 us (4%)
    all_to_all x1, starting transfers between devices, to_channels(): return lax.all_to_all(block, CTX, split_axis=0, concat_axis=1, tiled=True)  14.2 us
    reduce_scatter x1, waiting for transfers between devices, per_device(): lax.psum_scatter(jnp.dot(out_weight, gated_out, preferred_element_type=jn...  12.2 us
    all_gather x1, waiting for transfers between devices, weight_gradient(): group_gated = lax.all_gather(gated_out, CTX_LO, axis=1, tiled=True)  11.7 us
    all_to_all x1, starting transfers between devices, to_positions(): return lax.all_to_all(block, CTX, split_axis=1, concat_axis=0, tiled=True)  9.16 us
    all_to_all x1, starting transfers between devices, weight_gradient(): lax.all_to_all(by_target, CTX_LO, split_axis=0, concat_axis=0, tiled=True)  8.59 us
    all_to_all x1, starting transfers between devices, swap_layouts(): lax.all_to_all(outgoing, CTX, split_axis=0, concat_axis=0, tiled=True)  8.56 us
    unnamed x67, local copies, waits for them, and re-layouts  7.28 us
    all_to_all x1, waiting for transfers between devices, swap_layouts(): lax.all_to_all(outgoing, CTX, split_axis=0, concat_axis=0, tiled=True)  7.19 us
  transfers between devices with their start and end apart: 10, of which 6 were waited for; matrix products, arithmetic and copies ran while one was open for 23% of the time, Pallas kernels for 0%

commit v1 on v0

--- a/solution.py
+++ b/solution.py
@@ -154,8 +154,12 @@
     product = (shorts[1].astype(jnp.float32) * shorts[2].astype(jnp.float32)).astype(jnp.bfloat16)
     product_chan = to_channels(product)
     tables = make_tables(product_chan.shape[1], BLOCK)
-    kernel_re, kernel_im = spectrum(filters[0], tables)
-    product_re, product_im = spectrum(product_chan.astype(jnp.float32), tables)
+    channels = product_chan.shape[0]
+    joint_re, joint_im = spectrum(
+        jnp.concatenate([filters[0], product_chan.astype(jnp.float32)]), tables
+    )
+    kernel_re, product_re = joint_re[:channels], joint_re[channels:]
+    kernel_im, product_im = joint_im[:channels], joint_im[channels:]
     convolved_chan = inverse(
         product_re * kernel_re - product_im * kernel_im,
         product_re * kernel_im + product_im * kernel_re,
@@ -176,16 +180,23 @@
     )
     grad_out_weight = weight_gradient(full_cotangent, gated_out)
     gradient_re, gradient_im = spectrum(grad_chan.astype(jnp.float32), tables)
-    grad_product_chan = inverse(
-        kernel_re * gradient_re + kernel_im * gradient_im,
-        kernel_re * gradient_im - kernel_im * gradient_re,
+    pair = inverse(
+        jnp.concatenate(
+            [
+                kernel_re * gradient_re + kernel_im * gradient_im,
+                product_re * gradient_re + product_im * gradient_im,
+            ]
+        ),
+        jnp.concatenate(
+            [
+                kernel_re * gradient_im - kernel_im * gradient_re,
+                product_re * gradient_im - product_im * gradient_re,
+            ]
+        ),
         tables,
-    ).astype(jnp.bfloat16)
-    grad_filters = inverse(
-        product_re * gradient_re + product_im * gradient_im,
-        product_re * gradient_im - product_im * gradient_re,
-        tables,
-    ).reshape(filters.shape)
+    )
+    grad_product_chan = pair[:channels].astype(jnp.bfloat16)
+    grad_filters = pair[channels:].reshape(filters.shape)
     derivative_of_multiple = to_positions(grad_product_chan)
     grad_shorts = jnp.stack(
         [

time: 176 us -> 173 us (0.983); the launches traced: 173 us -> 172 us
  blocking collectives: 0 us -> 17.9 us
  starting transfers between devices: 51.8 us -> 41 us
  matrix products: 39.4 us -> 33.3 us
    all_to_all x0 -> x1, blocking collectives: none -> 17.9 us  [swap_layouts(): lax.all_to_all(outgoing, CTX, split_axis=0, concat_axis=0, tiled=True)]
    ppermute x2, waiting for transfers between devices: 0.01 us -> 13.6 us  [from_behind(): lax.ppermute(value, axis, [(source, source + steps) for source in range(f...]
    reduce_scatter x1, waiting for transfers between devices: 12.2 us -> 0.01 us  [per_device(): lax.psum_scatter(jnp.dot(out_weight, gated_out, preferred_element_type=jn...]
    all_to_all x1 -> x0, starting transfers between devices: 8.56 us -> none  [swap_layouts(): lax.all_to_all(outgoing, CTX, split_axis=0, concat_axis=0, tiled=True)]
    all_to_all x1 -> x0, waiting for transfers between devices: 7.19 us -> none  [swap_layouts(): lax.all_to_all(outgoing, CTX, split_axis=0, concat_axis=0, tiled=True)]
    all_to_all x1, waiting for transfers between devices: 1.7 us -> 7.3 us  [to_positions(): return lax.all_to_all(block, CTX, split_axis=1, concat_axis=0, tiled=True)]
    dot_general x3 -> x2, matrix products: 5.04 us -> 3.04 us  [spectrum(): jnp.matmul(turned_im, inner_re, precision=DFT_PRECISION)]
    unnamed x67 -> x50, local copies, waits for them, and re-layouts: 7.28 us -> 7.26 us
  transfers between devices with their start and end apart: 10 -> 9, of which waited for: 6 -> 6; matrix products, arithmetic and copies ran while one was open for 23% -> 24% of each run, Pallas kernels for 0% -> 0%
where the time goes in v1:
time: 173 us; the launch traced here: 172 us
  waiting for transfers between devices  45.3 us (26%)
  starting transfers between devices  41 us (24%)
  matrix products  33.3 us (19%)
  blocking collectives  17.9 us (10%)
  between operations  14.4 us (8%)
  local copies, waits for them, and re-layouts  14.3 us (8%)
  other arithmetic  5.87 us (3%)
    all_to_all x1, blocking collectives, swap_layouts(): lax.all_to_all(outgoing, CTX, split_axis=0, concat_axis=0, tiled=True)  17.9 us
    all_to_all x1, starting transfers between devices, to_channels(): return lax.all_to_all(block, CTX, split_axis=0, concat_axis=1, tiled=True)  15.5 us
    ppermute x2, waiting for transfers between devices, from_behind(): lax.ppermute(value, axis, [(source, source + steps) for source in range(f...  13.6 us
    all_gather x1, waiting for transfers between devices, weight_gradient(): group_gated = lax.all_gather(gated_out, CTX_LO, axis=1, tiled=True)  10.4 us
    all_to_all x1, starting transfers between devices, to_positions(): return lax.all_to_all(block, CTX, split_axis=1, concat_axis=0, tiled=True)  8.35 us
    all_to_all x1, starting transfers between devices, weight_gradient(): lax.all_to_all(by_target, CTX_LO, split_axis=0, concat_axis=0, tiled=True)  7.97 us
    all_to_all x1, waiting for transfers between devices, to_positions(): return lax.all_to_all(block, CTX, split_axis=1, concat_axis=0, tiled=True)  7.3 us
    unnamed x50, local copies, waits for them, and re-layouts  7.26 us
  transfers between devices with their start and end apart: 9, of which 6 were waited for; matrix products, arithmetic and copies ran while one was open for 24% of the time, Pallas kernels for 0%

profile of v1, /device:TPU:22, one launch (start us, length us, event | category | flops | bytes accessed | tf_op | source)
XLA Modules:
  0.0 172.1 jit_solution(15793337141172881837)
XLA Ops:
  7.9 1.0 copy.163
  8.9 1.0 copy.164
  9.9 1.0 copy.165
  11.0 3.5 %collective-permute-start = (bf16[3,512,6]{1,2,0:T(8,128)(2,1)S(1)}, bf16[3,512,6]{1,2,0:T(8,128)(2,1)S(1)}, u32[]{:S(2)}, u32[]{:S(2)}) collective-permute-start(bf16[3,512,6]{1,2,0:T(8,128)(2,1)S(1)} %pad_maximum_fusion.12), channel_id=1, source_target_pairs={{0,4},{4,8},{8,12},{12,16},{16,20},{20,24},{24,28},{28,32},{32,36}... | collective-permute-start | bytes 55304 | tf_op jit(solution)/shard_map/ppermute | solution.py:22
  14.5 1.2 fusion.167
  18.3 15.5 %all-to-all-start = ((bf16[64,8,128]{2,1,0:T(8,128)(2,1)}), bf16[64,8,128]{2,1,0:T(8,128)(2,1)S(1)}, u32[]{:S(2)}, u32[]{:S(2)}) async-start(bf16[64,8,128]{2,1,0:T(8,128)(2,1)} %bitcast.5), calls=%async_computation | async-start | bytes 262144 | tf_op jit(solution)/shard_map/all_to_all | solution.py:108
  35.2 7.1 %all-to-all-done = bf16[64,8,128]{2,1,0:T(8,128)(2,1)S(1)} async-done(((bf16[64,8,128]{2,1,0:T(8,128)(2,1)}), bf16[64,8,128]{2,1,0:T(8,128)(2,1)S(1)}, u32[]{:S(2)}, u32[]{:S(2)}) %all-to-all-start) | async-done | bytes 131104 | tf_op jit(solution)/shard_map/all_to_all | solution.py:108
  42.3 1.0 convolution_bitcast_fusion
  44.3 1.2 fusion.42
  45.5 1.2 fusion.43
  46.7 1.2 convolution_add_fusion.1
  47.9 1.2 convolution_subtract_fusion.1
  52.5 4.0 %fusion.47 = (bf16[512,128]{0,1:T(8,128)(2,1)S(1)}, f32[512,128]{0,1:T(8,128)}) fusion(bf16[3,512,128]{1,2,0:T(8,128)(2,1)S(1)} %fusion.25, bf16[4096,512]{1,0:T(8,128)(2,1)} %param.12, bf16[4096,128]{1,0:T(8,128)(2,1)} %all-gather.3.cloned.1.call-done), kind=kOutput, calls=%fused_computation.98 | convolution fusion | flops 537067520 | bytes 5767168 | tf_op jit(solution)/shard_map/dot_general | solution.py:169
  56.9 17.9 %all_to_all.35 = bf16[64,2,8,128]{3,2,1,0:T(8,128)(2,1)S(1)} all-to-all(bf16[64,2,8,128]{3,2,1,0:T(8,128)(2,1)S(1)} %copy.186), channel_id=1, replica_groups=mesh['ctx_hi'=8,'ctx_lo'=8,'tp'=4] {'ctx_hi','ctx_lo'}, dimensions={0} | all-to-all | bytes 524288 | tf_op jit(solution)/shard_map/all_to_all | solution.py:126
  76.2 1.4 fusion.55
  77.7 1.4 fusion.56
  79.1 1.8 %copy.188 = f32[512,128]{0,1:T(8,128)} copy(f32[512,128]{1,0:T(8,128)} %get-tuple-element.44) | data formatting | bytes 524288 | tf_op jit(solution)/shard_map/convert_element_type | solution.py:174
  80.9 1.8 %fusion.53 = (bf16[1,512,128]{1,2,0:T(8,128)(2,1)S(1)}, bf16[512,128]{0,1:T(8,128)(2,1)}) fusion(f32[512,128]{0,1:T(8,128)} %get-tuple-element.53, f32[512,128]{0,1:T(8,128)} %copy.188, bf16[3,512,128]{1,2,0:T(8,128)(2,1)} %copy-done), kind=kLoop, calls=%fused_computation.110 | loop fusion | flops 327680 | bytes 917504 | tf_op jit(solution)/shard_map/stack | solution.py:201
  82.7 1.7 convolution_subtract_fusion.2
  84.4 1.9 %multiply_add_fusion.2 = (f32[8,128,128]{2,1,0:T(8,128)S(1)}, f32[8,128,128]{2,1,0:T(8,128)S(1)}, f32[8,128,128]{2,1,0:T(8,128)S(1)}, f32[8,128,128]{2,1,0:T(8,128)S(1)}) fusion(f32[8,128,128]{2,1,0:T(8,128)S(1)} %convolution_subtract_fusion.2, f32[16,128,128]{2,1,0:T(8,128)S(1)} %convolution_add_fusion.1, ...), kind=kOutput, calls=%fused_computation.70 | convolution fusion | flops 102989824 | bytes 6422528 | tf_op jit(solution)/shard_map/dot_general | solution.py:57
  92.0 8.3 %all-to-all-start.2 = ((bf16[8,64,128]{2,0,1:T(8,128)(2,1)}), bf16[8,64,128]{2,0,1:T(8,128)(2,1)S(1)}, u32[]{:S(2)}, u32[]{:S(2)}) async-start(bf16[8,64,128]{2,0,1:T(8,128)(2,1)} %copy.209), calls=%async_computation.3 | async-start | bytes 262144 | tf_op jit(solution)/shard_map/all_to_all | solution.py:112
  100.4 1.1 copy.212
  101.4 7.3 %all-to-all-done.2 = bf16[8,64,128]{2,0,1:T(8,128)(2,1)S(1)} async-done(((bf16[8,64,128]{2,0,1:T(8,128)(2,1)}), bf16[8,64,128]{2,0,1:T(8,128)(2,1)S(1)}, u32[]{:S(2)}, u32[]{:S(2)}) %all-to-all-start.2) | async-done | bytes 131104 | tf_op jit(solution)/shard_map/all_to_all | solution.py:112
  108.7 8.0 %all-to-all-start.3 = ((bf16[8,8,64,128]{3,2,1,0:T(8,128)(2,1)}), bf16[8,8,64,128]{3,2,1,0:T(8,128)(2,1)S(1)}, u32[]{:S(2)}, u32[]{:S(2)}) async-start(bf16[8,8,64,128]{3,2,1,0:T(8,128)(2,1)} %copy.212), calls=%async_computation.4 | async-start | bytes 2097152 | tf_op jit(solution)/shard_map/all_to_all | solution.py:140
  116.7 4.7 %fusion = bf16[4096,128]{0,1:T(8,128)(2,1)} fusion(bf16[512,128]{0,1:T(8,128)(2,1)S(1)} %copy-done.2, bf16[4096,512]{1,0:T(8,128)(2,1)} %param.12), kind=kOutput, calls=%fused_computation.1 | convolution fusion | flops 537395200 | bytes 5373952 | tf_op jit(solution)/shard_map/dot_general | solution.py:176
  121.6 6.1 %all-to-all-done.3 = bf16[8,8,64,128]{3,2,1,0:T(8,128)(2,1)S(1)} async-done(((bf16[8,8,64,128]{3,2,1,0:T(8,128)(2,1)}), bf16[8,8,64,128]{3,2,1,0:T(8,128)(2,1)S(1)}, u32[]{:S(2)}, u32[]{:S(2)}) %all-to-all-start.3) | async-done | bytes 1048608 | tf_op jit(solution)/shard_map/all_to_all | solution.py:140
  127.7 10.4 %all-gather.5.cloned.1.call-done = bf16[512,1024]{0,1:T(8,128)(2,1)} async-done(((bf16[512,128]{0,1:T(8,128)(2,1)}), bf16[512,1024]{0,1:T(8,128)(2,1)}) %all-gather.5.cloned.1.call-update) | async-done | bytes 1048592 | tf_op jit(solution)/shard_map/all_gather | solution.py:137
  138.1 2.8 %fusion.2 = bf16[8,64,512]{2,1,0:T(8,128)(2,1)} fusion(bf16[512,8,128,1]{0,2,3,1:T(8,128)(2,1)} %bitcast.183, bf16[8,8,64,128]{3,2,1,0:T(8,128)(2,1)S(1)} %all-to-all-done.3), kind=kOutput, calls=%fused_computation.10 | convolution fusion | flops 537133056 | bytes 2621440 | tf_op jit(solution)/shard_map/dot_general | solution.py:141
  140.9 3.5 %all-to-all-start.4 = ((bf16[8,64,512]{2,1,0:T(8,128)(2,1)}), bf16[8,64,512]{2,1,0:T(8,128)(2,1)S(1)}, u32[]{:S(2)}, u32[]{:S(2)}) async-start(bf16[8,64,512]{2,1,0:T(8,128)(2,1)} %fusion.2), calls=%async_computation.5 | async-start | bytes 1048576 | tf_op jit(solution)/shard_map/all_to_all | solution.py:144
  144.5 1.9 %collective-permute-start.1 = (bf16[3,512,6]{1,2,0:T(8,128)(2,1)S(1)}, bf16[3,512,6]{1,2,0:T(8,128)(2,1)S(1)}, u32[]{:S(2)}, u32[]{:S(2)}) collective-permute-start(bf16[3,512,6]{1,2,0:T(8,128)(2,1)S(1)} %pad_maximum_fusion.10), channel_id=1, source_target_pairs={{4,0},{8,4},{12,8},{16,12},{20,16},{24,20},{28,24},{32,28},{36,32}... | collective-permute-start | bytes 55304 | tf_op jit(solution)/shard_map/ppermute | solution.py:22
  147.2 12.7 %collective-permute-done.1 = bf16[3,512,6]{1,2,0:T(8,128)(2,1)S(1)} collective-permute-done((bf16[3,512,6]{1,2,0:T(8,128)(2,1)S(1)}, bf16[3,512,6]{1,2,0:T(8,128)(2,1)S(1)}, u32[]{:S(2)}, u32[]{:S(2)}) %collective-permute-start.1) | collective-permute-done | bytes 18464 | tf_op jit(solution)/shard_map/ppermute | solution.py:22
  163.0 1.8 %copy.215 = bf16[1024,128]{1,0:T(8,128)(2,1)} copy(bf16[1024,128]{0,1:T(8,128)(2,1)} %reduce-scatter.2.cloned.1.call-done) | data formatting | bytes 524288
  (100 shorter events, 21.1 us)
Async XLA Ops:
  7.2 45.4 %all-gather.3.cloned.1.call-start = ((), (), s32[]{:S(2)}) async-start(), calls=%async_computation.6 | async-start | bytes 1310720 | tf_op jit(solution)/shard_map/all_gather | solution.py:168
  11.0 5.7 %collective-permute-start = (bf16[3,512,6]{1,2,0:T(8,128)(2,1)S(1)}, bf16[3,512,6]{1,2,0:T(8,128)(2,1)S(1)}, u32[]{:S(2)}, u32[]{:S(2)}) collective-permute-start(bf16[3,512,6]{1,2,0:T(8,128)(2,1)S(1)} %pad_maximum_fusion.12), channel_id=1, source_target_pairs={{0,4},{4,8},{8,12},{12,16},{16,20},{20,24},{24,28},{28,32},{32,36}... | collective-permute-start | bytes 55304 | tf_op jit(solution)/shard_map/ppermute | solution.py:22
  15.7 18.7 %copy-start.9 = (f32[3,512]{1,0:T(4,128)}, f32[3,512]{1,0:T(4,128)S(1)}, u32[]{:S(2)}) copy-start(f32[3,512]{1,0:T(4,128)S(1)} %get-tuple-element.58) | copy-start | bytes 18436
  15.7 18.7 %copy-start.11 = (f32[3,512]{1,0:T(4,128)}, f32[3,512]{1,0:T(4,128)S(1)}, u32[]{:S(2)}) copy-start(f32[3,512]{1,0:T(4,128)S(1)} %get-tuple-element.59) | copy-start | bytes 18436
  15.7 18.7 %copy-start.13 = (f32[3,512]{1,0:T(4,128)}, f32[3,512]{1,0:T(4,128)S(1)}, u32[]{:S(2)}) copy-start(f32[3,512]{1,0:T(4,128)S(1)} %get-tuple-element.54) | copy-start | bytes 18436
  15.8 18.7 %copy-start.15 = (f32[3,512]{1,0:T(4,128)}, f32[3,512]{1,0:T(4,128)S(1)}, u32[]{:S(2)}) copy-start(f32[3,512]{1,0:T(4,128)S(1)} %get-tuple-element.55) | copy-start | bytes 18436
  15.8 18.7 %copy-start.17 = (f32[3,512,1]{1,0,2:T(4,128)}, f32[3,512,1]{1,0,2:T(4,128)S(1)}, u32[]{:S(2)}) copy-start(f32[3,512,1]{1,0,2:T(4,128)S(1)} %copy.297) | copy-start | bytes 18436
  15.8 18.8 %copy-start.8 = (f32[1,8,8192]{2,1,0:T(8,128)S(1)}, f32[1,8,8192]{2,1,0:T(8,128)}, u32[]{:S(2)}) copy-start(f32[1,8,8192]{2,1,0:T(8,128)} %param.11) | copy-start | bytes 786436
  17.5 35.1 %copy-start = (bf16[3,512,128]{1,2,0:T(8,128)(2,1)}, bf16[3,512,128]{1,2,0:T(8,128)(2,1)S(1)}, u32[]{:S(2)}) copy-start(bf16[3,512,128]{1,2,0:T(8,128)(2,1)S(1)} %fusion.25) | copy-start | bytes 1179652
  18.3 24.0 %all-to-all-start = ((bf16[64,8,128]{2,1,0:T(8,128)(2,1)}), bf16[64,8,128]{2,1,0:T(8,128)(2,1)S(1)}, u32[]{:S(2)}, u32[]{:S(2)}) async-start(bf16[64,8,128]{2,1,0:T(8,128)(2,1)} %bitcast.5), calls=%async_computation | async-start | bytes 262144 | tf_op jit(solution)/shard_map/all_to_all | solution.py:108
  33.8 104.3 %all-gather.5.cloned.1.call-start = ((), (), s32[]{:S(2)}) async-start(), calls=%async_computation.8 | async-start | bytes 1179648 | tf_op jit(solution)/shard_map/all_gather | solution.py:137
  34.9 41.0 %copy-start.6 = (f32[128,128]{0,1:T(8,128)}, f32[128,128]{0,1:T(8,128)S(1)}, u32[]{:S(2)}) copy-start(f32[128,128]{0,1:T(8,128)S(1)} %fusion.87) | copy-start | bytes 196612
  35.2 40.3 %copy-start.4 = (f32[128,128]{0,1:T(8,128)}, f32[128,128]{0,1:T(8,128)S(1)}, u32[]{:S(2)}) copy-start(f32[128,128]{0,1:T(8,128)S(1)} %sine_negate_fusion.1) | copy-start | bytes 196612
  87.1 2.6 %copy-start.7 = (f32[128,128]{0,1:T(8,128)S(1)}, f32[128,128]{0,1:T(8,128)}, u32[]{:S(2)}) copy-start(f32[128,128]{0,1:T(8,128)} %copy-done.6) | copy-start | bytes 196612
  87.9 2.5 %copy-start.5 = (f32[128,128]{0,1:T(8,128)S(1)}, f32[128,128]{0,1:T(8,128)}, u32[]{:S(2)}) copy-start(f32[128,128]{0,1:T(8,128)} %copy-done.4) | copy-start | bytes 196612
  89.7 10.7 %copy-start.3 = (bf16[4096,128]{1,0:T(8,128)(2,1)S(1)}, bf16[4096,128]{1,0:T(8,128)(2,1)}, u32[]{:S(2)}) copy-start(bf16[4096,128]{1,0:T(8,128)(2,1)} %all-gather.3.cloned.1.call-done) | copy-start | bytes 3145732
  90.4 26.3 %copy-start.2 = (bf16[512,128]{0,1:T(8,128)(2,1)S(1)}, bf16[512,128]{0,1:T(8,128)(2,1)}, u32[]{:S(2)}) copy-start(bf16[512,128]{0,1:T(8,128)(2,1)} %get-tuple-element.42) | copy-start | bytes 393220
  92.0 16.7 %all-to-all-start.2 = ((bf16[8,64,128]{2,0,1:T(8,128)(2,1)}), bf16[8,64,128]{2,0,1:T(8,128)(2,1)S(1)}, u32[]{:S(2)}, u32[]{:S(2)}) async-start(bf16[8,64,128]{2,0,1:T(8,128)(2,1)} %copy.209), calls=%async_computation.3 | async-start | bytes 262144 | tf_op jit(solution)/shard_map/all_to_all | solution.py:112
  108.7 18.9 %all-to-all-start.3 = ((bf16[8,8,64,128]{3,2,1,0:T(8,128)(2,1)}), bf16[8,8,64,128]{3,2,1,0:T(8,128)(2,1)S(1)}, u32[]{:S(2)}, u32[]{:S(2)}) async-start(bf16[8,8,64,128]{3,2,1,0:T(8,128)(2,1)} %copy.212), calls=%async_computation.4 | async-start | bytes 2097152 | tf_op jit(solution)/shard_map/all_to_all | solution.py:140
  116.7 46.3 %reduce-scatter.2.cloned.1.call-start = ((), (), s32[]{:S(2)}) async-start(), calls=%async_computation.7 | async-start | bytes 1310720 | tf_op jit(solution)/shard_map/reduce_scatter | solution.py:175
  121.4 23.1 %copy-start.1 = (bf16[3,512,128]{1,2,0:T(8,128)(2,1)S(1)}, bf16[3,512,128]{1,2,0:T(8,128)(2,1)}, u32[]{:S(2)}) copy-start(bf16[3,512,128]{1,2,0:T(8,128)(2,1)} %copy-done) | copy-start | bytes 1179652
  138.1 21.9 %copy-start.10 = (f32[3,512]{1,0:T(4,128)S(1)}, f32[3,512]{1,0:T(4,128)}, u32[]{:S(2)}) copy-start(f32[3,512]{1,0:T(4,128)} %copy-done.9) | copy-start | bytes 18436
  138.1 21.9 %copy-start.12 = (f32[3,512]{1,0:T(4,128)S(1)}, f32[3,512]{1,0:T(4,128)}, u32[]{:S(2)}) copy-start(f32[3,512]{1,0:T(4,128)} %copy-done.11) | copy-start | bytes 18436
  138.1 21.9 %copy-start.14 = (f32[3,512]{1,0:T(4,128)S(1)}, f32[3,512]{1,0:T(4,128)}, u32[]{:S(2)}) copy-start(f32[3,512]{1,0:T(4,128)} %copy-done.13) | copy-start | bytes 18436
  138.1 21.9 %copy-start.16 = (f32[3,512]{1,0:T(4,128)S(1)}, f32[3,512]{1,0:T(4,128)}, u32[]{:S(2)}) copy-start(f32[3,512]{1,0:T(4,128)} %copy-done.15) | copy-start | bytes 18436
  138.1 21.9 %copy-start.18 = (f32[3,512,1]{1,0,2:T(4,128)S(1)}, f32[3,512,1]{1,0,2:T(4,128)}, u32[]{:S(2)}) copy-start(f32[3,512,1]{1,0,2:T(4,128)} %copy-done.17) | copy-start | bytes 18436
  140.9 23.9 %all-to-all-start.4 = ((bf16[8,64,512]{2,1,0:T(8,128)(2,1)}), bf16[8,64,512]{2,1,0:T(8,128)(2,1)S(1)}, u32[]{:S(2)}, u32[]{:S(2)}) async-start(bf16[8,64,512]{2,1,0:T(8,128)(2,1)} %fusion.2), calls=%async_computation.5 | async-start | bytes 1048576 | tf_op jit(solution)/shard_map/all_to_all | solution.py:144
  144.5 15.4 %collective-permute-start.1 = (bf16[3,512,6]{1,2,0:T(8,128)(2,1)S(1)}, bf16[3,512,6]{1,2,0:T(8,128)(2,1)S(1)}, u32[]{:S(2)}, u32[]{:S(2)}) collective-permute-start(bf16[3,512,6]{1,2,0:T(8,128)(2,1)S(1)} %pad_maximum_fusion.10), channel_id=1, source_target_pairs={{4,0},{8,4},{12,8},{16,12},{20,16},{24,20},{28,24},{32,28},{36,32}... | collective-permute-start | bytes 55304 | tf_op jit(solution)/shard_map/ppermute | solution.py:22
Sparse Core Ops, SparseCore 0:
  9.8 25.2 all-gather.2
  82.8 55.2 all-gather.4
  140.7 19.7 reduce-scatter.1

commit v2 on v1

--- a/solution.py
+++ b/solution.py
@@ -178,7 +178,8 @@
         scatter_dimension=0,
         tiled=True,
     )
-    grad_out_weight = weight_gradient(full_cotangent, gated_out)
+    gated_for_weights, mixed_out = lax.optimization_barrier((gated_out, mixed_out))
+    grad_out_weight = weight_gradient(full_cotangent, gated_for_weights)
     gradient_re, gradient_im = spectrum(grad_chan.astype(jnp.float32), tables)
     pair = inverse(
         jnp.concatenate(

time: 173 us -> 194 us (1.12)
  waiting for transfers between devices: 45.3 us -> 66.3 us
  starting transfers between devices: 41 us -> 47.3 us
  matrix products: 33.3 us -> 29.7 us
    reduce_scatter x1, waiting for transfers between devices: 0.01 us -> 13.7 us  [per_device(): lax.psum_scatter(jnp.dot(out_weight, gated_out, preferred_element_type=jn...]
    all_to_all x1, waiting for transfers between devices: 6.12 us -> 13.2 us  [weight_gradient(): lax.all_to_all(by_target, CTX_LO, split_axis=0, concat_axis=0, tiled=True)]
    all_to_all x1, starting transfers between devices: 8.35 us -> 12.9 us  [to_positions(): return lax.all_to_all(block, CTX, split_axis=1, concat_axis=0, tiled=True)]
    unnamed x50 -> x56, local copies, waits for them, and re-layouts: 7.26 us -> 6.32 us
  transfers between devices with their start and end apart: 9 -> 9, of which waited for: 6 -> 7; matrix products, arithmetic and copies ran while one was open for 24% -> 17% of each run, Pallas kernels for 0% -> 0%
where the time goes in v2:
time: 194 us; the launch traced here: 193 us
  waiting for transfers between devices  66.3 us (34%)
  starting transfers between devices  47.3 us (24%)
  matrix products  29.7 us (15%)
  blocking collectives  17.9 us (9%)
  between operations  14.5 us (7%)
  local copies, waits for them, and re-layouts  12.7 us (7%)
  other arithmetic  5.11 us (3%)
    all_to_all x1, blocking collectives, swap_layouts(): lax.all_to_all(outgoing, CTX, split_axis=0, concat_axis=0, tiled=True)  17.9 us
    all_to_all x1, starting transfers between devices, to_channels(): return lax.all_to_all(block, CTX, split_axis=0, concat_axis=1, tiled=True)  15.5 us
    reduce_scatter x1, waiting for transfers between devices, per_device(): lax.psum_scatter(jnp.dot(out_weight, gated_out, preferred_element_type=jn...  13.7 us
    all_to_all x1, waiting for transfers between devices, weight_gradient(): lax.all_to_all(by_target, CTX_LO, split_axis=0, concat_axis=0, tiled=True)  13.2 us
    ppermute x2, waiting for transfers between devices, from_behind(): lax.ppermute(value, axis, [(source, source + steps) for source in range(f...  13 us
    all_to_all x1, starting transfers between devices, to_positions(): return lax.all_to_all(block, CTX, split_axis=1, concat_axis=0, tiled=True)  12.9 us
    all_gather x1, waiting for transfers between devices, weight_gradient(): group_gated = lax.all_gather(gated_out, CTX_LO, axis=1, tiled=True)  10.8 us
    all_to_all x1, starting transfers between devices, weight_gradient(): lax.all_to_all(by_target, CTX_LO, split_axis=0, concat_axis=0, tiled=True)  8 us
  transfers between devices with their start and end apart: 9, of which 7 were waited for; matrix products, arithmetic and copies ran while one was open for 17% of the time, Pallas kernels for 0%

profile of v2, /device:TPU:22, one launch (start us, length us, event | category | flops | bytes accessed | tf_op | source)
XLA Modules:
  0.0 193.4 jit_solution(1338543192031251254)
XLA Ops:
  7.9 1.0 copy.163
  8.9 1.0 copy.164
  9.9 1.0 copy.165
  11.0 3.5 %collective-permute-start = (bf16[3,512,6]{1,2,0:T(8,128)(2,1)S(1)}, bf16[3,512,6]{1,2,0:T(8,128)(2,1)S(1)}, u32[]{:S(2)}, u32[]{:S(2)}) collective-permute-start(bf16[3,512,6]{1,2,0:T(8,128)(2,1)S(1)} %pad_maximum_fusion.12), channel_id=1, source_target_pairs={{0,4},{4,8},{8,12},{12,16},{16,20},{20,24},{24,28},{28,32},{32,36}... | collective-permute-start | bytes 55304 | tf_op jit(solution)/shard_map/ppermute | solution.py:22
  14.5 1.2 fusion.167
  15.8 0.9 collective-permute-done
  18.3 15.5 %all-to-all-start = ((bf16[64,8,128]{2,1,0:T(8,128)(2,1)}), bf16[64,8,128]{2,1,0:T(8,128)(2,1)S(1)}, u32[]{:S(2)}, u32[]{:S(2)}) async-start(bf16[64,8,128]{2,1,0:T(8,128)(2,1)} %bitcast.5), calls=%async_computation | async-start | bytes 262144 | tf_op jit(solution)/shard_map/all_to_all | solution.py:108
  35.2 7.1 %all-to-all-done = bf16[64,8,128]{2,1,0:T(8,128)(2,1)S(1)} async-done(((bf16[64,8,128]{2,1,0:T(8,128)(2,1)}), bf16[64,8,128]{2,1,0:T(8,128)(2,1)S(1)}, u32[]{:S(2)}, u32[]{:S(2)}) %all-to-all-start) | async-done | bytes 131104 | tf_op jit(solution)/shard_map/all_to_all | solution.py:108
  42.4 1.0 convolution_bitcast_fusion
  43.4 1.0 convolution_bitcast_fusion.1
  44.4 1.2 fusion.42
  45.6 1.2 fusion.43
  46.7 1.2 convolution_add_fusion.1
  47.9 1.2 convolution_subtract_fusion.1
  52.6 4.0 %fusion.47 = (bf16[512,128]{0,1:T(8,128)(2,1)S(1)}, f32[512,128]{0,1:T(8,128)}) fusion(bf16[3,512,128]{1,2,0:T(8,128)(2,1)S(1)} %fusion.25, bf16[4096,512]{1,0:T(8,128)(2,1)} %param.12, bf16[4096,128]{1,0:T(8,128)(2,1)} %all-gather.3.cloned.1.call-done), kind=kOutput, calls=%fused_computation.98 | convolution fusion | flops 537067520 | bytes 5767168 | tf_op jit(solution)/shard_map/dot_general | solution.py:169
  56.9 17.9 %all_to_all.35 = bf16[64,2,8,128]{3,2,1,0:T(8,128)(2,1)S(1)} all-to-all(bf16[64,2,8,128]{3,2,1,0:T(8,128)(2,1)S(1)} %copy.186), channel_id=1, replica_groups=mesh['ctx_hi'=8,'ctx_lo'=8,'tp'=4] {'ctx_hi','ctx_lo'}, dimensions={0} | all-to-all | bytes 524288 | tf_op jit(solution)/shard_map/all_to_all | solution.py:126
  75.5 1.1 copy.188
  76.6 1.0 fusion.53
  77.7 4.7 %fusion = bf16[4096,128]{0,1:T(8,128)(2,1)} fusion(bf16[512,128]{0,1:T(8,128)(2,1)S(1)} %get-tuple-element.9, bf16[4096,512]{1,0:T(8,128)(2,1)} %param.12), kind=kOutput, calls=%fused_computation.1 | convolution fusion | flops 537395200 | bytes 5373952 | tf_op jit(solution)/shard_map/dot_general | solution.py:176
  87.7 0.8 convolution_add_fusion
  88.5 13.7 %reduce-scatter.2.cloned.1.call-done = bf16[1024,128]{0,1:T(8,128)(2,1)} async-done(((bf16[4096,128]{0,1:T(8,128)(2,1)}), bf16[1024,128]{0,1:T(8,128)(2,1)}) %reduce-scatter.2.cloned.1.call-update) | async-done | bytes 262160 | tf_op jit(solution)/shard_map/reduce_scatter | solution.py:175
  102.3 0.8 convolution_subtract_fusion
  105.4 12.9 %all-to-all-start.2 = ((bf16[8,64,128]{2,0,1:T(8,128)(2,1)}), bf16[8,64,128]{2,0,1:T(8,128)(2,1)S(1)}, u32[]{:S(2)}, u32[]{:S(2)}) async-start(bf16[8,64,128]{2,0,1:T(8,128)(2,1)} %copy.209), calls=%async_computation.3 | async-start | bytes 262144 | tf_op jit(solution)/shard_map/all_to_all | solution.py:112
  118.3 1.1 copy.212
  119.4 7.7 %all-to-all-done.2 = bf16[8,64,128]{2,0,1:T(8,128)(2,1)S(1)} async-done(((bf16[8,64,128]{2,0,1:T(8,128)(2,1)}), bf16[8,64,128]{2,0,1:T(8,128)(2,1)S(1)}, u32[]{:S(2)}, u32[]{:S(2)}) %all-to-all-start.2) | async-done | bytes 131104 | tf_op jit(solution)/shard_map/all_to_all | solution.py:112
  127.2 8.0 %all-to-all-start.3 = ((bf16[8,8,64,128]{3,2,1,0:T(8,128)(2,1)}), bf16[8,8,64,128]{3,2,1,0:T(8,128)(2,1)S(1)}, u32[]{:S(2)}, u32[]{:S(2)}) async-start(bf16[8,8,64,128]{3,2,1,0:T(8,128)(2,1)} %copy.212), calls=%async_computation.4 | async-start | bytes 2097152 | tf_op jit(solution)/shard_map/all_to_all | solution.py:140
  135.3 13.2 %all-to-all-done.3 = bf16[8,8,64,128]{3,2,1,0:T(8,128)(2,1)S(1)} async-done(((bf16[8,8,64,128]{3,2,1,0:T(8,128)(2,1)}), bf16[8,8,64,128]{3,2,1,0:T(8,128)(2,1)S(1)}, u32[]{:S(2)}, u32[]{:S(2)}) %all-to-all-start.3) | async-done | bytes 1048608 | tf_op jit(solution)/shard_map/all_to_all | solution.py:140
  148.5 10.8 %all-gather.5.cloned.1.call-done = bf16[512,1024]{0,1:T(8,128)(2,1)} async-done(((bf16[512,128]{0,1:T(8,128)(2,1)}), bf16[512,1024]{0,1:T(8,128)(2,1)}) %all-gather.5.cloned.1.call-update) | async-done | bytes 1048592 | tf_op jit(solution)/shard_map/all_gather | solution.py:137
  159.4 2.8 %fusion.2 = bf16[8,64,512]{2,1,0:T(8,128)(2,1)} fusion(bf16[512,8,128,1]{0,2,3,1:T(8,128)(2,1)} %bitcast.183, bf16[8,8,64,128]{3,2,1,0:T(8,128)(2,1)S(1)} %all-to-all-done.3), kind=kOutput, calls=%fused_computation.10 | convolution fusion | flops 537133056 | bytes 2621440 | tf_op jit(solution)/shard_map/dot_general | solution.py:141
  162.2 4.1 %all-to-all-start.4 = ((bf16[8,64,512]{2,1,0:T(8,128)(2,1)}), bf16[8,64,512]{2,1,0:T(8,128)(2,1)S(1)}, u32[]{:S(2)}, u32[]{:S(2)}) async-start(bf16[8,64,512]{2,1,0:T(8,128)(2,1)} %fusion.2), calls=%async_computation.5 | async-start | bytes 1048576 | tf_op jit(solution)/shard_map/all_to_all | solution.py:144
  166.4 3.0 %collective-permute-start.1 = (bf16[3,512,6]{1,2,0:T(8,128)(2,1)S(1)}, bf16[3,512,6]{1,2,0:T(8,128)(2,1)S(1)}, u32[]{:S(2)}, u32[]{:S(2)}) collective-permute-start(bf16[3,512,6]{1,2,0:T(8,128)(2,1)S(1)} %pad_maximum_fusion.10), channel_id=1, source_target_pairs={{4,0},{8,4},{12,8},{16,12},{20,16},{24,20},{28,24},{32,28},{36,32}... | collective-permute-start | bytes 55304 | tf_op jit(solution)/shard_map/ppermute | solution.py:22
  170.1 12.1 %collective-permute-done.1 = bf16[3,512,6]{1,2,0:T(8,128)(2,1)S(1)} collective-permute-done((bf16[3,512,6]{1,2,0:T(8,128)(2,1)S(1)}, bf16[3,512,6]{1,2,0:T(8,128)(2,1)S(1)}, u32[]{:S(2)}, u32[]{:S(2)}) %collective-permute-start.1) | collective-permute-done | bytes 18464 | tf_op jit(solution)/shard_map/ppermute | solution.py:22
  (106 shorter events, 21.2 us)
Async XLA Ops:
  7.2 45.4 %all-gather.3.cloned.1.call-start = ((), (), s32[]{:S(2)}) async-start(), calls=%async_computation.6 | async-start | bytes 1310720 | tf_op jit(solution)/shard_map/all_gather | solution.py:168
  11.0 5.7 %collective-permute-start = (bf16[3,512,6]{1,2,0:T(8,128)(2,1)S(1)}, bf16[3,512,6]{1,2,0:T(8,128)(2,1)S(1)}, u32[]{:S(2)}, u32[]{:S(2)}) collective-permute-start(bf16[3,512,6]{1,2,0:T(8,128)(2,1)S(1)} %pad_maximum_fusion.12), channel_id=1, source_target_pairs={{0,4},{4,8},{8,12},{12,16},{16,20},{20,24},{24,28},{28,32},{32,36}... | collective-permute-start | bytes 55304 | tf_op jit(solution)/shard_map/ppermute | solution.py:22
  15.7 18.7 %copy-start.12 = (f32[3,512]{1,0:T(4,128)}, f32[3,512]{1,0:T(4,128)S(1)}, u32[]{:S(2)}) copy-start(f32[3,512]{1,0:T(4,128)S(1)} %get-tuple-element.62) | copy-start | bytes 18436
  15.7 18.7 %copy-start.14 = (f32[3,512]{1,0:T(4,128)}, f32[3,512]{1,0:T(4,128)S(1)}, u32[]{:S(2)}) copy-start(f32[3,512]{1,0:T(4,128)S(1)} %get-tuple-element.63) | copy-start | bytes 18436
  15.7 18.7 %copy-start.16 = (f32[3,512]{1,0:T(4,128)}, f32[3,512]{1,0:T(4,128)S(1)}, u32[]{:S(2)}) copy-start(f32[3,512]{1,0:T(4,128)S(1)} %get-tuple-element.58) | copy-start | bytes 18436
  15.8 18.7 %copy-start.18 = (f32[3,512]{1,0:T(4,128)}, f32[3,512]{1,0:T(4,128)S(1)}, u32[]{:S(2)}) copy-start(f32[3,512]{1,0:T(4,128)S(1)} %get-tuple-element.59) | copy-start | bytes 18436
  15.8 18.7 %copy-start.20 = (f32[3,512,1]{1,0,2:T(4,128)}, f32[3,512,1]{1,0,2:T(4,128)S(1)}, u32[]{:S(2)}) copy-start(f32[3,512,1]{1,0,2:T(4,128)S(1)} %copy.297) | copy-start | bytes 18436
  15.8 18.8 %copy-start.10 = (f32[1,8,8192]{2,1,0:T(8,128)S(1)}, f32[1,8,8192]{2,1,0:T(8,128)}, u32[]{:S(2)}) copy-start(f32[1,8,8192]{2,1,0:T(8,128)} %param.11) | copy-start | bytes 786436
  17.5 59.2 %copy-start = (bf16[3,512,128]{1,2,0:T(8,128)(2,1)}, bf16[3,512,128]{1,2,0:T(8,128)(2,1)S(1)}, u32[]{:S(2)}) copy-start(bf16[3,512,128]{1,2,0:T(8,128)(2,1)S(1)} %fusion.25) | copy-start | bytes 1179652
  18.3 24.0 %all-to-all-start = ((bf16[64,8,128]{2,1,0:T(8,128)(2,1)}), bf16[64,8,128]{2,1,0:T(8,128)(2,1)S(1)}, u32[]{:S(2)}, u32[]{:S(2)}) async-start(bf16[64,8,128]{2,1,0:T(8,128)(2,1)} %bitcast.5), calls=%async_computation | async-start | bytes 262144 | tf_op jit(solution)/shard_map/all_to_all | solution.py:108
  33.8 68.4 %reduce-scatter.2.cloned.1.call-start = ((), (), s32[]{:S(2)}) async-start(), calls=%async_computation.7 | async-start | bytes 1310720 | tf_op jit(solution)/shard_map/reduce_scatter | solution.py:175
  34.9 16.9 %copy-start.7 = (f32[128,128]{0,1:T(8,128)}, f32[128,128]{0,1:T(8,128)S(1)}, u32[]{:S(2)}) copy-start(f32[128,128]{0,1:T(8,128)S(1)} %fusion.87) | copy-start | bytes 196612
  35.2 17.0 %copy-start.4 = (f32[128,128]{0,1:T(8,128)}, f32[128,128]{0,1:T(8,128)S(1)}, u32[]{:S(2)}) copy-start(f32[128,128]{0,1:T(8,128)S(1)} %sine_negate_fusion.1) | copy-start | bytes 196612
  74.8 7.7 %copy-start.5 = (f32[128,128]{0,1:T(8,128)S(1)}, f32[128,128]{0,1:T(8,128)}, u32[]{:S(2)}) copy-start(f32[128,128]{0,1:T(8,128)} %copy-done.4) | copy-start | bytes 196612
  75.5 7.3 %copy-start.8 = (f32[128,128]{0,1:T(8,128)S(1)}, f32[128,128]{0,1:T(8,128)}, u32[]{:S(2)}) copy-start(f32[128,128]{0,1:T(8,128)} %copy-done.7) | copy-start | bytes 196612
  77.7 6.2 %copy-start.2 = (bf16[512,128]{0,1:T(8,128)(2,1)}, bf16[512,128]{0,1:T(8,128)(2,1)S(1)}, u32[]{:S(2)}) copy-start(bf16[512,128]{0,1:T(8,128)(2,1)S(1)} %get-tuple-element.9) | copy-start | bytes 393220
  82.4 77.0 %all-gather.5.cloned.1.call-start = ((), (), s32[]{:S(2)}) async-start(), calls=%async_computation.8 | async-start | bytes 1179648 | tf_op jit(solution)/shard_map/all_gather | solution.py:137
  86.8 16.3 %copy-start.9 = (f32[128,128]{0,1:T(8,128)S(1)}, f32[128,128]{0,1:T(8,128)}, u32[]{:S(2)}) copy-start(f32[128,128]{0,1:T(8,128)} %copy-done.7) | copy-start | bytes 196612
  87.7 16.2 %copy-start.6 = (f32[128,128]{0,1:T(8,128)S(1)}, f32[128,128]{0,1:T(8,128)}, u32[]{:S(2)}) copy-start(f32[128,128]{0,1:T(8,128)} %copy-done.4) | copy-start | bytes 196612
  103.1 15.2 %copy-start.3 = (bf16[4096,128]{1,0:T(8,128)(2,1)S(1)}, bf16[4096,128]{1,0:T(8,128)(2,1)}, u32[]{:S(2)}) copy-start(bf16[4096,128]{1,0:T(8,128)(2,1)} %all-gather.3.cloned.1.call-done) | copy-start | bytes 3145732
  105.4 21.8 %all-to-all-start.2 = ((bf16[8,64,128]{2,0,1:T(8,128)(2,1)}), bf16[8,64,128]{2,0,1:T(8,128)(2,1)S(1)}, u32[]{:S(2)}, u32[]{:S(2)}) async-start(bf16[8,64,128]{2,0,1:T(8,128)(2,1)} %copy.209), calls=%async_computation.3 | async-start | bytes 262144 | tf_op jit(solution)/shard_map/all_to_all | solution.py:112
  119.4 46.9 %copy-start.1 = (bf16[3,512,128]{1,2,0:T(8,128)(2,1)S(1)}, bf16[3,512,128]{1,2,0:T(8,128)(2,1)}, u32[]{:S(2)}) copy-start(bf16[3,512,128]{1,2,0:T(8,128)(2,1)} %copy-done) | copy-start | bytes 1179652
  127.2 21.4 %all-to-all-start.3 = ((bf16[8,8,64,128]{3,2,1,0:T(8,128)(2,1)}), bf16[8,8,64,128]{3,2,1,0:T(8,128)(2,1)S(1)}, u32[]{:S(2)}, u32[]{:S(2)}) async-start(bf16[8,8,64,128]{3,2,1,0:T(8,128)(2,1)} %copy.212), calls=%async_computation.4 | async-start | bytes 2097152 | tf_op jit(solution)/shard_map/all_to_all | solution.py:140
  159.4 23.0 %copy-start.13 = (f32[3,512]{1,0:T(4,128)S(1)}, f32[3,512]{1,0:T(4,128)}, u32[]{:S(2)}) copy-start(f32[3,512]{1,0:T(4,128)} %copy-done.12) | copy-start | bytes 18436
  159.4 23.0 %copy-start.15 = (f32[3,512]{1,0:T(4,128)S(1)}, f32[3,512]{1,0:T(4,128)}, u32[]{:S(2)}) copy-start(f32[3,512]{1,0:T(4,128)} %copy-done.14) | copy-start | bytes 18436
  159.4 23.0 %copy-start.17 = (f32[3,512]{1,0:T(4,128)S(1)}, f32[3,512]{1,0:T(4,128)}, u32[]{:S(2)}) copy-start(f32[3,512]{1,0:T(4,128)} %copy-done.16) | copy-start | bytes 18436
  159.4 23.0 %copy-start.19 = (f32[3,512]{1,0:T(4,128)S(1)}, f32[3,512]{1,0:T(4,128)}, u32[]{:S(2)}) copy-start(f32[3,512]{1,0:T(4,128)} %copy-done.18) | copy-start | bytes 18436
  159.4 23.0 %copy-start.21 = (f32[3,512,1]{1,0,2:T(4,128)S(1)}, f32[3,512,1]{1,0,2:T(4,128)}, u32[]{:S(2)}) copy-start(f32[3,512,1]{1,0,2:T(4,128)} %copy-done.20) | copy-start | bytes 18436
  162.2 24.0 %all-to-all-start.4 = ((bf16[8,64,512]{2,1,0:T(8,128)(2,1)}), bf16[8,64,512]{2,1,0:T(8,128)(2,1)S(1)}, u32[]{:S(2)}, u32[]{:S(2)}) async-start(bf16[8,64,512]{2,1,0:T(8,128)(2,1)} %fusion.2), calls=%async_computation.5 | async-start | bytes 1048576 | tf_op jit(solution)/shard_map/all_to_all | solution.py:144
  166.4 15.8 %collective-permute-start.1 = (bf16[3,512,6]{1,2,0:T(8,128)(2,1)S(1)}, bf16[3,512,6]{1,2,0:T(8,128)(2,1)S(1)}, u32[]{:S(2)}, u32[]{:S(2)}) collective-permute-start(bf16[3,512,6]{1,2,0:T(8,128)(2,1)S(1)} %pad_maximum_fusion.10), channel_id=1, source_target_pairs={{4,0},{8,4},{12,8},{16,12},{20,16},{24,20},{28,24},{32,28},{36,32}... | collective-permute-start | bytes 55304 | tf_op jit(solution)/shard_map/ppermute | solution.py:22
  170.1 15.2 %copy-start.11 = (bf16[1024,128]{0,1:T(8,128)(2,1)S(1)}, bf16[1024,128]{0,1:T(8,128)(2,1)}, u32[]{:S(2)}) copy-start(bf16[1024,128]{0,1:T(8,128)(2,1)} %reduce-scatter.2.cloned.1.call-done) | copy-start | bytes 786436
Sparse Core Ops, SparseCore 0:
  9.8 25.2 all-gather.2
  82.5 19.6 reduce-scatter.1
  105.4 53.8 all-gather.4

commit v3 on v1

--- a/solution.py
+++ b/solution.py
@@ -134,13 +134,18 @@
     lo_count = lax.axis_size(CTX_LO)
     features, local_len = full_cotangent.shape
     rows = features // (hi_count * lo_count)
-    group_gated = lax.all_gather(gated_out, CTX_LO, axis=1, tiled=True)
-    group_gated = group_gated.reshape(gated_out.shape[0], lo_count, local_len)
     by_target = full_cotangent.reshape(hi_count, lo_count, rows, local_len).transpose(1, 0, 2, 3)
-    group_rows = lax.all_to_all(by_target, CTX_LO, split_axis=0, concat_axis=0, tiled=True)
+    by_target = by_target.reshape(lo_count, hi_count * rows, local_len)
+    outgoing = jnp.concatenate(
+        [by_target, jnp.broadcast_to(gated_out, (lo_count,) + gated_out.shape)], axis=1
+    )
+    incoming = lax.all_to_all(outgoing, CTX_LO, split_axis=0, concat_axis=0, tiled=True)
+    group_rows = incoming[:, : hi_count * rows]
+    group_gated = incoming[:, hi_count * rows :]
     weight_partial = lax.dot_general(
-        group_rows, group_gated, (((0, 3), (1, 2)), ((), ())), preferred_element_type=jnp.float32
+        group_rows, group_gated, (((0, 2), (0, 2)), ((), ())), preferred_element_type=jnp.float32
     ).astype(jnp.bfloat16)
+    weight_partial = weight_partial.reshape(hi_count, rows, gated_out.shape[0])
     received = lax.all_to_all(weight_partial, CTX_HI, split_axis=0, concat_axis=0, tiled=True)
     return received.astype(jnp.float32).sum(0)
 

time: 173 us -> 175 us (1.012)
  blocking collectives: 17.9 us -> 0 us
  starting transfers between devices: 41 us -> 53.4 us
  waiting for transfers between devices: 45.3 us -> 49.6 us
  local copies, waits for them, and re-layouts: 14.3 us -> 16.4 us
    all_to_all x1 -> x2, waiting for transfers between devices: 6.12 us -> 24.2 us  [the longest x1 16.8 us: weight_gradient(): lax.all_to_all(outgoing, CTX_LO, split_axis=0, concat_axis=0, tiled=True)]
    all_to_all x1 -> x0, blocking collectives: 17.9 us -> none  [swap_layouts(): lax.all_to_all(outgoing, CTX, split_axis=0, concat_axis=0, tiled=True)]
    all_gather x1 -> x0, waiting for transfers between devices: 10.4 us -> none  [weight_gradient(): group_gated = lax.all_gather(gated_out, CTX_LO, axis=1, tiled=True)]
    all_to_all x1 -> x2, starting transfers between devices: 7.97 us -> 17.4 us  [the longest x1 8.74 us: weight_gradient(): lax.all_to_all(outgoing, CTX_LO, split_axis=0, concat_axis=0, tiled=True)]
    ppermute x2, starting transfers between devices: 5.43 us -> 8.57 us  [from_behind(): lax.ppermute(value, axis, [(source, source + steps) for source in range(f...]
    ppermute x2, waiting for transfers between devices: 13.6 us -> 10.7 us  [from_behind(): lax.ppermute(value, axis, [(source, source + steps) for source in range(f...]
    reshape x0 -> x1, local copies, waits for them, and re-layouts: none -> 2.29 us  [weight_gradient(): full_cotangent.reshape(hi_count, lo_count, rows, local_len)]
    unnamed x50 -> x44, local copies, waits for them, and re-layouts: 7.26 us -> 7.25 us
  transfers between devices with their start and end apart: 9 -> 9, of which waited for: 6 -> 6; matrix products, arithmetic and copies ran while one was open for 24% -> 20% of each run, Pallas kernels for 0% -> 0%
where the time goes in v3:
time: 175 us; the launch traced here: 173 us
  starting transfers between devices  53.4 us (31%)
  waiting for transfers between devices  49.6 us (28%)
  matrix products  33.6 us (19%)
  local copies, waits for them, and re-layouts  16.4 us (9%)
  between operations  14.7 us (8%)
  other arithmetic  5.64 us (3%)
    all_to_all x1, waiting for transfers between devices, weight_gradient(): lax.all_to_all(outgoing, CTX_LO, split_axis=0, concat_axis=0, tiled=True)  16.8 us
    all_to_all x1, starting transfers between devices, to_channels(): return lax.all_to_all(block, CTX, split_axis=0, concat_axis=1, tiled=True)  15.5 us
    ppermute x2, waiting for transfers between devices, from_behind(): lax.ppermute(value, axis, [(source, source + steps) for source in range(f...  10.7 us
    all_to_all x1, starting transfers between devices, weight_gradient(): lax.all_to_all(outgoing, CTX_LO, split_axis=0, concat_axis=0, tiled=True)  8.74 us
    all_to_all x1, starting transfers between devices, swap_layouts(): lax.all_to_all(outgoing, CTX, split_axis=0, concat_axis=0, tiled=True)  8.7 us
    ppermute x2, starting transfers between devices, from_behind(): lax.ppermute(value, axis, [(source, source + steps) for source in range(f...  8.57 us
    all_to_all x1, starting transfers between devices, to_positions(): return lax.all_to_all(block, CTX, split_axis=1, concat_axis=0, tiled=True)  8.35 us
    all_to_all x1, waiting for transfers between devices, swap_layouts(): lax.all_to_all(outgoing, CTX, split_axis=0, concat_axis=0, tiled=True)  7.44 us
  transfers between devices with their start and end apart: 9, of which 6 were waited for; matrix products, arithmetic and copies ran while one was open for 20% of the time, Pallas kernels for 0%

profile of v3, /device:TPU:22, one launch (start us, length us, event | category | flops | bytes accessed | tf_op | source)
XLA Modules:
  0.0 173.5 jit_solution(11152096996115684689)
XLA Ops:
  7.9 1.0 copy.110
  8.9 1.0 copy.111
  9.9 1.0 copy.112
  11.0 3.5 %collective-permute-start = (bf16[3,512,6]{1,2,0:T(8,128)(2,1)S(1)}, bf16[3,512,6]{1,2,0:T(8,128)(2,1)S(1)}, u32[]{:S(2)}, u32[]{:S(2)}) collective-permute-start(bf16[3,512,6]{1,2,0:T(8,128)(2,1)S(1)} %pad_maximum_fusion.13), channel_id=1, source_target_pairs={{0,4},{4,8},{8,12},{12,16},{16,20},{20,24},{24,28},{28,32},{32,36}... | collective-permute-start | bytes 55304 | tf_op jit(solution)/shard_map/ppermute | solution.py:22
  14.5 1.2 fusion.168
  18.3 15.5 %all-to-all-start = ((bf16[64,8,128]{2,1,0:T(8,128)(2,1)}), bf16[64,8,128]{2,1,0:T(8,128)(2,1)S(1)}, u32[]{:S(2)}, u32[]{:S(2)}) async-start(bf16[64,8,128]{2,1,0:T(8,128)(2,1)} %bitcast.5), calls=%async_computation | async-start | bytes 262144 | tf_op jit(solution)/shard_map/all_to_all | solution.py:108
  34.9 7.4 %all-to-all-done = bf16[64,8,128]{2,1,0:T(8,128)(2,1)S(1)} async-done(((bf16[64,8,128]{2,1,0:T(8,128)(2,1)}), bf16[64,8,128]{2,1,0:T(8,128)(2,1)S(1)}, u32[]{:S(2)}, u32[]{:S(2)}) %all-to-all-start) | async-done | bytes 131104 | tf_op jit(solution)/shard_map/all_to_all | solution.py:108
  43.3 1.0 convolution_bitcast_fusion.1
  44.4 1.2 fusion.43
  45.5 1.2 fusion.44
  46.7 1.2 convolution_add_fusion.1
  47.9 1.2 convolution_subtract_fusion.1
  52.5 4.0 %fusion.48 = (bf16[512,128]{0,1:T(8,128)(2,1)S(1)}, f32[512,128]{0,1:T(8,128)}) fusion(bf16[3,512,128]{1,2,0:T(8,128)(2,1)S(1)} %fusion.26, bf16[4096,512]{1,0:T(8,128)(2,1)} %param.12, bf16[4096,128]{1,0:T(8,128)(2,1)} %all-gather.2.cloned.1.call-done), kind=kOutput, calls=%fused_computation.100 | convolution fusion | flops 537067520 | bytes 5767168 | tf_op jit(solution)/shard_map/dot_general | solution.py:174
  57.6 8.7 %all-to-all-start.1 = ((bf16[64,2,8,128]{3,2,1,0:T(8,128)(2,1)}), bf16[64,2,8,128]{3,2,1,0:T(8,128)(2,1)S(1)}, u32[]{:S(2)}, u32[]{:S(2)}) async-start(bf16[64,2,8,128]{3,2,1,0:T(8,128)(2,1)} %copy.133), calls=%async_computation.1 | async-start | bytes 524288 | tf_op jit(solution)/shard_map/all_to_all | solution.py:126
  66.3 2.3 %copy.159 = bf16[8,8,64,128]{3,2,0,1:T(8,128)(2,1)} copy(bf16[8,8,64,128]{3,2,1,0:T(8,128)(2,1)} %bitcast.167) | data formatting | bytes 2097152 | tf_op jit(solution)/shard_map/reshape | solution.py:137
  68.6 7.4 %all-to-all-done.1 = bf16[64,2,8,128]{3,2,1,0:T(8,128)(2,1)S(1)} async-done(((bf16[64,2,8,128]{3,2,1,0:T(8,128)(2,1)}), bf16[64,2,8,128]{3,2,1,0:T(8,128)(2,1)S(1)}, u32[]{:S(2)}, u32[]{:S(2)}) %all-to-all-start.1) | async-done | bytes 262176 | tf_op jit(solution)/shard_map/all_to_all | solution.py:126
  77.5 1.4 fusion.56
  78.9 1.4 fusion.57
  80.3 1.8 %copy.135 = f32[512,128]{0,1:T(8,128)} copy(f32[512,128]{1,0:T(8,128)} %get-tuple-element.38) | data formatting | bytes 524288 | tf_op jit(solution)/shard_map/convert_element_type | solution.py:179
  82.1 1.7 convolution_subtract_fusion.2
  83.8 1.9 %multiply_add_fusion.2 = (f32[8,128,128]{2,1,0:T(8,128)S(1)}, f32[8,128,128]{2,1,0:T(8,128)S(1)}, f32[8,128,128]{2,1,0:T(8,128)S(1)}, f32[8,128,128]{2,1,0:T(8,128)S(1)}) fusion(f32[8,128,128]{2,1,0:T(8,128)S(1)} %convolution_subtract_fusion.2, f32[16,128,128]{2,1,0:T(8,128)S(1)} %convolution_add_fusion.1, ...), kind=kOutput, calls=%fused_computation.72 | convolution fusion | flops 102989824 | bytes 6422528 | tf_op jit(solution)/shard_map/dot_general | solution.py:57
  91.4 8.4 %all-to-all-start.2 = ((bf16[8,64,128]{2,0,1:T(8,128)(2,1)}), bf16[8,64,128]{2,0,1:T(8,128)(2,1)S(1)}, u32[]{:S(2)}, u32[]{:S(2)}) async-start(bf16[8,64,128]{2,0,1:T(8,128)(2,1)} %copy.156), calls=%async_computation.3 | async-start | bytes 262144 | tf_op jit(solution)/shard_map/all_to_all | solution.py:112
  100.1 1.5 pad_maximum_fusion
  101.6 6.5 %all-to-all-done.2 = bf16[8,64,128]{2,0,1:T(8,128)(2,1)S(1)} async-done(((bf16[8,64,128]{2,0,1:T(8,128)(2,1)}), bf16[8,64,128]{2,0,1:T(8,128)(2,1)S(1)}, u32[]{:S(2)}, u32[]{:S(2)}) %all-to-all-start.2) | async-done | bytes 131104 | tf_op jit(solution)/shard_map/all_to_all | solution.py:112
  108.2 8.7 %all-to-all-start.3 = ((bf16[8,1024,128]{2,1,0:T(8,128)(2,1)}), bf16[8,1024,128]{2,1,0:T(8,128)(2,1)}, u32[]{:S(2)}, u32[]{:S(2)}) async-start(bf16[8,1024,128]{2,1,0:T(8,128)(2,1)} %pad_maximum_fusion), calls=%async_computation.4 | async-start | bytes 4194304 | tf_op jit(solution)/shard_map/all_to_all | solution.py:142
  116.9 4.7 %fusion = bf16[4096,128]{0,1:T(8,128)(2,1)} fusion(bf16[512,128]{0,1:T(8,128)(2,1)S(1)} %get-tuple-element.36, bf16[4096,512]{1,0:T(8,128)(2,1)} %param.12), kind=kOutput, calls=%fused_computation.1 | convolution fusion | flops 537395200 | bytes 5373952 | tf_op jit(solution)/shard_map/dot_general | solution.py:181
  121.8 16.8 %all-to-all-done.3 = bf16[8,1024,128]{2,1,0:T(8,128)(2,1)} async-done(((bf16[8,1024,128]{2,1,0:T(8,128)(2,1)}), bf16[8,1024,128]{2,1,0:T(8,128)(2,1)}, u32[]{:S(2)}, u32[]{:S(2)}) %all-to-all-start.3) | async-done | bytes 2097184 | tf_op jit(solution)/shard_map/all_to_all | solution.py:142
  138.6 3.1 %fusion.1 = bf16[512,512]{1,0:T(8,128)(2,1)} fusion(bf16[8,1024,128]{2,1,0:T(8,128)(2,1)} %all-to-all-done.3), kind=kOutput, calls=%fused_computation.10 | convolution fusion | flops 537133056 | bytes 2621440 | tf_op jit(solution)/shard_map/dot_general | solution.py:145
  141.7 3.5 %all-to-all-start.4 = ((bf16[8,64,512]{2,1,0:T(8,128)(2,1)}), bf16[8,64,512]{2,1,0:T(8,128)(2,1)S(1)}, u32[]{:S(2)}, u32[]{:S(2)}) async-start(bf16[8,64,512]{2,1,0:T(8,128)(2,1)} %bitcast.53), calls=%async_computation.5 | async-start | bytes 1048576 | tf_op jit(solution)/shard_map/all_to_all | solution.py:149
  145.3 5.1 %collective-permute-start.1 = (bf16[3,512,6]{1,2,0:T(8,128)(2,1)S(1)}, bf16[3,512,6]{1,2,0:T(8,128)(2,1)S(1)}, u32[]{:S(2)}, u32[]{:S(2)}) collective-permute-start(bf16[3,512,6]{1,2,0:T(8,128)(2,1)S(1)} %pad_maximum_fusion.11), channel_id=1, source_target_pairs={{4,0},{8,4},{12,8},{16,12},{20,16},{24,20},{28,24},{32,28},{36,32}... | collective-permute-start | bytes 55304 | tf_op jit(solution)/shard_map/ppermute | solution.py:22
  151.2 9.8 %collective-permute-done.1 = bf16[3,512,6]{1,2,0:T(8,128)(2,1)S(1)} collective-permute-done((bf16[3,512,6]{1,2,0:T(8,128)(2,1)S(1)}, bf16[3,512,6]{1,2,0:T(8,128)(2,1)S(1)}, u32[]{:S(2)}, u32[]{:S(2)}) %collective-permute-start.1) | collective-permute-done | bytes 18464 | tf_op jit(solution)/shard_map/ppermute | solution.py:22
  164.1 1.8 %copy.161 = bf16[1024,128]{1,0:T(8,128)(2,1)} copy(bf16[1024,128]{0,1:T(8,128)(2,1)} %reduce-scatter.2.cloned.1.call-done) | data formatting | bytes 524288
  (95 shorter events, 21.9 us)
Async XLA Ops:
  7.2 45.4 %all-gather.2.cloned.1.call-start = ((), (), s32[]{:S(2)}) async-start(), calls=%async_computation.6 | async-start | bytes 1310720 | tf_op jit(solution)/shard_map/all_gather | solution.py:173
  11.0 5.7 %collective-permute-start = (bf16[3,512,6]{1,2,0:T(8,128)(2,1)S(1)}, bf16[3,512,6]{1,2,0:T(8,128)(2,1)S(1)}, u32[]{:S(2)}, u32[]{:S(2)}) collective-permute-start(bf16[3,512,6]{1,2,0:T(8,128)(2,1)S(1)} %pad_maximum_fusion.13), channel_id=1, source_target_pairs={{0,4},{4,8},{8,12},{12,16},{16,20},{20,24},{24,28},{28,32},{32,36}... | collective-permute-start | bytes 55304 | tf_op jit(solution)/shard_map/ppermute | solution.py:22
  15.7 18.5 %copy-start.6 = (f32[3,512]{1,0:T(4,128)}, f32[3,512]{1,0:T(4,128)S(1)}, u32[]{:S(2)}) copy-start(f32[3,512]{1,0:T(4,128)S(1)} %get-tuple-element.52) | copy-start | bytes 18436
  15.7 18.5 %copy-start.8 = (f32[3,512]{1,0:T(4,128)}, f32[3,512]{1,0:T(4,128)S(1)}, u32[]{:S(2)}) copy-start(f32[3,512]{1,0:T(4,128)S(1)} %get-tuple-element.53) | copy-start | bytes 18436
  15.7 18.5 %copy-start.10 = (f32[3,512]{1,0:T(4,128)}, f32[3,512]{1,0:T(4,128)S(1)}, u32[]{:S(2)}) copy-start(f32[3,512]{1,0:T(4,128)S(1)} %get-tuple-element.48) | copy-start | bytes 18436
  15.8 18.5 %copy-start.12 = (f32[3,512]{1,0:T(4,128)}, f32[3,512]{1,0:T(4,128)S(1)}, u32[]{:S(2)}) copy-start(f32[3,512]{1,0:T(4,128)S(1)} %get-tuple-element.49) | copy-start | bytes 18436
  15.8 18.5 %copy-start.14 = (f32[3,512,1]{1,0,2:T(4,128)}, f32[3,512,1]{1,0,2:T(4,128)S(1)}, u32[]{:S(2)}) copy-start(f32[3,512,1]{1,0,2:T(4,128)S(1)} %copy.240) | copy-start | bytes 18436
  15.8 18.6 %copy-start.5 = (f32[1,8,8192]{2,1,0:T(8,128)S(1)}, f32[1,8,8192]{2,1,0:T(8,128)}, u32[]{:S(2)}) copy-start(f32[1,8,8192]{2,1,0:T(8,128)} %param.11) | copy-start | bytes 786436
  17.5 35.1 %copy-start.1 = (bf16[3,512,128]{1,2,0:T(8,128)(2,1)}, bf16[3,512,128]{1,2,0:T(8,128)(2,1)S(1)}, u32[]{:S(2)}) copy-start(bf16[3,512,128]{1,2,0:T(8,128)(2,1)S(1)} %fusion.26) | copy-start | bytes 1179652
  18.3 24.0 %all-to-all-start = ((bf16[64,8,128]{2,1,0:T(8,128)(2,1)}), bf16[64,8,128]{2,1,0:T(8,128)(2,1)S(1)}, u32[]{:S(2)}, u32[]{:S(2)}) async-start(bf16[64,8,128]{2,1,0:T(8,128)(2,1)} %bitcast.5), calls=%async_computation | async-start | bytes 262144 | tf_op jit(solution)/shard_map/all_to_all | solution.py:108
  57.6 18.4 %all-to-all-start.1 = ((bf16[64,2,8,128]{3,2,1,0:T(8,128)(2,1)}), bf16[64,2,8,128]{3,2,1,0:T(8,128)(2,1)S(1)}, u32[]{:S(2)}, u32[]{:S(2)}) async-start(bf16[64,2,8,128]{3,2,1,0:T(8,128)(2,1)} %copy.133), calls=%async_computation.1 | async-start | bytes 524288 | tf_op jit(solution)/shard_map/all_to_all | solution.py:126
  89.1 10.7 %copy-start.2 = (bf16[3,512,128]{1,2,0:T(8,128)(2,1)S(1)}, bf16[3,512,128]{1,2,0:T(8,128)(2,1)}, u32[]{:S(2)}) copy-start(bf16[3,512,128]{1,2,0:T(8,128)(2,1)} %copy-done.1) | copy-start | bytes 1179652
  89.1 10.7 %copy-start.3 = (f32[512,128]{0,1:T(8,128)S(1)}, f32[512,128]{0,1:T(8,128)}, u32[]{:S(2)}) copy-start(f32[512,128]{0,1:T(8,128)} %copy.135) | copy-start | bytes 786436
  89.1 10.7 %copy-start.4 = (f32[512,128]{0,1:T(8,128)S(1)}, f32[512,128]{0,1:T(8,128)}, u32[]{:S(2)}) copy-start(f32[512,128]{0,1:T(8,128)} %get-tuple-element.47) | copy-start | bytes 786436
  89.1 11.0 %copy-start = (bf16[8,8,64,128]{3,2,0,1:T(8,128)(2,1)S(1)}, bf16[8,8,64,128]{3,2,0,1:T(8,128)(2,1)}, u32[]{:S(2)}) copy-start(bf16[8,8,64,128]{3,2,0,1:T(8,128)(2,1)} %copy.159) | copy-start | bytes 3145732
  91.4 16.8 %all-to-all-start.2 = ((bf16[8,64,128]{2,0,1:T(8,128)(2,1)}), bf16[8,64,128]{2,0,1:T(8,128)(2,1)S(1)}, u32[]{:S(2)}, u32[]{:S(2)}) async-start(bf16[8,64,128]{2,0,1:T(8,128)(2,1)} %copy.156), calls=%async_computation.3 | async-start | bytes 262144 | tf_op jit(solution)/shard_map/all_to_all | solution.py:112
  108.2 30.5 %all-to-all-start.3 = ((bf16[8,1024,128]{2,1,0:T(8,128)(2,1)}), bf16[8,1024,128]{2,1,0:T(8,128)(2,1)}, u32[]{:S(2)}, u32[]{:S(2)}) async-start(bf16[8,1024,128]{2,1,0:T(8,128)(2,1)} %pad_maximum_fusion), calls=%async_computation.4 | async-start | bytes 4194304 | tf_op jit(solution)/shard_map/all_to_all | solution.py:142
  116.9 47.2 %reduce-scatter.2.cloned.1.call-start = ((), (), s32[]{:S(2)}) async-start(), calls=%async_computation.7 | async-start | bytes 1310720 | tf_op jit(solution)/shard_map/reduce_scatter | solution.py:180
  121.8 39.3 %copy-start.7 = (f32[3,512]{1,0:T(4,128)S(1)}, f32[3,512]{1,0:T(4,128)}, u32[]{:S(2)}) copy-start(f32[3,512]{1,0:T(4,128)} %copy-done.6) | copy-start | bytes 18436
  121.8 39.3 %copy-start.9 = (f32[3,512]{1,0:T(4,128)S(1)}, f32[3,512]{1,0:T(4,128)}, u32[]{:S(2)}) copy-start(f32[3,512]{1,0:T(4,128)} %copy-done.8) | copy-start | bytes 18436
  121.8 39.3 %copy-start.11 = (f32[3,512]{1,0:T(4,128)S(1)}, f32[3,512]{1,0:T(4,128)}, u32[]{:S(2)}) copy-start(f32[3,512]{1,0:T(4,128)} %copy-done.10) | copy-start | bytes 18436
  121.8 39.3 %copy-start.13 = (f32[3,512]{1,0:T(4,128)S(1)}, f32[3,512]{1,0:T(4,128)}, u32[]{:S(2)}) copy-start(f32[3,512]{1,0:T(4,128)} %copy-done.12) | copy-start | bytes 18436
  121.8 39.3 %copy-start.15 = (f32[3,512,1]{1,0,2:T(4,128)S(1)}, f32[3,512,1]{1,0,2:T(4,128)}, u32[]{:S(2)}) copy-start(f32[3,512,1]{1,0,2:T(4,128)} %copy-done.14) | copy-start | bytes 18436
  141.7 24.2 %all-to-all-start.4 = ((bf16[8,64,512]{2,1,0:T(8,128)(2,1)}), bf16[8,64,512]{2,1,0:T(8,128)(2,1)S(1)}, u32[]{:S(2)}, u32[]{:S(2)}) async-start(bf16[8,64,512]{2,1,0:T(8,128)(2,1)} %bitcast.53), calls=%async_computation.5 | async-start | bytes 1048576 | tf_op jit(solution)/shard_map/all_to_all | solution.py:149
  145.3 15.7 %collective-permute-start.1 = (bf16[3,512,6]{1,2,0:T(8,128)(2,1)S(1)}, bf16[3,512,6]{1,2,0:T(8,128)(2,1)S(1)}, u32[]{:S(2)}, u32[]{:S(2)}) collective-permute-start(bf16[3,512,6]{1,2,0:T(8,128)(2,1)S(1)} %pad_maximum_fusion.11), channel_id=1, source_target_pairs={{4,0},{8,4},{12,8},{16,12},{20,16},{24,20},{28,24},{32,28},{36,32}... | collective-permute-start | bytes 55304 | tf_op jit(solution)/shard_map/ppermute | solution.py:22
Sparse Core Ops, SparseCore 0:
  9.8 25.2 all-gather.1
  121.7 25.1 reduce-scatter.1

commit v4 on v1

--- a/solution.py
+++ b/solution.py
@@ -60,20 +60,20 @@
     return (frequency_real_component, spec_im)
 
 
-def inverse(frequency_real_component, spec_im, tables):
+def inverse(frequency_real_component, spec_im, tables, precision=DFT_PRECISION):
     outer_re, outer_im, inner_re, inner_im, twist_re, twist_im = tables
     channels, row_count, block_width = frequency_real_component.shape
     half_rows = row_count // 2
-    back_re = jnp.matmul(frequency_real_component, inner_re, precision=DFT_PRECISION) + jnp.matmul(
-        spec_im, inner_im, precision=DFT_PRECISION
-    )
-    back_im = jnp.matmul(spec_im, inner_re, precision=DFT_PRECISION) - jnp.matmul(
-        frequency_real_component, inner_im, precision=DFT_PRECISION
+    back_re = jnp.matmul(frequency_real_component, inner_re, precision=precision) + jnp.matmul(
+        spec_im, inner_im, precision=precision
+    )
+    back_im = jnp.matmul(spec_im, inner_re, precision=precision) - jnp.matmul(
+        frequency_real_component, inner_im, precision=precision
     )
     turned_re = back_re * twist_re + back_im * twist_im
     turned_im = back_im * twist_re - back_re * twist_im
-    signal = jnp.einsum("nk,ckm->cnm", outer_re[:half_rows], turned_re, precision=DFT_PRECISION)
-    signal = signal + jnp.einsum("nk,ckm->cnm", outer_im[:half_rows], turned_im, precision=DFT_PRECISION)
+    signal = jnp.einsum("nk,ckm->cnm", outer_re[:half_rows], turned_re, precision=precision)
+    signal = signal + jnp.einsum("nk,ckm->cnm", outer_im[:half_rows], turned_im, precision=precision)
     return (signal / (row_count * block_width)).reshape(channels, half_rows * block_width)
 
 
@@ -164,6 +164,7 @@
         product_re * kernel_re - product_im * kernel_im,
         product_re * kernel_im + product_im * kernel_re,
         tables,
+        lax.Precision.DEFAULT,
     ).astype(jnp.bfloat16)
     full_cotangent = lax.all_gather(cotangent, "tp", axis=0, tiled=True)
     grad_gated = lax.dot_general(

time: 173 us -> 172 us (level)
  transfers between devices with their start and end apart: 9 -> 9, of which waited for: 6 -> 6; matrix products, arithmetic and copies ran while one was open for 24% -> 20% of each run, Pallas kernels for 0% -> 0%
where the time goes in v4:
time: 172 us; the launch traced here: 171 us
  waiting for transfers between devices  44.7 us (26%)
  starting transfers between devices  41 us (24%)
  matrix products  33.4 us (19%)
  blocking collectives  17.7 us (10%)
  between operations  14.4 us (8%)
  local copies, waits for them, and re-layouts  14.3 us (8%)
  other arithmetic  5.89 us (3%)
    all_to_all x1, blocking collectives, swap_layouts(): lax.all_to_all(outgoing, CTX, split_axis=0, concat_axis=0, tiled=True)  17.7 us
    all_to_all x1, starting transfers between devices, to_channels(): return lax.all_to_all(block, CTX, split_axis=0, concat_axis=1, tiled=True)  15.5 us
    ppermute x2, waiting for transfers between devices, from_behind(): lax.ppermute(value, axis, [(source, source + steps) for source in range(f...  13.7 us
    all_gather x1, waiting for transfers between devices, weight_gradient(): group_gated = lax.all_gather(gated_out, CTX_LO, axis=1, tiled=True)  10.7 us
    all_to_all x1, starting transfers between devices, to_positions(): return lax.all_to_all(block, CTX, split_axis=1, concat_axis=0, tiled=True)  8.34 us
    all_to_all x1, starting transfers between devices, weight_gradient(): lax.all_to_all(by_target, CTX_LO, split_axis=0, concat_axis=0, tiled=True)  7.97 us
    all_to_all x1, waiting for transfers between devices, to_positions(): return lax.all_to_all(block, CTX, split_axis=1, concat_axis=0, tiled=True)  7.3 us
    unnamed x50, local copies, waits for them, and re-layouts  7.26 us
  transfers between devices with their start and end apart: 9, of which 6 were waited for; matrix products, arithmetic and copies ran while one was open for 20% of the time, Pallas kernels for 0%

profile of v4, /device:TPU:22, one launch (start us, length us, event | category | flops | bytes accessed | tf_op | source)
XLA Modules:
  0.0 171.4 jit_solution(5498746149435712128)
XLA Ops:
  7.2 1.0 copy.165
  8.2 1.0 copy.164
  9.2 1.0 copy.163
  10.3 3.5 %collective-permute-start = (bf16[3,512,6]{1,2,0:T(8,128)(2,1)S(1)}, bf16[3,512,6]{1,2,0:T(8,128)(2,1)S(1)}, u32[]{:S(2)}, u32[]{:S(2)}) collective-permute-start(bf16[3,512,6]{1,2,0:T(8,128)(2,1)S(1)} %pad_maximum_fusion.12), channel_id=1, source_target_pairs={{0,4},{4,8},{8,12},{12,16},{16,20},{20,24},{24,28},{28,32},{32,36}... | collective-permute-start | bytes 55304 | tf_op jit(solution)/shard_map/ppermute | solution.py:22
  13.8 1.2 fusion.167
  17.6 15.5 %all-to-all-start = ((bf16[64,8,128]{2,1,0:T(8,128)(2,1)}), bf16[64,8,128]{2,1,0:T(8,128)(2,1)S(1)}, u32[]{:S(2)}, u32[]{:S(2)}) async-start(bf16[64,8,128]{2,1,0:T(8,128)(2,1)} %bitcast.5), calls=%async_computation | async-start | bytes 262144 | tf_op jit(solution)/shard_map/all_to_all | solution.py:108
  34.5 7.1 %all-to-all-done = bf16[64,8,128]{2,1,0:T(8,128)(2,1)S(1)} async-done(((bf16[64,8,128]{2,1,0:T(8,128)(2,1)}), bf16[64,8,128]{2,1,0:T(8,128)(2,1)S(1)}, u32[]{:S(2)}, u32[]{:S(2)}) %all-to-all-start) | async-done | bytes 131104 | tf_op jit(solution)/shard_map/all_to_all | solution.py:108
  41.6 1.0 convolution_bitcast_fusion
  43.7 1.2 fusion.42
  44.9 1.2 fusion.43
  46.0 1.2 convolution_add_fusion.1
  47.2 1.2 convolution_subtract_fusion.1
  50.9 4.0 %fusion.47 = (bf16[512,128]{0,1:T(8,128)(2,1)S(1)}, f32[512,128]{0,1:T(8,128)}) fusion(bf16[3,512,128]{1,2,0:T(8,128)(2,1)S(1)} %fusion.25, bf16[4096,512]{1,0:T(8,128)(2,1)} %param.12, bf16[4096,128]{1,0:T(8,128)(2,1)} %all-gather.3.cloned.1.call-done), kind=kOutput, calls=%fused_computation.98 | convolution fusion | flops 537067520 | bytes 5767168 | tf_op jit(solution)/shard_map/dot_general | solution.py:170
  55.3 17.7 %all_to_all.35 = bf16[64,2,8,128]{3,2,1,0:T(8,128)(2,1)S(1)} all-to-all(bf16[64,2,8,128]{3,2,1,0:T(8,128)(2,1)S(1)} %copy.186), channel_id=1, replica_groups=mesh['ctx_hi'=8,'ctx_lo'=8,'tp'=4] {'ctx_hi','ctx_lo'}, dimensions={0} | all-to-all | bytes 524288 | tf_op jit(solution)/shard_map/all_to_all | solution.py:126
  74.5 1.4 fusion.56
  75.9 1.4 fusion.55
  77.4 1.8 %copy.188 = f32[512,128]{0,1:T(8,128)} copy(f32[512,128]{1,0:T(8,128)} %get-tuple-element.44) | data formatting | bytes 524288 | tf_op jit(solution)/shard_map/convert_element_type | solution.py:175
  79.1 2.5 %convolution_subtract_fusion.2 = f32[8,128,128]{2,1,0:T(8,128)} fusion(f32[8,128,128]{2,1,0:T(8,128)} %fusion.56, f32[8,128,128]{2,1,0:T(8,128)S(1)} %convolution_bitcast_fusion.3, f32[8,128,128]{2,1,0:T(8,128)S(1)} %convolution_bitcast_fusion.4, f32[128,128]{1,0:T(8,128)S(1)} %copy.181, f32[128,128]{1,0:T(8,128)S(1)} %copy.178), kind=kOutput, calls=%fused_computation.17 | convolution fusion | flops 101433344 | bytes 2228224 | tf_op jit(solution)/shard_map/dot_general | solution.py:54
  81.6 1.8 %fusion.53 = (bf16[1,512,128]{1,2,0:T(8,128)(2,1)S(1)}, bf16[512,128]{0,1:T(8,128)(2,1)}) fusion(f32[512,128]{0,1:T(8,128)} %get-tuple-element.53, f32[512,128]{0,1:T(8,128)} %copy.188, bf16[3,512,128]{1,2,0:T(8,128)(2,1)} %copy-done), kind=kLoop, calls=%fused_computation.110 | loop fusion | flops 327680 | bytes 917504 | tf_op jit(solution)/shard_map/stack | solution.py:202
  83.4 2.0 %multiply_add_fusion.2 = (f32[8,128,128]{2,1,0:T(8,128)S(1)}, f32[8,128,128]{2,1,0:T(8,128)S(1)}, f32[8,128,128]{2,1,0:T(8,128)S(1)}, f32[8,128,128]{2,1,0:T(8,128)S(1)}) fusion(f32[8,128,128]{2,1,0:T(8,128)} %convolution_subtract_fusion.2, f32[16,128,128]{2,1,0:T(8,128)S(1)} %convolution_add_fusion.1, f32[16,128,128]{2,1,0:T(8,128)S(1)} %convolution_subtract_fusion.1, ...), kind=kOutput, calls=%fused_computation.70 | convolution fusion | flops 102989824 | bytes 6422528 | tf_op jit(solution)/shard_map/dot_general | solution.py:57
  91.2 8.3 %all-to-all-start.2 = ((bf16[8,64,128]{2,0,1:T(8,128)(2,1)}), bf16[8,64,128]{2,0,1:T(8,128)(2,1)S(1)}, u32[]{:S(2)}, u32[]{:S(2)}) async-start(bf16[8,64,128]{2,0,1:T(8,128)(2,1)} %copy.209), calls=%async_computation.3 | async-start | bytes 262144 | tf_op jit(solution)/shard_map/all_to_all | solution.py:112
  99.6 1.1 copy.212
  100.6 7.3 %all-to-all-done.2 = bf16[8,64,128]{2,0,1:T(8,128)(2,1)S(1)} async-done(((bf16[8,64,128]{2,0,1:T(8,128)(2,1)}), bf16[8,64,128]{2,0,1:T(8,128)(2,1)S(1)}, u32[]{:S(2)}, u32[]{:S(2)}) %all-to-all-start.2) | async-done | bytes 131104 | tf_op jit(solution)/shard_map/all_to_all | solution.py:112
  107.9 8.0 %all-to-all-start.3 = ((bf16[8,8,64,128]{3,2,1,0:T(8,128)(2,1)}), bf16[8,8,64,128]{3,2,1,0:T(8,128)(2,1)S(1)}, u32[]{:S(2)}, u32[]{:S(2)}) async-start(bf16[8,8,64,128]{3,2,1,0:T(8,128)(2,1)} %copy.212), calls=%async_computation.4 | async-start | bytes 2097152 | tf_op jit(solution)/shard_map/all_to_all | solution.py:140
  115.9 4.7 %fusion = bf16[4096,128]{0,1:T(8,128)(2,1)} fusion(bf16[512,128]{0,1:T(8,128)(2,1)S(1)} %copy-done.2, bf16[4096,512]{1,0:T(8,128)(2,1)} %param.12), kind=kOutput, calls=%fused_computation.1 | convolution fusion | flops 537395200 | bytes 5373952 | tf_op jit(solution)/shard_map/dot_general | solution.py:177
  120.8 5.8 %all-to-all-done.3 = bf16[8,8,64,128]{3,2,1,0:T(8,128)(2,1)S(1)} async-done(((bf16[8,8,64,128]{3,2,1,0:T(8,128)(2,1)}), bf16[8,8,64,128]{3,2,1,0:T(8,128)(2,1)S(1)}, u32[]{:S(2)}, u32[]{:S(2)}) %all-to-all-start.3) | async-done | bytes 1048608 | tf_op jit(solution)/shard_map/all_to_all | solution.py:140
  126.6 10.7 %all-gather.5.cloned.1.call-done = bf16[512,1024]{0,1:T(8,128)(2,1)} async-done(((bf16[512,128]{0,1:T(8,128)(2,1)}), bf16[512,1024]{0,1:T(8,128)(2,1)}) %all-gather.5.cloned.1.call-update) | async-done | bytes 1048592 | tf_op jit(solution)/shard_map/all_gather | solution.py:137
  137.3 2.8 %fusion.2 = bf16[8,64,512]{2,1,0:T(8,128)(2,1)} fusion(bf16[512,8,128,1]{0,2,3,1:T(8,128)(2,1)} %bitcast.183, bf16[8,8,64,128]{3,2,1,0:T(8,128)(2,1)S(1)} %all-to-all-done.3), kind=kOutput, calls=%fused_computation.10 | convolution fusion | flops 537133056 | bytes 2621440 | tf_op jit(solution)/shard_map/dot_general | solution.py:141
  140.1 3.5 %all-to-all-start.4 = ((bf16[8,64,512]{2,1,0:T(8,128)(2,1)}), bf16[8,64,512]{2,1,0:T(8,128)(2,1)S(1)}, u32[]{:S(2)}, u32[]{:S(2)}) async-start(bf16[8,64,512]{2,1,0:T(8,128)(2,1)} %fusion.2), calls=%async_computation.5 | async-start | bytes 1048576 | tf_op jit(solution)/shard_map/all_to_all | solution.py:144
  143.7 1.9 %collective-permute-start.1 = (bf16[3,512,6]{1,2,0:T(8,128)(2,1)S(1)}, bf16[3,512,6]{1,2,0:T(8,128)(2,1)S(1)}, u32[]{:S(2)}, u32[]{:S(2)}) collective-permute-start(bf16[3,512,6]{1,2,0:T(8,128)(2,1)S(1)} %pad_maximum_fusion.10), channel_id=1, source_target_pairs={{4,0},{8,4},{12,8},{16,12},{20,16},{24,20},{28,24},{32,28},{36,32}... | collective-permute-start | bytes 55304 | tf_op jit(solution)/shard_map/ppermute | solution.py:22
  146.4 12.8 %collective-permute-done.1 = bf16[3,512,6]{1,2,0:T(8,128)(2,1)S(1)} collective-permute-done((bf16[3,512,6]{1,2,0:T(8,128)(2,1)S(1)}, bf16[3,512,6]{1,2,0:T(8,128)(2,1)S(1)}, u32[]{:S(2)}, u32[]{:S(2)}) %collective-permute-start.1) | collective-permute-done | bytes 18464 | tf_op jit(solution)/shard_map/ppermute | solution.py:22
  162.3 1.8 %copy.215 = bf16[1024,128]{1,0:T(8,128)(2,1)} copy(bf16[1024,128]{0,1:T(8,128)(2,1)} %reduce-scatter.2.cloned.1.call-done) | data formatting | bytes 524288
  (100 shorter events, 19.5 us)
Async XLA Ops:
  7.2 43.8 %all-gather.3.cloned.1.call-start = ((), (), s32[]{:S(2)}) async-start(), calls=%async_computation.6 | async-start | bytes 1310720 | tf_op jit(solution)/shard_map/all_gather | solution.py:169
  10.3 5.7 %collective-permute-start = (bf16[3,512,6]{1,2,0:T(8,128)(2,1)S(1)}, bf16[3,512,6]{1,2,0:T(8,128)(2,1)S(1)}, u32[]{:S(2)}, u32[]{:S(2)}) collective-permute-start(bf16[3,512,6]{1,2,0:T(8,128)(2,1)S(1)} %pad_maximum_fusion.12), channel_id=1, source_target_pairs={{0,4},{4,8},{8,12},{12,16},{16,20},{20,24},{24,28},{28,32},{32,36}... | collective-permute-start | bytes 55304 | tf_op jit(solution)/shard_map/ppermute | solution.py:22
  15.0 18.7 %copy-start.8 = (f32[1,8,8192]{2,1,0:T(8,128)S(1)}, f32[1,8,8192]{2,1,0:T(8,128)}, u32[]{:S(2)}) copy-start(f32[1,8,8192]{2,1,0:T(8,128)} %param.11) | copy-start | bytes 786436
  15.1 18.6 %copy-start.9 = (f32[3,512]{1,0:T(4,128)}, f32[3,512]{1,0:T(4,128)S(1)}, u32[]{:S(2)}) copy-start(f32[3,512]{1,0:T(4,128)S(1)} %get-tuple-element.56) | copy-start | bytes 18436
  15.1 18.6 %copy-start.11 = (f32[3,512]{1,0:T(4,128)}, f32[3,512]{1,0:T(4,128)S(1)}, u32[]{:S(2)}) copy-start(f32[3,512]{1,0:T(4,128)S(1)} %get-tuple-element.57) | copy-start | bytes 18436
  15.1 18.6 %copy-start.13 = (f32[3,512]{1,0:T(4,128)}, f32[3,512]{1,0:T(4,128)S(1)}, u32[]{:S(2)}) copy-start(f32[3,512]{1,0:T(4,128)S(1)} %get-tuple-element.58) | copy-start | bytes 18436
  15.1 18.6 %copy-start.15 = (f32[3,512]{1,0:T(4,128)}, f32[3,512]{1,0:T(4,128)S(1)}, u32[]{:S(2)}) copy-start(f32[3,512]{1,0:T(4,128)S(1)} %get-tuple-element.59) | copy-start | bytes 18436
  15.1 18.5 %copy-start.17 = (f32[3,512,1]{1,0,2:T(4,128)}, f32[3,512,1]{1,0,2:T(4,128)S(1)}, u32[]{:S(2)}) copy-start(f32[3,512,1]{1,0,2:T(4,128)S(1)} %copy.297) | copy-start | bytes 18436
  16.8 34.2 %copy-start = (bf16[3,512,128]{1,2,0:T(8,128)(2,1)}, bf16[3,512,128]{1,2,0:T(8,128)(2,1)S(1)}, u32[]{:S(2)}) copy-start(bf16[3,512,128]{1,2,0:T(8,128)(2,1)S(1)} %fusion.25) | copy-start | bytes 1179652
  17.6 24.0 %all-to-all-start = ((bf16[64,8,128]{2,1,0:T(8,128)(2,1)}), bf16[64,8,128]{2,1,0:T(8,128)(2,1)S(1)}, u32[]{:S(2)}, u32[]{:S(2)}) async-start(bf16[64,8,128]{2,1,0:T(8,128)(2,1)} %bitcast.5), calls=%async_computation | async-start | bytes 262144 | tf_op jit(solution)/shard_map/all_to_all | solution.py:108
  33.1 104.1 %all-gather.5.cloned.1.call-start = ((), (), s32[]{:S(2)}) async-start(), calls=%async_computation.8 | async-start | bytes 1179648 | tf_op jit(solution)/shard_map/all_gather | solution.py:137
  34.2 39.5 %copy-start.4 = (f32[128,128]{0,1:T(8,128)}, f32[128,128]{0,1:T(8,128)S(1)}, u32[]{:S(2)}) copy-start(f32[128,128]{0,1:T(8,128)S(1)} %sine_negate_fusion.1) | copy-start | bytes 196612
  34.5 39.6 %copy-start.6 = (f32[128,128]{0,1:T(8,128)}, f32[128,128]{0,1:T(8,128)S(1)}, u32[]{:S(2)}) copy-start(f32[128,128]{0,1:T(8,128)S(1)} %fusion.87) | copy-start | bytes 196612
  86.3 2.6 %copy-start.7 = (f32[128,128]{0,1:T(8,128)S(1)}, f32[128,128]{0,1:T(8,128)}, u32[]{:S(2)}) copy-start(f32[128,128]{0,1:T(8,128)} %copy-done.6) | copy-start | bytes 196612
  87.1 2.5 %copy-start.5 = (f32[128,128]{0,1:T(8,128)S(1)}, f32[128,128]{0,1:T(8,128)}, u32[]{:S(2)}) copy-start(f32[128,128]{0,1:T(8,128)} %copy-done.4) | copy-start | bytes 196612
  88.9 10.7 %copy-start.3 = (bf16[4096,128]{1,0:T(8,128)(2,1)S(1)}, bf16[4096,128]{1,0:T(8,128)(2,1)}, u32[]{:S(2)}) copy-start(bf16[4096,128]{1,0:T(8,128)(2,1)} %all-gather.3.cloned.1.call-done) | copy-start | bytes 3145732
  89.6 26.3 %copy-start.2 = (bf16[512,128]{0,1:T(8,128)(2,1)S(1)}, bf16[512,128]{0,1:T(8,128)(2,1)}, u32[]{:S(2)}) copy-start(bf16[512,128]{0,1:T(8,128)(2,1)} %get-tuple-element.42) | copy-start | bytes 393220
  91.2 16.7 %all-to-all-start.2 = ((bf16[8,64,128]{2,0,1:T(8,128)(2,1)}), bf16[8,64,128]{2,0,1:T(8,128)(2,1)S(1)}, u32[]{:S(2)}, u32[]{:S(2)}) async-start(bf16[8,64,128]{2,0,1:T(8,128)(2,1)} %copy.209), calls=%async_computation.3 | async-start | bytes 262144 | tf_op jit(solution)/shard_map/all_to_all | solution.py:112
  107.9 18.7 %all-to-all-start.3 = ((bf16[8,8,64,128]{3,2,1,0:T(8,128)(2,1)}), bf16[8,8,64,128]{3,2,1,0:T(8,128)(2,1)S(1)}, u32[]{:S(2)}, u32[]{:S(2)}) async-start(bf16[8,8,64,128]{3,2,1,0:T(8,128)(2,1)} %copy.212), calls=%async_computation.4 | async-start | bytes 2097152 | tf_op jit(solution)/shard_map/all_to_all | solution.py:140
  115.9 46.4 %reduce-scatter.2.cloned.1.call-start = ((), (), s32[]{:S(2)}) async-start(), calls=%async_computation.7 | async-start | bytes 1310720 | tf_op jit(solution)/shard_map/reduce_scatter | solution.py:176
  120.6 23.0 %copy-start.1 = (bf16[3,512,128]{1,2,0:T(8,128)(2,1)S(1)}, bf16[3,512,128]{1,2,0:T(8,128)(2,1)}, u32[]{:S(2)}) copy-start(bf16[3,512,128]{1,2,0:T(8,128)(2,1)} %copy-done) | copy-start | bytes 1179652
  137.3 22.0 %copy-start.10 = (f32[3,512]{1,0:T(4,128)S(1)}, f32[3,512]{1,0:T(4,128)}, u32[]{:S(2)}) copy-start(f32[3,512]{1,0:T(4,128)} %copy-done.9) | copy-start | bytes 18436
  137.3 22.0 %copy-start.12 = (f32[3,512]{1,0:T(4,128)S(1)}, f32[3,512]{1,0:T(4,128)}, u32[]{:S(2)}) copy-start(f32[3,512]{1,0:T(4,128)} %copy-done.11) | copy-start | bytes 18436
  137.3 22.1 %copy-start.14 = (f32[3,512]{1,0:T(4,128)S(1)}, f32[3,512]{1,0:T(4,128)}, u32[]{:S(2)}) copy-start(f32[3,512]{1,0:T(4,128)} %copy-done.13) | copy-start | bytes 18436
  137.3 22.1 %copy-start.16 = (f32[3,512]{1,0:T(4,128)S(1)}, f32[3,512]{1,0:T(4,128)}, u32[]{:S(2)}) copy-start(f32[3,512]{1,0:T(4,128)} %copy-done.15) | copy-start | bytes 18436
  137.3 22.1 %copy-start.18 = (f32[3,512,1]{1,0,2:T(4,128)S(1)}, f32[3,512,1]{1,0,2:T(4,128)}, u32[]{:S(2)}) copy-start(f32[3,512,1]{1,0,2:T(4,128)} %copy-done.17) | copy-start | bytes 18436
  140.1 24.0 %all-to-all-start.4 = ((bf16[8,64,512]{2,1,0:T(8,128)(2,1)}), bf16[8,64,512]{2,1,0:T(8,128)(2,1)S(1)}, u32[]{:S(2)}, u32[]{:S(2)}) async-start(bf16[8,64,512]{2,1,0:T(8,128)(2,1)} %fusion.2), calls=%async_computation.5 | async-start | bytes 1048576 | tf_op jit(solution)/shard_map/all_to_all | solution.py:144
  143.7 15.5 %collective-permute-start.1 = (bf16[3,512,6]{1,2,0:T(8,128)(2,1)S(1)}, bf16[3,512,6]{1,2,0:T(8,128)(2,1)S(1)}, u32[]{:S(2)}, u32[]{:S(2)}) collective-permute-start(bf16[3,512,6]{1,2,0:T(8,128)(2,1)S(1)} %pad_maximum_fusion.10), channel_id=1, source_target_pairs={{4,0},{8,4},{12,8},{16,12},{20,16},{24,20},{28,24},{32,28},{36,32}... | collective-permute-start | bytes 55304 | tf_op jit(solution)/shard_map/ppermute | solution.py:22
Sparse Core Ops, SparseCore 0:
  13.9 26.2 all-gather.2
  83.5 53.6 all-gather.4
  139.8 19.8 reduce-scatter.1

commit v5 on v0

--- a/solution.py
+++ b/solution.py
@@ -60,20 +60,20 @@
     return (frequency_real_component, spec_im)
 
 
-def inverse(frequency_real_component, spec_im, tables):
+def inverse(frequency_real_component, spec_im, tables, precision=DFT_PRECISION):
     outer_re, outer_im, inner_re, inner_im, twist_re, twist_im = tables
     channels, row_count, block_width = frequency_real_component.shape
     half_rows = row_count // 2
-    back_re = jnp.matmul(frequency_real_component, inner_re, precision=DFT_PRECISION) + jnp.matmul(
-        spec_im, inner_im, precision=DFT_PRECISION
-    )
-    back_im = jnp.matmul(spec_im, inner_re, precision=DFT_PRECISION) - jnp.matmul(
-        frequency_real_component, inner_im, precision=DFT_PRECISION
+    back_re = jnp.matmul(frequency_real_component, inner_re, precision=precision) + jnp.matmul(
+        spec_im, inner_im, precision=precision
+    )
+    back_im = jnp.matmul(spec_im, inner_re, precision=precision) - jnp.matmul(
+        frequency_real_component, inner_im, precision=precision
     )
     turned_re = back_re * twist_re + back_im * twist_im
     turned_im = back_im * twist_re - back_re * twist_im
-    signal = jnp.einsum("nk,ckm->cnm", outer_re[:half_rows], turned_re, precision=DFT_PRECISION)
-    signal = signal + jnp.einsum("nk,ckm->cnm", outer_im[:half_rows], turned_im, precision=DFT_PRECISION)
+    signal = jnp.einsum("nk,ckm->cnm", outer_re[:half_rows], turned_re, precision=precision)
+    signal = signal + jnp.einsum("nk,ckm->cnm", outer_im[:half_rows], turned_im, precision=precision)
     return (signal / (row_count * block_width)).reshape(channels, half_rows * block_width)
 
 
@@ -154,12 +154,17 @@
     product = (shorts[1].astype(jnp.float32) * shorts[2].astype(jnp.float32)).astype(jnp.bfloat16)
     product_chan = to_channels(product)
     tables = make_tables(product_chan.shape[1], BLOCK)
-    kernel_re, kernel_im = spectrum(filters[0], tables)
-    product_re, product_im = spectrum(product_chan.astype(jnp.float32), tables)
+    channels = product_chan.shape[0]
+    joint_re, joint_im = spectrum(
+        jnp.concatenate([filters[0], product_chan.astype(jnp.float32)]), tables
+    )
+    kernel_re, product_re = joint_re[:channels], joint_re[channels:]
+    kernel_im, product_im = joint_im[:channels], joint_im[channels:]
     convolved_chan = inverse(
         product_re * kernel_re - product_im * kernel_im,
         product_re * kernel_im + product_im * kernel_re,
         tables,
+        lax.Precision.DEFAULT,
     ).astype(jnp.bfloat16)
     full_cotangent = lax.all_gather(cotangent, "tp", axis=0, tiled=True)
     grad_gated = lax.dot_general(
@@ -180,6 +185,7 @@
         kernel_re * gradient_re + kernel_im * gradient_im,
         kernel_re * gradient_im - kernel_im * gradient_re,
         tables,
+        lax.Precision.DEFAULT,
     ).astype(jnp.bfloat16)
     grad_filters = inverse(
         product_re * gradient_re + product_im * gradient_im,

time: 176 us -> 176 us (level)
  matrix products: 39.4 us -> 31.9 us
  starting transfers between devices: 51.8 us -> 54.8 us
  waiting for transfers between devices: 45.3 us -> 48.3 us
    dot_general x18, matrix products: 10.2 us -> 7.67 us  [the longest x3 1.55 us: inverse(): jnp.matmul(frequency_real_component, inner_im, precision=precision)]
    dot_general x1, matrix products: 4.74 us -> 2.46 us  [per_device(): jnp.dot(out_weight, gated_out, preferred_element_type=jnp.float32)]
    all_to_all x1, starting transfers between devices: 4.7 us -> 6.9 us  [weight_gradient(): lax.all_to_all(weight_partial, CTX_HI, split_axis=0, concat_axis=0, tiled...]
    all_gather x1, waiting for transfers between devices: 11.7 us -> 13.9 us  [weight_gradient(): group_gated = lax.all_gather(gated_out, CTX_LO, axis=1, tiled=True)]
    dot_general x3 -> x2, matrix products: 5.04 us -> 3.92 us  [spectrum(): jnp.matmul(turned_im, inner_re, precision=DFT_PRECISION)]
    unnamed x67 -> x48, local copies, waits for them, and re-layouts: 7.28 us -> 7.25 us
  transfers between devices with their start and end apart: 10 -> 10, of which waited for: 6 -> 7; matrix products, arithmetic and copies ran while one was open for 23% -> 19% of each run, Pallas kernels for 0% -> 0%
where the time goes in v5:
time: 176 us; the launch traced here: 174 us
  starting transfers between devices  54.8 us (31%)
  waiting for transfers between devices  48.3 us (27%)
  matrix products  31.9 us (18%)
  local copies, waits for them, and re-layouts  16.2 us (9%)
  between operations  14.4 us (8%)
  other arithmetic  8.15 us (5%)
    all_to_all x1, starting transfers between devices, to_channels(): return lax.all_to_all(block, CTX, split_axis=0, concat_axis=1, tiled=True)  15.5 us
    all_gather x1, waiting for transfers between devices, weight_gradient(): group_gated = lax.all_gather(gated_out, CTX_LO, axis=1, tiled=True)  13.9 us
    reduce_scatter x1, waiting for transfers between devices, per_device(): lax.psum_scatter(jnp.dot(out_weight, gated_out, preferred_element_type=jn...  12.3 us
    all_to_all x1, starting transfers between devices, to_positions(): return lax.all_to_all(block, CTX, split_axis=1, concat_axis=0, tiled=True)  8.67 us
    all_to_all x1, starting transfers between devices, weight_gradient(): lax.all_to_all(by_target, CTX_LO, split_axis=0, concat_axis=0, tiled=True)  8.57 us
    all_to_all x1, starting transfers between devices, swap_layouts(): lax.all_to_all(outgoing, CTX, split_axis=0, concat_axis=0, tiled=True)  8.49 us
    all_to_all x1, waiting for transfers between devices, to_channels(): return lax.all_to_all(block, CTX, split_axis=0, concat_axis=1, tiled=True)  7.41 us
    unnamed x48, local copies, waits for them, and re-layouts  7.25 us
  transfers between devices with their start and end apart: 10, of which 7 were waited for; matrix products, arithmetic and copies ran while one was open for 19% of the time, Pallas kernels for 0%

profile of v5, /device:TPU:22, one launch (start us, length us, event | category | flops | bytes accessed | tf_op | source)
XLA Modules:
  0.0 173.7 jit_solution(2442504439409830359)
XLA Ops:
  8.2 1.0 copy.164
  9.2 1.0 copy.163
  10.3 3.5 %collective-permute-start = (bf16[3,512,6]{1,2,0:T(8,128)(2,1)S(1)}, bf16[3,512,6]{1,2,0:T(8,128)(2,1)S(1)}, u32[]{:S(2)}, u32[]{:S(2)}) collective-permute-start(bf16[3,512,6]{1,2,0:T(8,128)(2,1)S(1)} %pad_maximum_fusion.6), channel_id=1, source_target_pairs={{0,4},{4,8},{8,12},{12,16},{16,20},{20,24},{24,28},{28,32},{32,36}... | collective-permute-start | bytes 55304 | tf_op jit(solution)/shard_map/ppermute | solution.py:22
  13.8 1.2 fusion.201
  17.6 15.5 %all-to-all-start = ((bf16[64,8,128]{2,1,0:T(8,128)(2,1)}), bf16[64,8,128]{2,1,0:T(8,128)(2,1)S(1)}, u32[]{:S(2)}, u32[]{:S(2)}) async-start(bf16[64,8,128]{2,1,0:T(8,128)(2,1)} %bitcast.5), calls=%async_computation | async-start | bytes 262144 | tf_op jit(solution)/shard_map/all_to_all | solution.py:108
  34.2 7.4 %all-to-all-done = bf16[64,8,128]{2,1,0:T(8,128)(2,1)S(1)} async-done(((bf16[64,8,128]{2,1,0:T(8,128)(2,1)}), bf16[64,8,128]{2,1,0:T(8,128)(2,1)S(1)}, u32[]{:S(2)}, u32[]{:S(2)}) %all-to-all-start) | async-done | bytes 131104 | tf_op jit(solution)/shard_map/all_to_all | solution.py:108
  43.7 1.2 fusion.46
  44.9 1.2 fusion.47
  46.1 1.2 convolution_add_fusion
  47.3 1.2 convolution_subtract_fusion
  51.0 4.0 %fusion.51 = (bf16[512,128]{0,1:T(8,128)(2,1)S(1)}, f32[512,128]{0,1:T(8,128)}) fusion(bf16[3,512,128]{1,2,0:T(8,128)(2,1)S(1)} %fusion.19, bf16[4096,512]{1,0:T(8,128)(2,1)} %param.12, bf16[4096,128]{1,0:T(8,128)(2,1)} %all-gather.3.cloned.1.call-done), kind=kOutput, calls=%fused_computation.103 | convolution fusion | flops 537067520 | bytes 5767168 | tf_op jit(solution)/shard_map/dot_general | solution.py:170
  56.0 8.5 %all-to-all-start.1 = ((bf16[64,2,8,128]{3,2,1,0:T(8,128)(2,1)}), bf16[64,2,8,128]{3,2,1,0:T(8,128)(2,1)S(1)}, u32[]{:S(2)}, u32[]{:S(2)}) async-start(bf16[64,2,8,128]{3,2,1,0:T(8,128)(2,1)} %copy.186), calls=%async_computation.1 | async-start | bytes 524288 | tf_op jit(solution)/shard_map/all_to_all | solution.py:126
  64.8 2.3 %copy.212 = bf16[8,8,64,128]{3,2,1,0:T(8,128)(2,1)} copy(bf16[8,8,64,128]{3,2,0,1:T(8,128)(2,1)} %bitcast.204) | data formatting | bytes 2097152 | tf_op jit(solution)/shard_map/transpose | solution.py:139
  67.1 7.1 %all-to-all-done.1 = bf16[64,2,8,128]{3,2,1,0:T(8,128)(2,1)S(1)} async-done(((bf16[64,2,8,128]{3,2,1,0:T(8,128)(2,1)}), bf16[64,2,8,128]{3,2,1,0:T(8,128)(2,1)S(1)}, u32[]{:S(2)}, u32[]{:S(2)}) %all-to-all-start.1) | async-done | bytes 262176 | tf_op jit(solution)/shard_map/all_to_all | solution.py:126
  75.7 1.4 fusion.68
  77.1 1.4 fusion.67
  78.6 1.8 %copy.188 = f32[512,128]{0,1:T(8,128)} copy(f32[512,128]{1,0:T(8,128)} %get-tuple-element.44) | data formatting | bytes 524288 | tf_op jit(solution)/shard_map/convert_element_type | solution.py:175
  80.3 1.7 convolution_subtract_fusion.3
  82.1 2.7 %multiply_add_fusion.2 = (bf16[8,128,128]{2,1,0:T(8,128)(2,1)S(1)}, bf16[8,128,128]{2,1,0:T(8,128)(2,1)S(1)}, f32[8,128,128]{2,1,0:T(8,128)}) fusion(f32[8,128,128]{2,1,0:T(8,128)S(1)} %convolution_subtract_fusion.3, f32[16,128,128]{2,1,0:T(8,128)S(1)} %convolution_add_fusion, f32[16,128,128]{2,1,0:T(8,128)S(1)} %convolution_subtract_fusion, ...), kind=kOutput, calls=%fused_computation.79 | convolution fusion | flops 102465536 | bytes 4325376 | tf_op jit(solution)/shard_map/dot_general | solution.py:57
  86.7 1.6 fusion.65
  89.5 8.7 %all-to-all-start.2 = ((bf16[8,64,128]{2,0,1:T(8,128)(2,1)}), bf16[8,64,128]{2,0,1:T(8,128)(2,1)}, u32[]{:S(2)}, u32[]{:S(2)}) async-start(bf16[8,64,128]{2,0,1:T(8,128)(2,1)} %copy.203), calls=%async_computation.3 | async-start | bytes 262144 | tf_op jit(solution)/shard_map/all_to_all | solution.py:112
  98.2 1.5 multiply_add_fusion.1
  101.0 2.5 %fusion = bf16[4096,128]{0,1:T(8,128)(2,1)} fusion(bf16[512,128]{0,1:T(8,128)(2,1)S(1)} %copy-done.4, bf16[4096,512]{1,0:T(8,128)(2,1)S(1)} %copy-done.1), kind=kOutput, calls=%fused_computation.1 | convolution fusion | flops 537395200 | bytes 5373952 | tf_op jit(solution)/shard_map/dot_general | solution.py:177
  104.1 2.5 %all-to-all-done.2 = bf16[8,64,128]{2,0,1:T(8,128)(2,1)} async-done(((bf16[8,64,128]{2,0,1:T(8,128)(2,1)}), bf16[8,64,128]{2,0,1:T(8,128)(2,1)}, u32[]{:S(2)}, u32[]{:S(2)}) %all-to-all-start.2) | async-done | bytes 131104 | tf_op jit(solution)/shard_map/all_to_all | solution.py:112
  106.6 8.6 %all-to-all-start.3 = ((bf16[8,8,64,128]{3,2,1,0:T(8,128)(2,1)}), bf16[8,8,64,128]{3,2,1,0:T(8,128)(2,1)}, u32[]{:S(2)}, u32[]{:S(2)}) async-start(bf16[8,8,64,128]{3,2,1,0:T(8,128)(2,1)} %copy.212), calls=%async_computation.4 | async-start | bytes 2097152 | tf_op jit(solution)/shard_map/all_to_all | solution.py:140
  117.4 2.8 %collective-permute-start.1 = (bf16[3,512,6]{1,2,0:T(8,128)(2,1)S(1)}, bf16[3,512,6]{1,2,0:T(8,128)(2,1)S(1)}, u32[]{:S(2)}, u32[]{:S(2)}) collective-permute-start(bf16[3,512,6]{1,2,0:T(8,128)(2,1)S(1)} %pad_maximum_fusion.4), channel_id=1, source_target_pairs={{4,0},{8,4},{12,8},{16,12},{20,16},{24,20},{28,24},{32,28},{36,32}... | collective-permute-start | bytes 55304 | tf_op jit(solution)/shard_map/ppermute | solution.py:22
  120.1 4.0 %all-to-all-done.3 = bf16[8,8,64,128]{3,2,1,0:T(8,128)(2,1)} async-done(((bf16[8,8,64,128]{3,2,1,0:T(8,128)(2,1)}), bf16[8,8,64,128]{3,2,1,0:T(8,128)(2,1)}, u32[]{:S(2)}, u32[]{:S(2)}) %all-to-all-start.3) | async-done | bytes 1048608 | tf_op jit(solution)/shard_map/all_to_all | solution.py:140
  124.1 13.9 %all-gather.5.cloned.1.call-done = bf16[512,1024]{0,1:T(8,128)(2,1)} async-done(((bf16[512,128]{0,1:T(8,128)(2,1)}), bf16[512,1024]{0,1:T(8,128)(2,1)}) %all-gather.5.cloned.1.call-update) | async-done | bytes 1048592 | tf_op jit(solution)/shard_map/all_gather | solution.py:137
  138.1 3.1 %fusion.2 = bf16[8,64,512]{2,1,0:T(8,128)(2,1)} fusion(bf16[512,8,128,1]{0,2,3,1:T(8,128)(2,1)} %bitcast.209, bf16[8,8,64,128]{3,2,1,0:T(8,128)(2,1)} %all-to-all-done.3), kind=kOutput, calls=%fused_computation.8 | convolution fusion | flops 537133056 | bytes 2621440 | tf_op jit(solution)/shard_map/dot_general | solution.py:141
  141.2 6.9 %all-to-all-start.4 = ((bf16[8,64,512]{2,1,0:T(8,128)(2,1)}), bf16[8,64,512]{2,1,0:T(8,128)(2,1)S(1)}, u32[]{:S(2)}, u32[]{:S(2)}) async-start(bf16[8,64,512]{2,1,0:T(8,128)(2,1)} %fusion.2), calls=%async_computation.5 | async-start | bytes 1048576 | tf_op jit(solution)/shard_map/all_to_all | solution.py:144
  152.3 12.3 %reduce-scatter.2.cloned.1.call-done = bf16[1024,128]{0,1:T(8,128)(2,1)} async-done(((bf16[4096,128]{0,1:T(8,128)(2,1)}), bf16[1024,128]{0,1:T(8,128)(2,1)}) %reduce-scatter.2.cloned.1.call-update) | async-done | bytes 262160 | tf_op jit(solution)/shard_map/reduce_scatter | solution.py:176
  164.6 1.8 %copy.215 = bf16[1024,128]{1,0:T(8,128)(2,1)} copy(bf16[1024,128]{0,1:T(8,128)(2,1)} %reduce-scatter.2.cloned.1.call-done) | data formatting | bytes 524288
  (104 shorter events, 23.7 us)
Async XLA Ops:
  7.2 43.8 %all-gather.3.cloned.1.call-start = ((), (), s32[]{:S(2)}) async-start(), calls=%async_computation.6 | async-start | bytes 1310720 | tf_op jit(solution)/shard_map/all_gather | solution.py:169
  10.3 5.7 %collective-permute-start = (bf16[3,512,6]{1,2,0:T(8,128)(2,1)S(1)}, bf16[3,512,6]{1,2,0:T(8,128)(2,1)S(1)}, u32[]{:S(2)}, u32[]{:S(2)}) collective-permute-start(bf16[3,512,6]{1,2,0:T(8,128)(2,1)S(1)} %pad_maximum_fusion.6), channel_id=1, source_target_pairs={{0,4},{4,8},{8,12},{12,16},{16,20},{20,24},{24,28},{28,32},{32,36}... | collective-permute-start | bytes 55304 | tf_op jit(solution)/shard_map/ppermute | solution.py:22
  15.0 18.4 %copy-start.7 = (f32[1,8,8192]{2,1,0:T(8,128)S(1)}, f32[1,8,8192]{2,1,0:T(8,128)}, u32[]{:S(2)}) copy-start(f32[1,8,8192]{2,1,0:T(8,128)} %param.11) | copy-start | bytes 786436
  15.1 2.5 %copy-start.8 = (f32[3,512]{1,0:T(4,128)}, f32[3,512]{1,0:T(4,128)S(1)}, u32[]{:S(2)}) copy-start(f32[3,512]{1,0:T(4,128)S(1)} %get-tuple-element.57) | copy-start | bytes 18436
  15.1 2.5 %copy-start.10 = (f32[3,512]{1,0:T(4,128)}, f32[3,512]{1,0:T(4,128)S(1)}, u32[]{:S(2)}) copy-start(f32[3,512]{1,0:T(4,128)S(1)} %get-tuple-element.58) | copy-start | bytes 18436
  15.1 2.5 %copy-start.12 = (f32[3,512]{1,0:T(4,128)}, f32[3,512]{1,0:T(4,128)S(1)}, u32[]{:S(2)}) copy-start(f32[3,512]{1,0:T(4,128)S(1)} %get-tuple-element.59) | copy-start | bytes 18436
  15.1 2.5 %copy-start.14 = (f32[3,512]{1,0:T(4,128)}, f32[3,512]{1,0:T(4,128)S(1)}, u32[]{:S(2)}) copy-start(f32[3,512]{1,0:T(4,128)S(1)} %get-tuple-element.60) | copy-start | bytes 18436
  15.1 2.5 %copy-start.16 = (f32[3,512,1]{1,0,2:T(4,128)}, f32[3,512,1]{1,0,2:T(4,128)S(1)}, u32[]{:S(2)}) copy-start(f32[3,512,1]{1,0,2:T(4,128)S(1)} %copy.303) | copy-start | bytes 18436
  16.8 34.2 %copy-start.2 = (bf16[3,512,128]{1,2,0:T(8,128)(2,1)}, bf16[3,512,128]{1,2,0:T(8,128)(2,1)S(1)}, u32[]{:S(2)}) copy-start(bf16[3,512,128]{1,2,0:T(8,128)(2,1)S(1)} %fusion.19) | copy-start | bytes 1179652
  17.6 24.0 %all-to-all-start = ((bf16[64,8,128]{2,1,0:T(8,128)(2,1)}), bf16[64,8,128]{2,1,0:T(8,128)(2,1)S(1)}, u32[]{:S(2)}, u32[]{:S(2)}) async-start(bf16[64,8,128]{2,1,0:T(8,128)(2,1)} %bitcast.5), calls=%async_computation | async-start | bytes 262144 | tf_op jit(solution)/shard_map/all_to_all | solution.py:108
  56.0 18.2 %all-to-all-start.1 = ((bf16[64,2,8,128]{3,2,1,0:T(8,128)(2,1)}), bf16[64,2,8,128]{3,2,1,0:T(8,128)(2,1)S(1)}, u32[]{:S(2)}, u32[]{:S(2)}) async-start(bf16[64,2,8,128]{3,2,1,0:T(8,128)(2,1)} %copy.186), calls=%async_computation.1 | async-start | bytes 524288 | tf_op jit(solution)/shard_map/all_to_all | solution.py:126
  64.5 73.5 %all-gather.5.cloned.1.call-start = ((), (), s32[]{:S(2)}) async-start(), calls=%async_computation.8 | async-start | bytes 1179648 | tf_op jit(solution)/shard_map/all_gather | solution.py:137
  82.0 4.6 %copy-start = (f32[8,128,128]{2,1,0:T(8,128)}, f32[8,128,128]{2,1,0:T(8,128)S(1)}, u32[]{:S(2)}) copy-start(f32[8,128,128]{2,1,0:T(8,128)S(1)} %convolution_subtract_fusion.3) | copy-start | bytes 1572868
  82.0 4.6 %copy-start.5 = (f32[512,128]{0,1:T(8,128)S(1)}, f32[512,128]{0,1:T(8,128)}, u32[]{:S(2)}) copy-start(f32[512,128]{0,1:T(8,128)} %copy.188) | copy-start | bytes 786436
  82.0 4.6 %copy-start.6 = (f32[512,128]{0,1:T(8,128)S(1)}, f32[512,128]{0,1:T(8,128)}, u32[]{:S(2)}) copy-start(f32[512,128]{0,1:T(8,128)} %get-tuple-element.53) | copy-start | bytes 786436
  89.5 17.1 %all-to-all-start.2 = ((bf16[8,64,128]{2,0,1:T(8,128)(2,1)}), bf16[8,64,128]{2,0,1:T(8,128)(2,1)}, u32[]{:S(2)}, u32[]{:S(2)}) async-start(bf16[8,64,128]{2,0,1:T(8,128)(2,1)} %copy.203), calls=%async_computation.3 | async-start | bytes 262144 | tf_op jit(solution)/shard_map/all_to_all | solution.py:112
  98.2 2.8 %copy-start.1 = (bf16[4096,512]{1,0:T(8,128)(2,1)S(1)}, bf16[4096,512]{1,0:T(8,128)(2,1)}, u32[]{:S(2)}) copy-start(bf16[4096,512]{1,0:T(8,128)(2,1)} %param.12) | copy-start | bytes 12582916
  98.2 2.8 %copy-start.4 = (bf16[512,128]{0,1:T(8,128)(2,1)S(1)}, bf16[512,128]{0,1:T(8,128)(2,1)}, u32[]{:S(2)}) copy-start(bf16[512,128]{0,1:T(8,128)(2,1)} %get-tuple-element.42) | copy-start | bytes 393220
  103.5 13.8 %copy-start.3 = (bf16[3,512,128]{1,2,0:T(8,128)(2,1)S(1)}, bf16[3,512,128]{1,2,0:T(8,128)(2,1)}, u32[]{:S(2)}) copy-start(bf16[3,512,128]{1,2,0:T(8,128)(2,1)} %copy-done.2) | copy-start | bytes 1179652
  106.6 17.5 %all-to-all-start.3 = ((bf16[8,8,64,128]{3,2,1,0:T(8,128)(2,1)}), bf16[8,8,64,128]{3,2,1,0:T(8,128)(2,1)}, u32[]{:S(2)}, u32[]{:S(2)}) async-start(bf16[8,8,64,128]{3,2,1,0:T(8,128)(2,1)} %copy.212), calls=%async_computation.4 | async-start | bytes 2097152 | tf_op jit(solution)/shard_map/all_to_all | solution.py:140
  115.2 49.5 %reduce-scatter.2.cloned.1.call-start = ((), (), s32[]{:S(2)}) async-start(), calls=%async_computation.7 | async-start | bytes 1310720 | tf_op jit(solution)/shard_map/reduce_scatter | solution.py:176
  117.4 31.8 %collective-permute-start.1 = (bf16[3,512,6]{1,2,0:T(8,128)(2,1)S(1)}, bf16[3,512,6]{1,2,0:T(8,128)(2,1)S(1)}, u32[]{:S(2)}, u32[]{:S(2)}) collective-permute-start(bf16[3,512,6]{1,2,0:T(8,128)(2,1)S(1)} %pad_maximum_fusion.4), channel_id=1, source_target_pairs={{4,0},{8,4},{12,8},{16,12},{20,16},{24,20},{28,24},{32,28},{36,32}... | collective-permute-start | bytes 55304 | tf_op jit(solution)/shard_map/ppermute | solution.py:22
  138.0 11.2 %copy-start.9 = (f32[3,512]{1,0:T(4,128)S(1)}, f32[3,512]{1,0:T(4,128)}, u32[]{:S(2)}) copy-start(f32[3,512]{1,0:T(4,128)} %copy-done.8) | copy-start | bytes 18436
  138.0 11.2 %copy-start.11 = (f32[3,512]{1,0:T(4,128)S(1)}, f32[3,512]{1,0:T(4,128)}, u32[]{:S(2)}) copy-start(f32[3,512]{1,0:T(4,128)} %copy-done.10) | copy-start | bytes 18436
  138.0 11.2 %copy-start.13 = (f32[3,512]{1,0:T(4,128)S(1)}, f32[3,512]{1,0:T(4,128)}, u32[]{:S(2)}) copy-start(f32[3,512]{1,0:T(4,128)} %copy-done.12) | copy-start | bytes 18436
  138.0 11.3 %copy-start.15 = (f32[3,512]{1,0:T(4,128)S(1)}, f32[3,512]{1,0:T(4,128)}, u32[]{:S(2)}) copy-start(f32[3,512]{1,0:T(4,128)} %copy-done.14) | copy-start | bytes 18436
  138.0 11.3 %copy-start.17 = (f32[3,512,1]{1,0,2:T(4,128)S(1)}, f32[3,512,1]{1,0,2:T(4,128)}, u32[]{:S(2)}) copy-start(f32[3,512,1]{1,0,2:T(4,128)} %copy-done.16) | copy-start | bytes 18436
  141.2 25.2 %all-to-all-start.4 = ((bf16[8,64,512]{2,1,0:T(8,128)(2,1)}), bf16[8,64,512]{2,1,0:T(8,128)(2,1)S(1)}, u32[]{:S(2)}, u32[]{:S(2)}) async-start(bf16[8,64,512]{2,1,0:T(8,128)(2,1)} %fusion.2), calls=%async_computation.5 | async-start | bytes 1048576 | tf_op jit(solution)/shard_map/all_to_all | solution.py:144
Sparse Core Ops, SparseCore 0:
  13.9 26.2 all-gather.2
  88.4 49.5 all-gather.4
  140.6 23.9 reduce-scatter.1

commit v6 on v4

--- a/solution.py
+++ b/solution.py
@@ -41,21 +41,21 @@
     return (outer_re, outer_im, inner_re, inner_im, jnp.cos(angles), -jnp.sin(angles))
 
 
-def spectrum(signal, tables):
+def spectrum(signal, tables, precision=DFT_PRECISION):
     outer_re, outer_im, inner_re, inner_im, twist_re, twist_im = tables
     channels, length = signal.shape
     block_width = inner_re.shape[0]
     half_rows = length // block_width
     blocks = signal.reshape(channels, half_rows, block_width)
-    section_re = jnp.einsum("kn,cnm->ckm", outer_re[:, :half_rows], blocks, precision=DFT_PRECISION)
-    section_im = jnp.einsum("kn,cnm->ckm", outer_im[:, :half_rows], blocks, precision=DFT_PRECISION)
+    section_re = jnp.einsum("kn,cnm->ckm", outer_re[:, :half_rows], blocks, precision=precision)
+    section_im = jnp.einsum("kn,cnm->ckm", outer_im[:, :half_rows], blocks, precision=precision)
     turned_re = section_re * twist_re - section_im * twist_im
     turned_im = section_re * twist_im + section_im * twist_re
-    frequency_real_component = jnp.matmul(turned_re, inner_re, precision=DFT_PRECISION) - jnp.matmul(
-        turned_im, inner_im, precision=DFT_PRECISION
-    )
-    spec_im = jnp.matmul(turned_re, inner_im, precision=DFT_PRECISION) + jnp.matmul(
-        turned_im, inner_re, precision=DFT_PRECISION
+    frequency_real_component = jnp.matmul(turned_re, inner_re, precision=precision) - jnp.matmul(
+        turned_im, inner_im, precision=precision
+    )
+    spec_im = jnp.matmul(turned_re, inner_im, precision=precision) + jnp.matmul(
+        turned_im, inner_re, precision=precision
     )
     return (frequency_real_component, spec_im)
 
@@ -156,7 +156,9 @@
     tables = make_tables(product_chan.shape[1], BLOCK)
     channels = product_chan.shape[0]
     joint_re, joint_im = spectrum(
-        jnp.concatenate([filters[0], product_chan.astype(jnp.float32)]), tables
+        jnp.concatenate([filters[0], product_chan.astype(jnp.float32)]),
+        tables,
+        lax.Precision.DEFAULT,
     )
     kernel_re, product_re = joint_re[:channels], joint_re[channels:]
     kernel_im, product_im = joint_im[:channels], joint_im[channels:]

time: 172 us -> 169 us (0.983)
  matrix products: 33.4 us -> 29.7 us
    dot_general x12, matrix products: 14.8 us -> 11.1 us  [the longest x2 3.08 us: spectrum(): jnp.matmul(turned_im, inner_im, precision=precision)]
  transfers between devices with their start and end apart: 9 -> 9, of which waited for: 6 -> 6; matrix products, arithmetic and copies ran while one was open for 20% -> 19% of each run, Pallas kernels for 0% -> 0%
where the time goes in v6:
time: 169 us; the launch traced here: 168 us
  waiting for transfers between devices  45.3 us (27%)
  starting transfers between devices  40.9 us (24%)
  matrix products  29.7 us (18%)
  blocking collectives  17.7 us (10%)
  between operations  14.4 us (9%)
  local copies, waits for them, and re-layouts  14.3 us (8%)
  other arithmetic  5.87 us (3%)
    all_to_all x1, blocking collectives, swap_layouts(): lax.all_to_all(outgoing, CTX, split_axis=0, concat_axis=0, tiled=True)  17.7 us
    all_to_all x1, starting transfers between devices, to_channels(): return lax.all_to_all(block, CTX, split_axis=0, concat_axis=1, tiled=True)  15.5 us
    ppermute x2, waiting for transfers between devices, from_behind(): lax.ppermute(value, axis, [(source, source + steps) for source in range(f...  13.5 us
    all_gather x1, waiting for transfers between devices, weight_gradient(): group_gated = lax.all_gather(gated_out, CTX_LO, axis=1, tiled=True)  10.7 us
    all_to_all x1, starting transfers between devices, to_positions(): return lax.all_to_all(block, CTX, split_axis=1, concat_axis=0, tiled=True)  8.36 us
    all_to_all x1, starting transfers between devices, weight_gradient(): lax.all_to_all(by_target, CTX_LO, split_axis=0, concat_axis=0, tiled=True)  7.97 us
    all_to_all x1, waiting for transfers between devices, to_channels(): return lax.all_to_all(block, CTX, split_axis=0, concat_axis=1, tiled=True)  7.35 us
    all_to_all x1, waiting for transfers between devices, to_positions(): return lax.all_to_all(block, CTX, split_axis=1, concat_axis=0, tiled=True)  7.3 us
  transfers between devices with their start and end apart: 9, of which 6 were waited for; matrix products, arithmetic and copies ran while one was open for 19% of the time, Pallas kernels for 0%

profile of v6, /device:TPU:22, one launch (start us, length us, event | category | flops | bytes accessed | tf_op | source)
XLA Modules:
  0.0 168.1 jit_solution(17225023423450547552)
XLA Ops:
  7.2 1.0 copy.165
  8.2 1.0 copy.164
  9.2 1.0 copy.163
  10.3 3.5 %collective-permute-start = (bf16[3,512,6]{1,2,0:T(8,128)(2,1)S(1)}, bf16[3,512,6]{1,2,0:T(8,128)(2,1)S(1)}, u32[]{:S(2)}, u32[]{:S(2)}) collective-permute-start(bf16[3,512,6]{1,2,0:T(8,128)(2,1)S(1)} %pad_maximum_fusion.12), channel_id=1, source_target_pairs={{0,4},{4,8},{8,12},{12,16},{16,20},{20,24},{24,28},{28,32},{32,36}... | collective-permute-start | bytes 55304 | tf_op jit(solution)/shard_map/ppermute | solution.py:22
  13.8 1.2 fusion.167
  15.1 0.9 collective-permute-done
  17.6 15.5 %all-to-all-start = ((bf16[64,8,128]{2,1,0:T(8,128)(2,1)}), bf16[64,8,128]{2,1,0:T(8,128)(2,1)S(1)}, u32[]{:S(2)}, u32[]{:S(2)}) async-start(bf16[64,8,128]{2,1,0:T(8,128)(2,1)} %bitcast.5), calls=%async_computation | async-start | bytes 262144 | tf_op jit(solution)/shard_map/all_to_all | solution.py:108
  34.3 7.3 %all-to-all-done = bf16[64,8,128]{2,1,0:T(8,128)(2,1)S(1)} async-done(((bf16[64,8,128]{2,1,0:T(8,128)(2,1)}), bf16[64,8,128]{2,1,0:T(8,128)(2,1)S(1)}, u32[]{:S(2)}, u32[]{:S(2)}) %all-to-all-start) | async-done | bytes 131104 | tf_op jit(solution)/shard_map/all_to_all | solution.py:108
  47.3 4.0 %fusion.47 = (bf16[512,128]{0,1:T(8,128)(2,1)S(1)}, f32[512,128]{0,1:T(8,128)}) fusion(bf16[3,512,128]{1,2,0:T(8,128)(2,1)S(1)} %fusion.25, bf16[4096,512]{1,0:T(8,128)(2,1)} %param.12, bf16[4096,128]{1,0:T(8,128)(2,1)} %all-gather.3.cloned.1.call-done), kind=kOutput, calls=%fused_computation.98 | convolution fusion | flops 537067520 | bytes 5767168 | tf_op jit(solution)/shard_map/dot_general | solution.py:172
  51.6 17.7 %all_to_all.35 = bf16[64,2,8,128]{3,2,1,0:T(8,128)(2,1)S(1)} all-to-all(bf16[64,2,8,128]{3,2,1,0:T(8,128)(2,1)S(1)} %copy.186), channel_id=1, replica_groups=mesh['ctx_hi'=8,'ctx_lo'=8,'tp'=4] {'ctx_hi','ctx_lo'}, dimensions={0} | all-to-all | bytes 524288 | tf_op jit(solution)/shard_map/all_to_all | solution.py:126
  70.8 1.4 fusion.56
  72.2 1.4 fusion.55
  73.7 1.8 %copy.188 = f32[512,128]{0,1:T(8,128)} copy(f32[512,128]{1,0:T(8,128)} %get-tuple-element.44) | data formatting | bytes 524288 | tf_op jit(solution)/shard_map/convert_element_type | solution.py:177
  75.5 2.5 %convolution_subtract_fusion.2 = f32[8,128,128]{2,1,0:T(8,128)} fusion(f32[8,128,128]{2,1,0:T(8,128)} %fusion.56, f32[8,128,128]{2,1,0:T(8,128)S(1)} %convolution_bitcast_fusion.3, f32[8,128,128]{2,1,0:T(8,128)S(1)} %convolution_bitcast_fusion.4, f32[128,128]{1,0:T(8,128)S(1)} %copy.181, f32[128,128]{1,0:T(8,128)S(1)} %copy.178), kind=kOutput, calls=%fused_computation.17 | convolution fusion | flops 101433344 | bytes 2228224 | tf_op jit(solution)/shard_map/dot_general | solution.py:54
  77.9 1.8 %fusion.53 = (bf16[1,512,128]{1,2,0:T(8,128)(2,1)S(1)}, bf16[512,128]{0,1:T(8,128)(2,1)}) fusion(f32[512,128]{0,1:T(8,128)} %get-tuple-element.53, f32[512,128]{0,1:T(8,128)} %copy.188, bf16[3,512,128]{1,2,0:T(8,128)(2,1)} %copy-done), kind=kLoop, calls=%fused_computation.110 | loop fusion | flops 327680 | bytes 917504 | tf_op jit(solution)/shard_map/stack | solution.py:204
  79.7 2.0 %multiply_add_fusion.2 = (f32[8,128,128]{2,1,0:T(8,128)S(1)}, f32[8,128,128]{2,1,0:T(8,128)S(1)}, f32[8,128,128]{2,1,0:T(8,128)S(1)}, f32[8,128,128]{2,1,0:T(8,128)S(1)}) fusion(f32[8,128,128]{2,1,0:T(8,128)} %convolution_subtract_fusion.2, f32[16,128,128]{2,1,0:T(8,128)S(1)} %convolution_add_fusion.1, f32[16,128,128]{2,1,0:T(8,128)S(1)} %convolution_subtract_fusion.1, ...), kind=kOutput, calls=%fused_computation.70 | convolution fusion | flops 102989824 | bytes 6422528 | tf_op jit(solution)/shard_map/dot_general | solution.py:57
  81.8 0.8 fusion.15
  82.6 0.8 fusion.16
  83.5 0.9 convolution_subtract_fusion
  84.3 0.8 convolution_add_fusion
  87.5 8.4 %all-to-all-start.2 = ((bf16[8,64,128]{2,0,1:T(8,128)(2,1)}), bf16[8,64,128]{2,0,1:T(8,128)(2,1)S(1)}, u32[]{:S(2)}, u32[]{:S(2)}) async-start(bf16[8,64,128]{2,0,1:T(8,128)(2,1)} %copy.209), calls=%async_computation.3 | async-start | bytes 262144 | tf_op jit(solution)/shard_map/all_to_all | solution.py:112
  95.9 1.1 copy.212
  97.0 7.3 %all-to-all-done.2 = bf16[8,64,128]{2,0,1:T(8,128)(2,1)S(1)} async-done(((bf16[8,64,128]{2,0,1:T(8,128)(2,1)}), bf16[8,64,128]{2,0,1:T(8,128)(2,1)S(1)}, u32[]{:S(2)}, u32[]{:S(2)}) %all-to-all-start.2) | async-done | bytes 131104 | tf_op jit(solution)/shard_map/all_to_all | solution.py:112
  104.3 8.0 %all-to-all-start.3 = ((bf16[8,8,64,128]{3,2,1,0:T(8,128)(2,1)}), bf16[8,8,64,128]{3,2,1,0:T(8,128)(2,1)S(1)}, u32[]{:S(2)}, u32[]{:S(2)}) async-start(bf16[8,8,64,128]{3,2,1,0:T(8,128)(2,1)} %copy.212), calls=%async_computation.4 | async-start | bytes 2097152 | tf_op jit(solution)/shard_map/all_to_all | solution.py:140
  112.2 4.7 %fusion = bf16[4096,128]{0,1:T(8,128)(2,1)} fusion(bf16[512,128]{0,1:T(8,128)(2,1)S(1)} %copy-done.2, bf16[4096,512]{1,0:T(8,128)(2,1)} %param.12), kind=kOutput, calls=%fused_computation.1 | convolution fusion | flops 537395200 | bytes 5373952 | tf_op jit(solution)/shard_map/dot_general | solution.py:179
  117.1 6.4 %all-to-all-done.3 = bf16[8,8,64,128]{3,2,1,0:T(8,128)(2,1)S(1)} async-done(((bf16[8,8,64,128]{3,2,1,0:T(8,128)(2,1)}), bf16[8,8,64,128]{3,2,1,0:T(8,128)(2,1)S(1)}, u32[]{:S(2)}, u32[]{:S(2)}) %all-to-all-start.3) | async-done | bytes 1048608 | tf_op jit(solution)/shard_map/all_to_all | solution.py:140
  123.5 10.7 %all-gather.5.cloned.1.call-done = bf16[512,1024]{0,1:T(8,128)(2,1)} async-done(((bf16[512,128]{0,1:T(8,128)(2,1)}), bf16[512,1024]{0,1:T(8,128)(2,1)}) %all-gather.5.cloned.1.call-update) | async-done | bytes 1048592 | tf_op jit(solution)/shard_map/all_gather | solution.py:137
  134.2 2.8 %fusion.2 = bf16[8,64,512]{2,1,0:T(8,128)(2,1)} fusion(bf16[512,8,128,1]{0,2,3,1:T(8,128)(2,1)} %bitcast.186, bf16[8,8,64,128]{3,2,1,0:T(8,128)(2,1)S(1)} %all-to-all-done.3), kind=kOutput, calls=%fused_computation.10 | convolution fusion | flops 537133056 | bytes 2621440 | tf_op jit(solution)/shard_map/dot_general | solution.py:141
  137.0 3.5 %all-to-all-start.4 = ((bf16[8,64,512]{2,1,0:T(8,128)(2,1)}), bf16[8,64,512]{2,1,0:T(8,128)(2,1)S(1)}, u32[]{:S(2)}, u32[]{:S(2)}) async-start(bf16[8,64,512]{2,1,0:T(8,128)(2,1)} %fusion.2), calls=%async_computation.5 | async-start | bytes 1048576 | tf_op jit(solution)/shard_map/all_to_all | solution.py:144
  140.6 1.9 %collective-permute-start.1 = (bf16[3,512,6]{1,2,0:T(8,128)(2,1)S(1)}, bf16[3,512,6]{1,2,0:T(8,128)(2,1)S(1)}, u32[]{:S(2)}, u32[]{:S(2)}) collective-permute-start(bf16[3,512,6]{1,2,0:T(8,128)(2,1)S(1)} %pad_maximum_fusion.10), channel_id=1, source_target_pairs={{4,0},{8,4},{12,8},{16,12},{20,16},{24,20},{28,24},{32,28},{36,32}... | collective-permute-start | bytes 55304 | tf_op jit(solution)/shard_map/ppermute | solution.py:22
  143.3 12.6 %collective-permute-done.1 = bf16[3,512,6]{1,2,0:T(8,128)(2,1)S(1)} collective-permute-done((bf16[3,512,6]{1,2,0:T(8,128)(2,1)S(1)}, bf16[3,512,6]{1,2,0:T(8,128)(2,1)S(1)}, u32[]{:S(2)}, u32[]{:S(2)}) %collective-permute-start.1) | collective-permute-done | bytes 18464 | tf_op jit(solution)/shard_map/ppermute | solution.py:22
  159.0 1.8 %copy.215 = bf16[1024,128]{1,0:T(8,128)(2,1)} copy(bf16[1024,128]{0,1:T(8,128)(2,1)} %reduce-scatter.2.cloned.1.call-done) | data formatting | bytes 524288
  (100 shorter events, 17.2 us)
Async XLA Ops:
  7.2 40.1 %all-gather.3.cloned.1.call-start = ((), (), s32[]{:S(2)}) async-start(), calls=%async_computation.6 | async-start | bytes 1310720 | tf_op jit(solution)/shard_map/all_gather | solution.py:171
  10.3 5.7 %collective-permute-start = (bf16[3,512,6]{1,2,0:T(8,128)(2,1)S(1)}, bf16[3,512,6]{1,2,0:T(8,128)(2,1)S(1)}, u32[]{:S(2)}, u32[]{:S(2)}) collective-permute-start(bf16[3,512,6]{1,2,0:T(8,128)(2,1)S(1)} %pad_maximum_fusion.12), channel_id=1, source_target_pairs={{0,4},{4,8},{8,12},{12,16},{16,20},{20,24},{24,28},{28,32},{32,36}... | collective-permute-start | bytes 55304 | tf_op jit(solution)/shard_map/ppermute | solution.py:22
  15.0 18.5 %copy-start.8 = (f32[1,8,8192]{2,1,0:T(8,128)S(1)}, f32[1,8,8192]{2,1,0:T(8,128)}, u32[]{:S(2)}) copy-start(f32[1,8,8192]{2,1,0:T(8,128)} %param.11) | copy-start | bytes 786436
  15.1 2.5 %copy-start.9 = (f32[3,512]{1,0:T(4,128)}, f32[3,512]{1,0:T(4,128)S(1)}, u32[]{:S(2)}) copy-start(f32[3,512]{1,0:T(4,128)S(1)} %get-tuple-element.56) | copy-start | bytes 18436
  15.1 2.5 %copy-start.11 = (f32[3,512]{1,0:T(4,128)}, f32[3,512]{1,0:T(4,128)S(1)}, u32[]{:S(2)}) copy-start(f32[3,512]{1,0:T(4,128)S(1)} %get-tuple-element.57) | copy-start | bytes 18436
  15.1 2.5 %copy-start.13 = (f32[3,512]{1,0:T(4,128)}, f32[3,512]{1,0:T(4,128)S(1)}, u32[]{:S(2)}) copy-start(f32[3,512]{1,0:T(4,128)S(1)} %get-tuple-element.58) | copy-start | bytes 18436
  15.1 2.5 %copy-start.15 = (f32[3,512]{1,0:T(4,128)}, f32[3,512]{1,0:T(4,128)S(1)}, u32[]{:S(2)}) copy-start(f32[3,512]{1,0:T(4,128)S(1)} %get-tuple-element.59) | copy-start | bytes 18436
  15.1 2.5 %copy-start.17 = (f32[3,512,1]{1,0,2:T(4,128)}, f32[3,512,1]{1,0,2:T(4,128)S(1)}, u32[]{:S(2)}) copy-start(f32[3,512,1]{1,0,2:T(4,128)S(1)} %copy.298) | copy-start | bytes 18436
  16.8 30.5 %copy-start = (bf16[3,512,128]{1,2,0:T(8,128)(2,1)}, bf16[3,512,128]{1,2,0:T(8,128)(2,1)S(1)}, u32[]{:S(2)}) copy-start(bf16[3,512,128]{1,2,0:T(8,128)(2,1)S(1)} %fusion.25) | copy-start | bytes 1179652
  17.6 24.0 %all-to-all-start = ((bf16[64,8,128]{2,1,0:T(8,128)(2,1)}), bf16[64,8,128]{2,1,0:T(8,128)(2,1)S(1)}, u32[]{:S(2)}, u32[]{:S(2)}) async-start(bf16[64,8,128]{2,1,0:T(8,128)(2,1)} %bitcast.5), calls=%async_computation | async-start | bytes 262144 | tf_op jit(solution)/shard_map/all_to_all | solution.py:108
  33.2 101.0 %all-gather.5.cloned.1.call-start = ((), (), s32[]{:S(2)}) async-start(), calls=%async_computation.8 | async-start | bytes 1179648 | tf_op jit(solution)/shard_map/all_gather | solution.py:137
  34.0 36.0 %copy-start.4 = (f32[128,128]{0,1:T(8,128)}, f32[128,128]{0,1:T(8,128)S(1)}, u32[]{:S(2)}) copy-start(f32[128,128]{0,1:T(8,128)S(1)} %sine_negate_fusion.1) | copy-start | bytes 196612
  34.3 36.1 %copy-start.6 = (f32[128,128]{0,1:T(8,128)}, f32[128,128]{0,1:T(8,128)S(1)}, u32[]{:S(2)}) copy-start(f32[128,128]{0,1:T(8,128)S(1)} %fusion.87) | copy-start | bytes 196612
  82.6 2.6 %copy-start.7 = (f32[128,128]{0,1:T(8,128)S(1)}, f32[128,128]{0,1:T(8,128)}, u32[]{:S(2)}) copy-start(f32[128,128]{0,1:T(8,128)} %copy-done.6) | copy-start | bytes 196612
  83.5 2.5 %copy-start.5 = (f32[128,128]{0,1:T(8,128)S(1)}, f32[128,128]{0,1:T(8,128)}, u32[]{:S(2)}) copy-start(f32[128,128]{0,1:T(8,128)} %copy-done.4) | copy-start | bytes 196612
  85.2 10.7 %copy-start.3 = (bf16[4096,128]{1,0:T(8,128)(2,1)S(1)}, bf16[4096,128]{1,0:T(8,128)(2,1)}, u32[]{:S(2)}) copy-start(bf16[4096,128]{1,0:T(8,128)(2,1)} %all-gather.3.cloned.1.call-done) | copy-start | bytes 3145732
  86.0 26.3 %copy-start.2 = (bf16[512,128]{0,1:T(8,128)(2,1)S(1)}, bf16[512,128]{0,1:T(8,128)(2,1)}, u32[]{:S(2)}) copy-start(bf16[512,128]{0,1:T(8,128)(2,1)} %get-tuple-element.42) | copy-start | bytes 393220
  87.5 16.8 %all-to-all-start.2 = ((bf16[8,64,128]{2,0,1:T(8,128)(2,1)}), bf16[8,64,128]{2,0,1:T(8,128)(2,1)S(1)}, u32[]{:S(2)}, u32[]{:S(2)}) async-start(bf16[8,64,128]{2,0,1:T(8,128)(2,1)} %copy.209), calls=%async_computation.3 | async-start | bytes 262144 | tf_op jit(solution)/shard_map/all_to_all | solution.py:112
  104.3 19.2 %all-to-all-start.3 = ((bf16[8,8,64,128]{3,2,1,0:T(8,128)(2,1)}), bf16[8,8,64,128]{3,2,1,0:T(8,128)(2,1)S(1)}, u32[]{:S(2)}, u32[]{:S(2)}) async-start(bf16[8,8,64,128]{3,2,1,0:T(8,128)(2,1)} %copy.212), calls=%async_computation.4 | async-start | bytes 2097152 | tf_op jit(solution)/shard_map/all_to_all | solution.py:140
  112.2 46.8 %reduce-scatter.2.cloned.1.call-start = ((), (), s32[]{:S(2)}) async-start(), calls=%async_computation.7 | async-start | bytes 1310720 | tf_op jit(solution)/shard_map/reduce_scatter | solution.py:178
  116.9 23.6 %copy-start.1 = (bf16[3,512,128]{1,2,0:T(8,128)(2,1)S(1)}, bf16[3,512,128]{1,2,0:T(8,128)(2,1)}, u32[]{:S(2)}) copy-start(bf16[3,512,128]{1,2,0:T(8,128)(2,1)} %copy-done) | copy-start | bytes 1179652
  134.2 21.8 %copy-start.10 = (f32[3,512]{1,0:T(4,128)S(1)}, f32[3,512]{1,0:T(4,128)}, u32[]{:S(2)}) copy-start(f32[3,512]{1,0:T(4,128)} %copy-done.9) | copy-start | bytes 18436
  134.2 21.8 %copy-start.12 = (f32[3,512]{1,0:T(4,128)S(1)}, f32[3,512]{1,0:T(4,128)}, u32[]{:S(2)}) copy-start(f32[3,512]{1,0:T(4,128)} %copy-done.11) | copy-start | bytes 18436
  134.2 21.9 %copy-start.14 = (f32[3,512]{1,0:T(4,128)S(1)}, f32[3,512]{1,0:T(4,128)}, u32[]{:S(2)}) copy-start(f32[3,512]{1,0:T(4,128)} %copy-done.13) | copy-start | bytes 18436
  134.2 21.9 %copy-start.16 = (f32[3,512]{1,0:T(4,128)S(1)}, f32[3,512]{1,0:T(4,128)}, u32[]{:S(2)}) copy-start(f32[3,512]{1,0:T(4,128)} %copy-done.15) | copy-start | bytes 18436
  134.2 21.9 %copy-start.18 = (f32[3,512,1]{1,0,2:T(4,128)S(1)}, f32[3,512,1]{1,0,2:T(4,128)}, u32[]{:S(2)}) copy-start(f32[3,512,1]{1,0,2:T(4,128)} %copy-done.17) | copy-start | bytes 18436
  137.0 23.8 %all-to-all-start.4 = ((bf16[8,64,512]{2,1,0:T(8,128)(2,1)}), bf16[8,64,512]{2,1,0:T(8,128)(2,1)S(1)}, u32[]{:S(2)}, u32[]{:S(2)}) async-start(bf16[8,64,512]{2,1,0:T(8,128)(2,1)} %fusion.2), calls=%async_computation.5 | async-start | bytes 1048576 | tf_op jit(solution)/shard_map/all_to_all | solution.py:144
  140.6 15.3 %collective-permute-start.1 = (bf16[3,512,6]{1,2,0:T(8,128)(2,1)S(1)}, bf16[3,512,6]{1,2,0:T(8,128)(2,1)S(1)}, u32[]{:S(2)}, u32[]{:S(2)}) collective-permute-start(bf16[3,512,6]{1,2,0:T(8,128)(2,1)S(1)} %pad_maximum_fusion.10), channel_id=1, source_target_pairs={{4,0},{8,4},{12,8},{16,12},{20,16},{24,20},{28,24},{32,28},{36,32}... | collective-permute-start | bytes 55304 | tf_op jit(solution)/shard_map/ppermute | solution.py:22
Sparse Core Ops, SparseCore 0:
  13.9 26.2 all-gather.2
  79.9 54.2 all-gather.4
  136.7 19.2 reduce-scatter.1

commit v7 on v6

--- a/solution.py
+++ b/solution.py
@@ -182,7 +182,7 @@
         tiled=True,
     )
     grad_out_weight = weight_gradient(full_cotangent, gated_out)
-    gradient_re, gradient_im = spectrum(grad_chan.astype(jnp.float32), tables)
+    gradient_re, gradient_im = spectrum(grad_chan.astype(jnp.float32), tables, lax.Precision.DEFAULT)
     pair = inverse(
         jnp.concatenate(
             [

time: 169 us -> 168 us (level)
  no operation moved by 1% of the time
where the time goes in v7:
time: 168 us; the launch traced here: 167 us
  waiting for transfers between devices  45.3 us (27%)
  starting transfers between devices  40.9 us (24%)
  matrix products  29 us (17%)
  blocking collectives  17.7 us (11%)
  between operations  14.4 us (9%)
  local copies, waits for them, and re-layouts  14.3 us (9%)
  other arithmetic  5.87 us (3%)
    all_to_all x1, blocking collectives, swap_layouts(): lax.all_to_all(outgoing, CTX, split_axis=0, concat_axis=0, tiled=True)  17.7 us
    all_to_all x1, starting transfers between devices, to_channels(): return lax.all_to_all(block, CTX, split_axis=0, concat_axis=1, tiled=True)  15.5 us
    ppermute x2, waiting for transfers between devices, from_behind(): lax.ppermute(value, axis, [(source, source + steps) for source in range(f...  13.6 us
    all_gather x1, waiting for transfers between devices, weight_gradient(): group_gated = lax.all_gather(gated_out, CTX_LO, axis=1, tiled=True)  10.7 us
    all_to_all x1, starting transfers between devices, to_positions(): return lax.all_to_all(block, CTX, split_axis=1, concat_axis=0, tiled=True)  8.36 us
    all_to_all x1, starting transfers between devices, weight_gradient(): lax.all_to_all(by_target, CTX_LO, split_axis=0, concat_axis=0, tiled=True)  7.97 us
    all_to_all x1, waiting for transfers between devices, to_channels(): return lax.all_to_all(block, CTX, split_axis=0, concat_axis=1, tiled=True)  7.35 us
    all_to_all x1, waiting for transfers between devices, to_positions(): return lax.all_to_all(block, CTX, split_axis=1, concat_axis=0, tiled=True)  7.3 us
  transfers between devices with their start and end apart: 9, of which 6 were waited for; matrix products, arithmetic and copies ran while one was open for 19% of the time, Pallas kernels for 0%

profile of v7, /device:TPU:22, one launch (start us, length us, event | category | flops | bytes accessed | tf_op | source)
XLA Modules:
  0.0 167.4 jit_solution(18018054454647556389)
XLA Ops:
  7.2 1.0 copy.165
  8.2 1.0 copy.164
  9.2 1.0 copy.163
  10.3 3.5 %collective-permute-start = (bf16[3,512,6]{1,2,0:T(8,128)(2,1)S(1)}, bf16[3,512,6]{1,2,0:T(8,128)(2,1)S(1)}, u32[]{:S(2)}, u32[]{:S(2)}) collective-permute-start(bf16[3,512,6]{1,2,0:T(8,128)(2,1)S(1)} %pad_maximum_fusion.12), channel_id=1, source_target_pairs={{0,4},{4,8},{8,12},{12,16},{16,20},{20,24},{24,28},{28,32},{32,36}... | collective-permute-start | bytes 55304 | tf_op jit(solution)/shard_map/ppermute | solution.py:22
  13.8 1.2 fusion.167
  15.1 0.9 collective-permute-done
  17.6 15.5 %all-to-all-start = ((bf16[64,8,128]{2,1,0:T(8,128)(2,1)}), bf16[64,8,128]{2,1,0:T(8,128)(2,1)S(1)}, u32[]{:S(2)}, u32[]{:S(2)}) async-start(bf16[64,8,128]{2,1,0:T(8,128)(2,1)} %bitcast.5), calls=%async_computation | async-start | bytes 262144 | tf_op jit(solution)/shard_map/all_to_all | solution.py:108
  34.3 7.3 %all-to-all-done = bf16[64,8,128]{2,1,0:T(8,128)(2,1)S(1)} async-done(((bf16[64,8,128]{2,1,0:T(8,128)(2,1)}), bf16[64,8,128]{2,1,0:T(8,128)(2,1)S(1)}, u32[]{:S(2)}, u32[]{:S(2)}) %all-to-all-start) | async-done | bytes 131104 | tf_op jit(solution)/shard_map/all_to_all | solution.py:108
  47.3 4.0 %fusion.47 = (bf16[512,128]{0,1:T(8,128)(2,1)S(1)}, f32[512,128]{0,1:T(8,128)}) fusion(bf16[3,512,128]{1,2,0:T(8,128)(2,1)S(1)} %fusion.25, bf16[4096,512]{1,0:T(8,128)(2,1)} %param.12, bf16[4096,128]{1,0:T(8,128)(2,1)} %all-gather.3.cloned.1.call-done), kind=kOutput, calls=%fused_computation.98 | convolution fusion | flops 537067520 | bytes 5767168 | tf_op jit(solution)/shard_map/dot_general | solution.py:172
  51.6 17.7 %all_to_all.35 = bf16[64,2,8,128]{3,2,1,0:T(8,128)(2,1)S(1)} all-to-all(bf16[64,2,8,128]{3,2,1,0:T(8,128)(2,1)S(1)} %copy.186), channel_id=1, replica_groups=mesh['ctx_hi'=8,'ctx_lo'=8,'tp'=4] {'ctx_hi','ctx_lo'}, dimensions={0} | all-to-all | bytes 524288 | tf_op jit(solution)/shard_map/all_to_all | solution.py:126
  70.6 1.3 fusion.56
  71.9 1.3 fusion.55
  73.2 1.8 %copy.188 = f32[512,128]{0,1:T(8,128)} copy(f32[512,128]{1,0:T(8,128)} %get-tuple-element.44) | data formatting | bytes 524288 | tf_op jit(solution)/shard_map/convert_element_type | solution.py:177
  75.0 2.3 %convolution_subtract_fusion.2 = f32[8,128,128]{2,1,0:T(8,128)} fusion(f32[8,128,128]{2,1,0:T(8,128)} %fusion.56, f32[8,128,128]{2,1,0:T(8,128)S(1)} %convolution_bitcast_fusion.3, f32[8,128,128]{2,1,0:T(8,128)S(1)} %convolution_bitcast_fusion.4, f32[128,128]{1,0:T(8,128)S(1)} %copy.181, f32[128,128]{1,0:T(8,128)S(1)} %copy.178), kind=kOutput, calls=%fused_computation.17 | convolution fusion | flops 34324480 | bytes 2228224 | tf_op jit(solution)/shard_map/dot_general | solution.py:54
  77.3 1.8 %fusion.53 = (bf16[1,512,128]{1,2,0:T(8,128)(2,1)S(1)}, bf16[512,128]{0,1:T(8,128)(2,1)}) fusion(f32[512,128]{0,1:T(8,128)} %get-tuple-element.53, f32[512,128]{0,1:T(8,128)} %copy.188, bf16[3,512,128]{1,2,0:T(8,128)(2,1)} %copy-done), kind=kLoop, calls=%fused_computation.110 | loop fusion | flops 327680 | bytes 917504 | tf_op jit(solution)/shard_map/stack | solution.py:204
  79.1 1.9 %multiply_add_fusion.2 = (f32[8,128,128]{2,1,0:T(8,128)S(1)}, f32[8,128,128]{2,1,0:T(8,128)S(1)}, f32[8,128,128]{2,1,0:T(8,128)S(1)}, f32[8,128,128]{2,1,0:T(8,128)S(1)}) fusion(f32[8,128,128]{2,1,0:T(8,128)} %convolution_subtract_fusion.2, f32[16,128,128]{2,1,0:T(8,128)S(1)} %convolution_add_fusion.1, f32[16,128,128]{2,1,0:T(8,128)S(1)} %convolution_subtract_fusion.1, ...), kind=kOutput, calls=%fused_computation.70 | convolution fusion | flops 35880960 | bytes 6422528 | tf_op jit(solution)/shard_map/dot_general | solution.py:57
  81.0 0.8 fusion.15
  81.8 0.8 fusion.16
  82.7 0.9 convolution_subtract_fusion
  83.6 0.8 convolution_add_fusion
  86.7 8.4 %all-to-all-start.2 = ((bf16[8,64,128]{2,0,1:T(8,128)(2,1)}), bf16[8,64,128]{2,0,1:T(8,128)(2,1)S(1)}, u32[]{:S(2)}, u32[]{:S(2)}) async-start(bf16[8,64,128]{2,0,1:T(8,128)(2,1)} %copy.209), calls=%async_computation.3 | async-start | bytes 262144 | tf_op jit(solution)/shard_map/all_to_all | solution.py:112
  95.1 1.1 copy.212
  96.2 7.3 %all-to-all-done.2 = bf16[8,64,128]{2,0,1:T(8,128)(2,1)S(1)} async-done(((bf16[8,64,128]{2,0,1:T(8,128)(2,1)}), bf16[8,64,128]{2,0,1:T(8,128)(2,1)S(1)}, u32[]{:S(2)}, u32[]{:S(2)}) %all-to-all-start.2) | async-done | bytes 131104 | tf_op jit(solution)/shard_map/all_to_all | solution.py:112
  103.5 8.0 %all-to-all-start.3 = ((bf16[8,8,64,128]{3,2,1,0:T(8,128)(2,1)}), bf16[8,8,64,128]{3,2,1,0:T(8,128)(2,1)S(1)}, u32[]{:S(2)}, u32[]{:S(2)}) async-start(bf16[8,8,64,128]{3,2,1,0:T(8,128)(2,1)} %copy.212), calls=%async_computation.4 | async-start | bytes 2097152 | tf_op jit(solution)/shard_map/all_to_all | solution.py:140
  111.5 4.8 %fusion = bf16[4096,128]{0,1:T(8,128)(2,1)} fusion(bf16[512,128]{0,1:T(8,128)(2,1)S(1)} %copy-done.2, bf16[4096,512]{1,0:T(8,128)(2,1)} %param.12), kind=kOutput, calls=%fused_computation.1 | convolution fusion | flops 537395200 | bytes 5373952 | tf_op jit(solution)/shard_map/dot_general | solution.py:179
  116.4 6.3 %all-to-all-done.3 = bf16[8,8,64,128]{3,2,1,0:T(8,128)(2,1)S(1)} async-done(((bf16[8,8,64,128]{3,2,1,0:T(8,128)(2,1)}), bf16[8,8,64,128]{3,2,1,0:T(8,128)(2,1)S(1)}, u32[]{:S(2)}, u32[]{:S(2)}) %all-to-all-start.3) | async-done | bytes 1048608 | tf_op jit(solution)/shard_map/all_to_all | solution.py:140
  122.7 10.7 %all-gather.5.cloned.1.call-done = bf16[512,1024]{0,1:T(8,128)(2,1)} async-done(((bf16[512,128]{0,1:T(8,128)(2,1)}), bf16[512,1024]{0,1:T(8,128)(2,1)}) %all-gather.5.cloned.1.call-update) | async-done | bytes 1048592 | tf_op jit(solution)/shard_map/all_gather | solution.py:137
  133.4 2.8 %fusion.2 = bf16[8,64,512]{2,1,0:T(8,128)(2,1)} fusion(bf16[512,8,128,1]{0,2,3,1:T(8,128)(2,1)} %bitcast.186, bf16[8,8,64,128]{3,2,1,0:T(8,128)(2,1)S(1)} %all-to-all-done.3), kind=kOutput, calls=%fused_computation.10 | convolution fusion | flops 537133056 | bytes 2621440 | tf_op jit(solution)/shard_map/dot_general | solution.py:141
  136.2 3.5 %all-to-all-start.4 = ((bf16[8,64,512]{2,1,0:T(8,128)(2,1)}), bf16[8,64,512]{2,1,0:T(8,128)(2,1)S(1)}, u32[]{:S(2)}, u32[]{:S(2)}) async-start(bf16[8,64,512]{2,1,0:T(8,128)(2,1)} %fusion.2), calls=%async_computation.5 | async-start | bytes 1048576 | tf_op jit(solution)/shard_map/all_to_all | solution.py:144
  139.8 1.9 %collective-permute-start.1 = (bf16[3,512,6]{1,2,0:T(8,128)(2,1)S(1)}, bf16[3,512,6]{1,2,0:T(8,128)(2,1)S(1)}, u32[]{:S(2)}, u32[]{:S(2)}) collective-permute-start(bf16[3,512,6]{1,2,0:T(8,128)(2,1)S(1)} %pad_maximum_fusion.10), channel_id=1, source_target_pairs={{4,0},{8,4},{12,8},{16,12},{20,16},{24,20},{28,24},{32,28},{36,32}... | collective-permute-start | bytes 55304 | tf_op jit(solution)/shard_map/ppermute | solution.py:22
  142.5 12.7 %collective-permute-done.1 = bf16[3,512,6]{1,2,0:T(8,128)(2,1)S(1)} collective-permute-done((bf16[3,512,6]{1,2,0:T(8,128)(2,1)S(1)}, bf16[3,512,6]{1,2,0:T(8,128)(2,1)S(1)}, u32[]{:S(2)}, u32[]{:S(2)}) %collective-permute-start.1) | collective-permute-done | bytes 18464 | tf_op jit(solution)/shard_map/ppermute | solution.py:22
  158.4 1.8 %copy.215 = bf16[1024,128]{1,0:T(8,128)(2,1)} copy(bf16[1024,128]{0,1:T(8,128)(2,1)} %reduce-scatter.2.cloned.1.call-done) | data formatting | bytes 524288
  (100 shorter events, 17.0 us)
Async XLA Ops:
  7.2 40.1 %all-gather.3.cloned.1.call-start = ((), (), s32[]{:S(2)}) async-start(), calls=%async_computation.6 | async-start | bytes 1310720 | tf_op jit(solution)/shard_map/all_gather | solution.py:171
  10.3 5.7 %collective-permute-start = (bf16[3,512,6]{1,2,0:T(8,128)(2,1)S(1)}, bf16[3,512,6]{1,2,0:T(8,128)(2,1)S(1)}, u32[]{:S(2)}, u32[]{:S(2)}) collective-permute-start(bf16[3,512,6]{1,2,0:T(8,128)(2,1)S(1)} %pad_maximum_fusion.12), channel_id=1, source_target_pairs={{0,4},{4,8},{8,12},{12,16},{16,20},{20,24},{24,28},{28,32},{32,36}... | collective-permute-start | bytes 55304 | tf_op jit(solution)/shard_map/ppermute | solution.py:22
  15.0 18.5 %copy-start.8 = (f32[1,8,8192]{2,1,0:T(8,128)S(1)}, f32[1,8,8192]{2,1,0:T(8,128)}, u32[]{:S(2)}) copy-start(f32[1,8,8192]{2,1,0:T(8,128)} %param.11) | copy-start | bytes 786436
  15.1 2.5 %copy-start.9 = (f32[3,512]{1,0:T(4,128)}, f32[3,512]{1,0:T(4,128)S(1)}, u32[]{:S(2)}) copy-start(f32[3,512]{1,0:T(4,128)S(1)} %get-tuple-element.56) | copy-start | bytes 18436
  15.1 2.5 %copy-start.11 = (f32[3,512]{1,0:T(4,128)}, f32[3,512]{1,0:T(4,128)S(1)}, u32[]{:S(2)}) copy-start(f32[3,512]{1,0:T(4,128)S(1)} %get-tuple-element.57) | copy-start | bytes 18436
  15.1 2.5 %copy-start.13 = (f32[3,512]{1,0:T(4,128)}, f32[3,512]{1,0:T(4,128)S(1)}, u32[]{:S(2)}) copy-start(f32[3,512]{1,0:T(4,128)S(1)} %get-tuple-element.58) | copy-start | bytes 18436
  15.1 2.5 %copy-start.15 = (f32[3,512]{1,0:T(4,128)}, f32[3,512]{1,0:T(4,128)S(1)}, u32[]{:S(2)}) copy-start(f32[3,512]{1,0:T(4,128)S(1)} %get-tuple-element.59) | copy-start | bytes 18436
  15.1 2.5 %copy-start.17 = (f32[3,512,1]{1,0,2:T(4,128)}, f32[3,512,1]{1,0,2:T(4,128)S(1)}, u32[]{:S(2)}) copy-start(f32[3,512,1]{1,0,2:T(4,128)S(1)} %copy.298) | copy-start | bytes 18436
  16.8 30.5 %copy-start = (bf16[3,512,128]{1,2,0:T(8,128)(2,1)}, bf16[3,512,128]{1,2,0:T(8,128)(2,1)S(1)}, u32[]{:S(2)}) copy-start(bf16[3,512,128]{1,2,0:T(8,128)(2,1)S(1)} %fusion.25) | copy-start | bytes 1179652
  17.6 24.0 %all-to-all-start = ((bf16[64,8,128]{2,1,0:T(8,128)(2,1)}), bf16[64,8,128]{2,1,0:T(8,128)(2,1)S(1)}, u32[]{:S(2)}, u32[]{:S(2)}) async-start(bf16[64,8,128]{2,1,0:T(8,128)(2,1)} %bitcast.5), calls=%async_computation | async-start | bytes 262144 | tf_op jit(solution)/shard_map/all_to_all | solution.py:108
  33.2 100.2 %all-gather.5.cloned.1.call-start = ((), (), s32[]{:S(2)}) async-start(), calls=%async_computation.8 | async-start | bytes 1179648 | tf_op jit(solution)/shard_map/all_gather | solution.py:137
  34.0 36.0 %copy-start.4 = (f32[128,128]{0,1:T(8,128)}, f32[128,128]{0,1:T(8,128)S(1)}, u32[]{:S(2)}) copy-start(f32[128,128]{0,1:T(8,128)S(1)} %sine_negate_fusion.1) | copy-start | bytes 196612
  34.3 36.0 %copy-start.6 = (f32[128,128]{0,1:T(8,128)}, f32[128,128]{0,1:T(8,128)S(1)}, u32[]{:S(2)}) copy-start(f32[128,128]{0,1:T(8,128)S(1)} %fusion.87) | copy-start | bytes 196612
  81.8 2.6 %copy-start.7 = (f32[128,128]{0,1:T(8,128)S(1)}, f32[128,128]{0,1:T(8,128)}, u32[]{:S(2)}) copy-start(f32[128,128]{0,1:T(8,128)} %copy-done.6) | copy-start | bytes 196612
  82.7 2.5 %copy-start.5 = (f32[128,128]{0,1:T(8,128)S(1)}, f32[128,128]{0,1:T(8,128)}, u32[]{:S(2)}) copy-start(f32[128,128]{0,1:T(8,128)} %copy-done.4) | copy-start | bytes 196612
  84.4 10.7 %copy-start.3 = (bf16[4096,128]{1,0:T(8,128)(2,1)S(1)}, bf16[4096,128]{1,0:T(8,128)(2,1)}, u32[]{:S(2)}) copy-start(bf16[4096,128]{1,0:T(8,128)(2,1)} %all-gather.3.cloned.1.call-done) | copy-start | bytes 3145732
  85.2 26.3 %copy-start.2 = (bf16[512,128]{0,1:T(8,128)(2,1)S(1)}, bf16[512,128]{0,1:T(8,128)(2,1)}, u32[]{:S(2)}) copy-start(bf16[512,128]{0,1:T(8,128)(2,1)} %get-tuple-element.42) | copy-start | bytes 393220
  86.7 16.8 %all-to-all-start.2 = ((bf16[8,64,128]{2,0,1:T(8,128)(2,1)}), bf16[8,64,128]{2,0,1:T(8,128)(2,1)S(1)}, u32[]{:S(2)}, u32[]{:S(2)}) async-start(bf16[8,64,128]{2,0,1:T(8,128)(2,1)} %copy.209), calls=%async_computation.3 | async-start | bytes 262144 | tf_op jit(solution)/shard_map/all_to_all | solution.py:112
  103.5 19.2 %all-to-all-start.3 = ((bf16[8,8,64,128]{3,2,1,0:T(8,128)(2,1)}), bf16[8,8,64,128]{3,2,1,0:T(8,128)(2,1)S(1)}, u32[]{:S(2)}, u32[]{:S(2)}) async-start(bf16[8,8,64,128]{3,2,1,0:T(8,128)(2,1)} %copy.212), calls=%async_computation.4 | async-start | bytes 2097152 | tf_op jit(solution)/shard_map/all_to_all | solution.py:140
  111.5 46.9 %reduce-scatter.2.cloned.1.call-start = ((), (), s32[]{:S(2)}) async-start(), calls=%async_computation.7 | async-start | bytes 1310720 | tf_op jit(solution)/shard_map/reduce_scatter | solution.py:178
  116.2 23.5 %copy-start.1 = (bf16[3,512,128]{1,2,0:T(8,128)(2,1)S(1)}, bf16[3,512,128]{1,2,0:T(8,128)(2,1)}, u32[]{:S(2)}) copy-start(bf16[3,512,128]{1,2,0:T(8,128)(2,1)} %copy-done) | copy-start | bytes 1179652
  133.4 22.0 %copy-start.10 = (f32[3,512]{1,0:T(4,128)S(1)}, f32[3,512]{1,0:T(4,128)}, u32[]{:S(2)}) copy-start(f32[3,512]{1,0:T(4,128)} %copy-done.9) | copy-start | bytes 18436
  133.4 22.0 %copy-start.12 = (f32[3,512]{1,0:T(4,128)S(1)}, f32[3,512]{1,0:T(4,128)}, u32[]{:S(2)}) copy-start(f32[3,512]{1,0:T(4,128)} %copy-done.11) | copy-start | bytes 18436
  133.4 22.0 %copy-start.14 = (f32[3,512]{1,0:T(4,128)S(1)}, f32[3,512]{1,0:T(4,128)}, u32[]{:S(2)}) copy-start(f32[3,512]{1,0:T(4,128)} %copy-done.13) | copy-start | bytes 18436
  133.4 22.0 %copy-start.16 = (f32[3,512]{1,0:T(4,128)S(1)}, f32[3,512]{1,0:T(4,128)}, u32[]{:S(2)}) copy-start(f32[3,512]{1,0:T(4,128)} %copy-done.15) | copy-start | bytes 18436
  133.4 22.0 %copy-start.18 = (f32[3,512,1]{1,0,2:T(4,128)S(1)}, f32[3,512,1]{1,0,2:T(4,128)}, u32[]{:S(2)}) copy-start(f32[3,512,1]{1,0,2:T(4,128)} %copy-done.17) | copy-start | bytes 18436
  136.2 24.0 %all-to-all-start.4 = ((bf16[8,64,512]{2,1,0:T(8,128)(2,1)}), bf16[8,64,512]{2,1,0:T(8,128)(2,1)S(1)}, u32[]{:S(2)}, u32[]{:S(2)}) async-start(bf16[8,64,512]{2,1,0:T(8,128)(2,1)} %fusion.2), calls=%async_computation.5 | async-start | bytes 1048576 | tf_op jit(solution)/shard_map/all_to_all | solution.py:144
  139.8 15.5 %collective-permute-start.1 = (bf16[3,512,6]{1,2,0:T(8,128)(2,1)S(1)}, bf16[3,512,6]{1,2,0:T(8,128)(2,1)S(1)}, u32[]{:S(2)}, u32[]{:S(2)}) collective-permute-start(bf16[3,512,6]{1,2,0:T(8,128)(2,1)S(1)} %pad_maximum_fusion.10), channel_id=1, source_target_pairs={{4,0},{8,4},{12,8},{16,12},{20,16},{24,20},{28,24},{32,28},{36,32}... | collective-permute-start | bytes 55304 | tf_op jit(solution)/shard_map/ppermute | solution.py:22
Sparse Core Ops, SparseCore 0:
  13.9 26.2 all-gather.2
  79.2 54.1 all-gather.4
  136.0 19.5 reduce-scatter.1
